TPU v7x, 256 devices: a whole 4x4x8 slice. The times are simulated.
256 devices in a mesh: tile: 32 (over x, z), atom: 8 (over y, core).
Axes of the slice: x: 4, y: 4, z: 8, core: 2. Of those that a mesh axis runs over, the one named last changes fastest.
Arguments:
- images: float32 [1024, 1024], P(('tile', 'atom')), may hold values from -6 to 6
- active: int32 [1024, 2], P(('tile', 'atom')), may hold values from 0 to 7, all different within a row; in each aligned block of 4 rows (0 to 3, 4 to 7, ...) at most 2 rows name the same one
- dictionary: float32 [8, 32, 1024], P('atom', 'tile'), may hold values from -6 to 6
Outputs:
- reconstruction: float32 [1024, 1024], P(('tile', 'atom'))
- new_dictionary: float32 [8, 32, 1024], P('atom', 'tile')
Inputs may be any that keep to these rules, and one draw needn't show every extreme that they name: `active`: each tile names 2 different atom blocks. Among the 4 tiles of one device no block is named by more than 2 tiles, and on some devices one block is named by exactly 2. Every block is named by some tile.
All inputs are finite; a program needn't handle non-finite values.
Results may differ from a plain program's by a relative error of at most 0.0001.
Values sent between devices are 32-bit elements; how exact they have to be, the bound alone decides.
No kernel may reach another device: no remote copies, remote signals or barrier semaphores. Data moves between devices by JAX's collectives and lax.ppermute only.
A program may use at most 128 MiB of HBM per device.

v0:
```python
import math

import jax
import jax.numpy as jnp
from jax import lax
from jax.sharding import PartitionSpec as P

SIDE = 32
BLK = 32
NBLK = 8
ACT = 2
MOST = 2
ITERS = 2


shrink_scale = 0.5
step_ratio = 0.5
epsilon = 1e-06
highest = lax.Precision.HIGHEST


def momentum_weights(count):
    weights = []
    current = 1.0
    for sweep in range(count):
        following = (1.0 + math.sqrt(1.0 + 4.0 * current * current)) / 2.0
        weights.append((current - 1.0) / following)
        current = following
    return weights


def unit_rows(values):
    return values / jnp.sqrt(jnp.mean(values * values, axis=-1, keepdims=True) + epsilon)


def fourier_table(length):
    position = jnp.arange(length, dtype=jnp.int32)
    phase = position[:, None] * position[None, :] % length
    angle = phase.astype(jnp.float32) * (2.0 * math.pi / length)
    cosine = jnp.cos(angle)
    sine = jnp.sin(angle)
    forward_right = jnp.stack([cosine, -sine], axis=1)
    forward_left = jnp.stack(
        [jnp.stack([cosine, sine], axis=1), jnp.stack([-sine, cosine], axis=1)], axis=0
    )
    inverse_right = jnp.stack(
        [jnp.stack([cosine, sine], axis=1), jnp.stack([-sine, cosine], axis=1)], axis=0
    )
    inverse_left = jnp.stack([cosine, -sine], axis=0)
    return (forward_right, forward_left, inverse_right, inverse_left)


def forward(values, table):
    forward_right, forward_left = (table[0], table[1])
    length = forward_right.shape[0]
    field = values.reshape(values.shape[:-1] + (length, length))
    across = jnp.einsum(
        "...uw,wdq->...udq",
        field,
        forward_right,
        precision=highest,
        preferred_element_type=jnp.float32,
    )
    result = jnp.einsum(
        "cpdu,...udq->...cpq",
        forward_left,
        across,
        precision=highest,
        preferred_element_type=jnp.float32,
    )
    return result.reshape(values.shape[:-1] + (2 * length * length,))


def inverse(spectra, table):
    inverse_right, inverse_left = (table[2], table[3])
    length = inverse_left.shape[1]
    shaped = spectra.reshape(spectra.shape[:-1] + (2, length, length))
    across = jnp.einsum(
        "...cpq,cqew->...pew",
        shaped,
        inverse_right,
        precision=highest,
        preferred_element_type=jnp.float32,
    )
    result = jnp.einsum(
        "lmq,...qlg->...mg",
        inverse_left,
        across,
        precision=highest,
        preferred_element_type=jnp.float32,
    )
    return result.reshape(spectra.shape[:-1] + (length * length,)) / (length * length)


def split_parts(packed):
    middle = packed.shape[-1] // 2
    return (packed[..., :middle], packed[..., middle:])


def times_conj(first, second):
    first_real, first_imag = split_parts(first)
    second_real, second_imag = split_parts(second)
    real_part = first_real * second_real + first_imag * second_imag
    imag_part = first_real * second_imag - first_imag * second_real
    return jnp.concatenate([real_part, imag_part], axis=-1)


def product_sum(atom_spec, code_spec):
    atom_real, atom_imag = split_parts(atom_spec)
    code_real, code_imag = split_parts(code_spec)
    real_sum = jnp.sum(atom_real * code_real - atom_imag * code_imag, axis=(1, 2))
    imag_sum = jnp.sum(atom_real * code_imag + atom_imag * code_real, axis=(1, 2))
    return jnp.concatenate([real_sum, imag_sum], axis=-1)


def on_device(images, active, dictionary):
    tiles_here = images.shape[0]
    pixels = images.shape[1]
    rows_owned = dictionary.shape[1]
    table = fourier_table(SIDE)
    image_spec = forward(images, table)
    atoms = unit_rows(dictionary)
    slot_count = tiles_here * ACT
    flat_ids = active.reshape(slot_count)
    block_range = jnp.arange(NBLK, dtype=jnp.int32)
    slot_index = jnp.arange(slot_count, dtype=jnp.int32)
    earlier = slot_index[None, :] < slot_index[:, None]
    same_block = flat_ids[:, None] == flat_ids[None, :]
    rank = jnp.sum((earlier & same_block).astype(jnp.int32), axis=1)
    slot_range = jnp.arange(MOST, dtype=jnp.int32)
    placing = (block_range[:, None, None] == flat_ids[None, None, :]) & (
        slot_range[None, :, None] == rank[None, None, :]
    )
    placing = placing.astype(jnp.float32).reshape(NBLK * MOST, slot_count)
    codes = jnp.zeros((tiles_here, ACT, BLK, pixels), jnp.float32)
    code_spec = jnp.zeros((tiles_here, ACT, BLK, 2 * pixels), jnp.float32)
    weights = momentum_weights(ITERS)
    own_spec = forward(atoms, table)
    every = lax.all_gather(own_spec, ("tile", "atom"), axis=0, tiled=True)
    tile_groups = lax.axis_size("tile")
    every = every.reshape(tile_groups, NBLK, rows_owned, 2 * pixels)
    chosen = jnp.take(every, flat_ids, axis=1)
    chosen = jnp.transpose(chosen, (1, 0, 2, 3)).reshape(tiles_here, ACT, BLK, 2 * pixels)
    chosen_real, chosen_imag = split_parts(chosen)
    power = chosen_real * chosen_real + chosen_imag * chosen_imag
    bound = jnp.max(jnp.sum(power, axis=(1, 2)), axis=1) + epsilon
    rate = (1.0 / bound)[:, None, None, None]
    limit = rate * (shrink_scale * SIDE)
    prior = codes
    prior_spec = code_spec
    guess = codes
    guess_spec = code_spec
    for sweep in range(ITERS):
        residual_spec = product_sum(chosen, guess_spec) - image_spec
        gradient = inverse(times_conj(chosen, residual_spec[:, None, None, :]), table)
        moved = guess - rate * gradient
        fresh = moved - jnp.clip(moved, -limit, limit)
        fresh_spec = forward(fresh, table)
        guess = fresh + weights[sweep] * (fresh - prior)
        guess_spec = fresh_spec + weights[sweep] * (fresh_spec - prior_spec)
        prior, prior_spec = (fresh, fresh_spec)
    recon_spec = product_sum(chosen, prior_spec)
    residual_spec = recon_spec - image_spec
    slot_terms = times_conj(prior_spec, residual_spec[:, None, None, :]).reshape(
        slot_count, BLK * 2 * pixels
    )
    outgoing = jnp.dot(placing, slot_terms, precision=highest, preferred_element_type=jnp.float32)
    outgoing = outgoing.reshape(NBLK, MOST, BLK, 2 * pixels)
    arrived = lax.all_to_all(outgoing, "atom", split_axis=0, concat_axis=1, tiled=True)
    owner_sum = jnp.sum(arrived, axis=1)
    total = lax.psum(owner_sum, "tile")
    offset = lax.axis_index("tile") * rows_owned
    mine = lax.dynamic_slice_in_dim(total, offset, rows_owned, 1)
    atom_grad = inverse(mine, table)
    scale = jnp.sqrt(jnp.mean(atom_grad * atom_grad, axis=-1, keepdims=True) + epsilon)
    atoms = unit_rows(atoms - step_ratio * atom_grad / scale)
    recon = inverse(recon_spec, table)
    return (recon, atoms)


def solution(mesh):
    in_specs = (P(("tile", "atom"), None), P(("tile", "atom"), None), P("atom", "tile", None))
    out_specs = (P(("tile", "atom"), None), P("atom", "tile", None))
    return jax.shard_map(
        on_device, mesh=mesh, in_specs=in_specs, out_specs=out_specs, check_vma=False
    )
```

profile of v0, /device:TPU:8, one launch (start us, length us, event | category | flops | bytes accessed | tf_op | source)
XLA Modules:
  0.0 500.6 jit_solution(15187165786976593706)
XLA Ops:
  7.4 1.3 multiply_reduce_fusion.2
  9.4 0.5 broadcast.415
  9.9 1.3 fusion.91
  11.9 0.7 reshape.499
  12.6 0.8 copy.66
  13.6 0.8 reshape.527
  14.4 0.5 convolution_bitcast_fusion.2
  14.9 0.3 convolution_bitcast_fusion.1
  15.7 104.0 %all-gather.2.cloned.1.call-done = f32[256,1,2048]{2,1,0:T(1,128)} async-done(((f32[1,1,2048]{2,1,0:T(1,128)}), f32[256,1,2048]{2,1,0:T(1,128)}) %all-gather.2.cloned.1.call-update) | async-done | bytes 2097168 | tf_op jit(solution)/shard_map/all_gather | solution.py:139
  119.8 2.5 copy.160
  122.2 1.2 copy.70
  123.5 2.0 gather_fusion
  125.5 1.9 bitcast_select_fusion
  127.4 0.4 add_reduce_fusion.2
  127.9 0.3 multiply_add_fusion.4
  128.2 1.5 pad_maximum_fusion
  129.7 6.5 %reshape.531 = f32[4,2,32,2,32,32,1]{5,4,3,2,1,0,6:T(8,128)} reshape(f32[4,2,32,2048]{3,2,1,0:T(8,128)} %pad_maximum_fusion) | data formatting | bytes 4194304 | tf_op jit(solution)/shard_map/reshape | solution.py:77
  136.2 23.9 %fusion.6 = f32[4,2,32,32,2,32,1]{3,5,4,6,2,1,0:T(8,128)} fusion(f32[4,2,32,2,32,32,1]{5,4,3,2,1,0,6:T(8,128)} %reshape.531, f32[1,32,2,32]{3,1,2,0:T(8,128)S(1)} %get-tuple-element.28, f32[1,32,2,32]{3,1,2,0:T(8,128)S(1)} %get-tuple-element.27), kind=kOutput, calls=%fused_computation.7 | convolution fusion | flops 402657280 | bytes 4210688 | tf_op jit(solution)/shard_map/...cpq,cqew->...pew/dot_general | solution.py:78
  160.2 10.9 %fusion.4 = f32[4,2,32,32,32,1]{4,3,5,2,1,0:T(8,128)S(1)} fusion(f32[4,2,32,32,2,32,1]{3,5,4,6,2,1,0:T(8,128)} %fusion.6, f32[1,32,32]{2,1,0:T(8,128)S(1)} %get-tuple-element.35, f32[1,32,32]{2,1,0:T(8,128)S(1)} %get-tuple-element.36), kind=kOutput, calls=%fused_computation.5 | convolution fusion | flops 201328640 | bytes 3153920 | tf_op jit(solution)/shard_map/lmq,...qlg->...mg/dot_general | solution.py:85
  171.2 7.1 %fusion.15 = f32[4,2,32,32,2,32]{3,5,4,2,1,0:T(8,128)S(1)} fusion(f32[4,2,32,32,32,1]{4,3,5,2,1,0:T(8,128)S(1)} %fusion.4, f32[4]{0:T(128)S(1)} %get-tuple-element.30, f32[4]{0:T(128)S(1)} %get-tuple-element.29, f32[4]{0:T(128)S(1)} %get-tuple-element.11, f32[32,1,32]{2,0,1:T(8,128)S(1)} %get-tuple-element.33, f32[32,1,32]{2,0,1:T(8,128)S(1)} %get-tuple-element.34), kind=kOutput, calls=%fused_computation.17 | convolution fusion | flops 202639360 | bytes 3153968 | tf_op jit(solution)/shard_map/...uw,wdq->...udq/dot_general | solution.py:57
  178.4 8.9 %fusion.23 = f32[4,2,32,2,32,32]{4,5,3,2,1,0:T(8,128)} fusion(f32[4,2,32,32,2,32]{3,5,4,2,1,0:T(8,128)S(1)} %fusion.15, f32[1,32,2,32]{3,1,2,0:T(8,128)S(1)} %get-tuple-element.28, f32[1,32,2,32]{3,1,2,0:T(8,128)S(1)} %get-tuple-element.27), kind=kOutput, calls=%fused_computation.28 | convolution fusion | flops 402657280 | bytes 4210688 | tf_op jit(solution)/shard_map/cpdu,...udq->...cpq/dot_general | solution.py:64
  187.3 8.9 %copy.78 = f32[4,2,32,2,32,32]{5,4,3,2,1,0:T(8,128)} copy(f32[4,2,32,2,32,32]{4,5,3,2,1,0:T(8,128)} %fusion.23) | data formatting | bytes 4194304 | tf_op jit(solution)/shard_map/cpdu,...udq->...cpq/transpose | solution.py:64
  196.2 7.6 %reshape.506 = f32[4,2,32,2048]{3,2,1,0:T(8,128)} reshape(f32[4,2,32,2,32,32]{5,4,3,2,1,0:T(8,128)} %copy.78) | data formatting | bytes 4194304 | tf_op jit(solution)/shard_map/reshape | solution.py:71
  203.9 1.8 multiply_add_fusion.1
  205.6 0.6 subtract_reduce_fusion.1
  206.2 0.3 multiply_add_fusion.3
  206.5 1.5 pad_maximum_fusion.1
  208.1 6.3 %reshape.541 = f32[4,2,32,2,32,32,1]{5,4,3,2,1,0,6:T(8,128)} reshape(f32[4,2,32,2048]{3,2,1,0:T(8,128)} %pad_maximum_fusion.1) | data formatting | bytes 4194304 | tf_op jit(solution)/shard_map/reshape | solution.py:77
  214.3 22.6 %fusion.2 = f32[4,2,32,32,2,32,1]{3,5,4,6,2,1,0:T(8,128)S(1)} fusion(f32[4,2,32,2,32,32,1]{5,4,3,2,1,0,6:T(8,128)} %reshape.541, f32[1,32,2,32]{3,1,2,0:T(8,128)S(1)} %get-tuple-element.28, f32[1,32,2,32]{3,1,2,0:T(8,128)S(1)} %get-tuple-element.27), kind=kOutput, calls=%fused_computation.3 | convolution fusion | flops 402657280 | bytes 4210688 | tf_op jit(solution)/shard_map/...cpq,cqew->...pew/dot_general | solution.py:78
  237.0 6.7 %fusion = f32[4,2,32,32,32,1]{4,3,5,2,1,0:T(8,128)S(1)} fusion(f32[4,2,32,32,2,32,1]{3,5,4,6,2,1,0:T(8,128)S(1)} %fusion.2, f32[1,32,32]{2,1,0:T(8,128)S(1)} %get-tuple-element.35, f32[1,32,32]{2,1,0:T(8,128)S(1)} %get-tuple-element.36), kind=kOutput, calls=%fused_computation.1 | convolution fusion | flops 201328640 | bytes 3153920 | tf_op jit(solution)/shard_map/lmq,...qlg->...mg/dot_general | solution.py:85
  243.6 8.9 %fusion.13 = f32[4,2,32,32,2,32]{3,5,4,2,1,0:T(8,128)S(1)} fusion(f32[4,2,32,32,32,1]{4,3,5,2,1,0:T(8,128)S(1)} %fusion, f32[4,2,32,32,32,1]{4,3,5,2,1,0:T(8,128)S(1)} %copy-done.1, f32[4]{0:T(128)S(1)} %get-tuple-element.30, f32[4]{0:T(128)S(1)} %get-tuple-element.29, f32[4]{0:T(128)S(1)} %get-tuple-element.11, f32[32,1,32]{2,0,1:T(8,128)S(1)} %get-tuple-element.33, ...), kind=kOutput, calls=%fused_computation.15 | convolution fusion | flops 204474368 | bytes 4202544 | tf_op jit(solution)/shard_map/...uw,wdq->...udq/dot_general | solution.py:57
  252.5 8.9 %fusion.26 = f32[4,2,32,2,32,32]{4,5,3,2,1,0:T(8,128)} fusion(f32[4,2,32,32,2,32]{3,5,4,2,1,0:T(8,128)S(1)} %fusion.13, f32[1,32,2,32]{3,1,2,0:T(8,128)S(1)} %get-tuple-element.28, f32[1,32,2,32]{3,1,2,0:T(8,128)S(1)} %get-tuple-element.27), kind=kOutput, calls=%fused_computation.29 | convolution fusion | flops 402657280 | bytes 4210688 | tf_op jit(solution)/shard_map/cpdu,...udq->...cpq/dot_general | solution.py:64
  261.5 8.9 %copy.83 = f32[4,2,32,2,32,32]{5,4,3,2,1,0:T(8,128)} copy(f32[4,2,32,2,32,32]{4,5,3,2,1,0:T(8,128)} %fusion.26) | data formatting | bytes 4194304 | tf_op jit(solution)/shard_map/cpdu,...udq->...cpq/transpose | solution.py:64
  270.4 7.7 %reshape.508 = f32[4,2,32,2048]{3,2,1,0:T(8,128)} reshape(f32[4,2,32,2,32,32]{5,4,3,2,1,0:T(8,128)} %copy.83) | data formatting | bytes 4194304 | tf_op jit(solution)/shard_map/reshape | solution.py:71
  278.1 2.3 subtract_reduce_fusion
  280.4 0.4 multiply_add_fusion.2
  281.1 2.7 fusion.72
  283.8 4.4 copy.87
  288.2 4.9 all-to-all-start
  293.3 48.2 %all-to-all-done = f32[8,2,32,2048]{3,2,1,0:T(8,128)} async-done(((f32[8,2,32,2048]{3,2,1,0:T(8,128)}), f32[8,2,32,2048]{3,2,1,0:T(8,128)}, u32[]{:S(2)}, u32[]{:S(2)}) %all-to-all-start) | async-done | bytes 4194336 | tf_op jit(solution)/shard_map/all_to_all | solution.py:169
  341.5 3.1 reduce_sum.119
  344.6 0.5 convolution_bitcast_fusion
  345.5 0.7 div.88
  346.2 142.3 %all-reduce.2.cloned.1.call-done = f32[1,32,2048]{2,1,0:T(8,128)} async-done(((f32[1,32,2048]{2,1,0:T(8,128)}), f32[1,32,2048]{2,1,0:T(8,128)}) %all-reduce.2.cloned.1.call-update) | async-done | bytes 262160 | tf_op jit(solution)/shard_map/psum | solution.py:171
  488.5 0.9 dynamic-slice_reduce_fusion
  489.8 0.8 multiply_reduce_fusion
  491.4 0.6 multiply_reduce_fusion.1
  492.7 0.6 broadcast_divide_fusion
  (47 shorter events, 3.0 us)
Async XLA Ops:
  7.2 112.6 %all-gather.2.cloned.1.call-start = ((), (), s32[]{:S(2)}) async-start(), calls=%async_computation.1 | async-start | bytes 2105344 | tf_op jit(solution)/shard_map/all_gather | solution.py:139
  171.2 7.2 %copy-start = (f32[4,2,32,32,32,1]{4,3,5,2,1,0:T(8,128)}, f32[4,2,32,32,32,1]{4,3,5,2,1,0:T(8,128)S(1)}, u32[]{:S(2)}) copy-start(f32[4,2,32,32,32,1]{4,3,5,2,1,0:T(8,128)S(1)} %fusion.4) | copy-start | bytes 3145732
  237.0 6.7 %copy-start.1 = (f32[4,2,32,32,32,1]{4,3,5,2,1,0:T(8,128)S(1)}, f32[4,2,32,32,32,1]{4,3,5,2,1,0:T(8,128)}, u32[]{:S(2)}) copy-start(f32[4,2,32,32,32,1]{4,3,5,2,1,0:T(8,128)} %copy-done) | copy-start | bytes 3145732
  278.1 2.3 copy-start.2
  288.2 53.3 %all-to-all-start = ((f32[8,2,32,2048]{3,2,1,0:T(8,128)}), f32[8,2,32,2048]{3,2,1,0:T(8,128)}, u32[]{:S(2)}, u32[]{:S(2)}) async-start(f32[8,2,32,2048]{3,2,1,0:T(8,128)} %copy.87), calls=%async_computation | async-start | bytes 8388608 | tf_op jit(solution)/shard_map/all_to_all | solution.py:169
  293.2 195.3 %all-reduce.2.cloned.1.call-start = ((), (), s32[]{:S(2)}) async-start(), calls=%async_computation.2 | async-start | bytes 524288 | tf_op jit(solution)/shard_map/psum | solution.py:171
Sparse Core Ops, SparseCore 0:
  12.8 106.9 all-gather.1
  344.8 143.7 all-reduce.1
where the time goes:
time: 506 us; the launch traced here: 501 us
  waiting for transfers between devices  295 us (58%)
  matrix products  104 us (21%)
  local copies, waits for them, and re-layouts  61.4 us (12%)
  other arithmetic  18.9 us (4%)
  between operations  16.9 us (3%)
    psum x1, waiting for transfers between devices, on_device(): total = lax.psum(owner_sum, 'tile')  142 us
    all_gather x1, waiting for transfers between devices, on_device(): every = lax.all_gather(own_spec, ('tile', 'atom'), axis=0, tiled=True)  104 us
    all_to_all x1, waiting for transfers between devices, on_device(): lax.all_to_all(outgoing, 'atom', split_axis=0, concat_axis=1, tiled=True)  48.2 us
    dot_general x4, matrix products, inverse(): jnp.einsum('...cpq,cqew->...pew', shaped, inverse_right, precision=highes...  47.3 us
    dot_general x4, matrix products, inverse(): jnp.einsum('lmq,...qlg->...mg', inverse_left, across, precision=highest,...  18.6 us
    dot_general x4, matrix products, forward(): jnp.einsum('cpdu,...udq->...cpq', forward_left, across, precision=highest...  18.4 us
    transpose x4, local copies, waits for them, and re-layouts, forward(): jnp.einsum('cpdu,...udq->...cpq', forward_left, across, precision=highest...  18 us
    dot_general x4, matrix products, forward(): jnp.einsum('...uw,wdq->...udq', field, forward_right, precision=highest,...  16.8 us
  transfers between devices with their start and end apart: 3, of which 3 were waited for; matrix products, arithmetic and copies ran while one was open for 1% of the time, Pallas kernels for 0%

commit v1 on v0

v1 whole, which is shorter than its diff:
```python
import math

import numpy as np
import jax
import jax.numpy as jnp
from jax import lax
from jax.sharding import PartitionSpec as P

SIDE = 32
BLK = 32
NBLK = 8
ACT = 2
ITERS = 2

shrink_scale = 0.5
step_ratio = 0.5
epsilon = 1e-06
highest = lax.Precision.HIGHEST

HALF = SIDE // 2 + 1
USED = SIDE * HALF
PART = 640


def momentum_weights(count):
    weights = []
    current = 1.0
    for sweep in range(count):
        following = (1.0 + math.sqrt(1.0 + 4.0 * current * current)) / 2.0
        weights.append((current - 1.0) / following)
        current = following
    return weights


def unit_rows(values):
    return values / jnp.sqrt(jnp.mean(values * values, axis=-1, keepdims=True) + epsilon)


def half_table():
    side = np.arange(SIDE)
    phase = (side[:, None, None, None] * side[None, None, :, None]
             + side[None, :, None, None] * np.arange(HALF)[None, None, None, :]) % SIDE
    angle = phase * (2.0 * np.pi / SIDE)
    table = np.zeros((SIDE * SIDE, 2 * PART), np.float32)
    table[:, :USED] = np.cos(angle).reshape(SIDE * SIDE, USED)
    table[:, PART:PART + USED] = -np.sin(angle).reshape(SIDE * SIDE, USED)
    column = np.arange(HALF)
    pair = np.where((column == 0) | (column == SIDE // 2), 1.0, 2.0) / (SIDE * SIDE)
    weight = np.zeros((2 * PART,), np.float32)
    weight[:USED] = np.tile(pair, SIDE)
    weight[PART:PART + USED] = np.tile(pair, SIDE)
    return table, weight


def forward(values, table):
    return jnp.dot(values, table, precision=highest, preferred_element_type=jnp.float32)


def inverse(spectra, table, weight):
    return lax.dot_general(
        spectra * weight, table, (((spectra.ndim - 1,), (1,)), ((), ())),
        precision=highest, preferred_element_type=jnp.float32,
    )


def parts(packed):
    return (packed[..., :PART], packed[..., PART:])


def conj_times(first, second):
    first_real, first_imag = parts(first)
    second_real, second_imag = parts(second)
    real_part = first_real * second_real + first_imag * second_imag
    imag_part = first_real * second_imag - first_imag * second_real
    return jnp.concatenate([real_part, imag_part], axis=-1)


def product_sum(atom_spec, code_spec):
    atom_real, atom_imag = parts(atom_spec)
    code_real, code_imag = parts(code_spec)
    real_sum = jnp.sum(atom_real * code_real - atom_imag * code_imag, axis=1)
    imag_sum = jnp.sum(atom_real * code_imag + atom_imag * code_real, axis=1)
    return jnp.concatenate([real_sum, imag_sum], axis=-1)


def on_device(images, active, dictionary):
    tiles_here, pixels = images.shape
    tile_count = lax.axis_size("tile")
    atom_count = lax.axis_size("atom")
    table_host, weight_host = half_table()
    table = jnp.asarray(table_host)
    weight = jnp.asarray(weight_host)
    width = table.shape[1]

    own = unit_rows(dictionary.reshape(1, pixels))
    step = lax.all_to_all(jnp.broadcast_to(own[None], (tile_count, 1, pixels)), "tile", 0, 0, tiled=True)
    every = lax.all_to_all(
        jnp.broadcast_to(step[None], (atom_count, tile_count, 1, pixels)), "atom", 0, 0, tiled=True
    )
    every = every.reshape(atom_count, tile_count * pixels)

    image_spec = forward(images, table)
    slot_count = tiles_here * ACT
    flat_ids = active.reshape(slot_count)
    chosen_atoms = jnp.take(every, flat_ids, axis=0).reshape(slot_count * BLK, pixels)
    rows = ACT * BLK
    chosen = forward(chosen_atoms, table).reshape(tiles_here, rows, width)
    chosen_real, chosen_imag = parts(chosen)
    power = jnp.sum(chosen_real * chosen_real + chosen_imag * chosen_imag, axis=1)
    bound = jnp.max(power, axis=1) + epsilon
    rate = (1.0 / bound)[:, None, None]
    limit = rate * (shrink_scale * SIDE)
    weights = momentum_weights(ITERS)

    prior = None
    guess = None
    guess_spec = None
    for sweep in range(ITERS):
        if guess is None:
            residual_spec = -image_spec
        else:
            residual_spec = product_sum(chosen, guess_spec) - image_spec
        gradient = inverse(conj_times(chosen, residual_spec[:, None, :]).reshape(tiles_here * rows, width), table, weight)
        gradient = gradient.reshape(tiles_here, rows, pixels)
        if guess is None:
            moved = -(rate * gradient)
        else:
            moved = guess - rate * gradient
        fresh = moved - jnp.clip(moved, -limit, limit)
        if prior is None:
            guess = fresh + weights[sweep] * fresh
        else:
            guess = fresh + weights[sweep] * (fresh - prior)
        prior = fresh
        if sweep + 1 < ITERS:
            guess_spec = forward(guess.reshape(tiles_here * rows, pixels), table).reshape(tiles_here, rows, width)

    code_spec = forward(prior.reshape(tiles_here * rows, pixels), table).reshape(tiles_here, rows, width)
    recon_spec = product_sum(chosen, code_spec)
    recon = inverse(recon_spec, table, weight)
    residual_spec = recon_spec - image_spec
    slot_terms = conj_times(code_spec, residual_spec[:, None, :]).reshape(slot_count, BLK * width)
    member = (jnp.arange(NBLK, dtype=jnp.int32)[:, None] == flat_ids[None, :]).astype(jnp.float32)
    block_spec = jnp.dot(member, slot_terms, precision=highest, preferred_element_type=jnp.float32)
    partial = inverse(block_spec.reshape(NBLK * BLK, width), table, weight).reshape(NBLK, BLK, pixels)

    arrived = jnp.sum(lax.all_to_all(partial, "atom", 0, 0, tiled=True), axis=0)
    arrived = arrived.reshape(tile_count, 1, pixels)
    atom_grad = jnp.sum(lax.all_to_all(arrived, "tile", 0, 0, tiled=True), axis=0)

    scale = jnp.sqrt(jnp.mean(atom_grad * atom_grad, axis=-1, keepdims=True) + epsilon)
    atoms = unit_rows(own - step_ratio * atom_grad / scale)
    return (recon, atoms.reshape(dictionary.shape))


def solution(mesh):
    in_specs = (P(("tile", "atom"), None), P(("tile", "atom"), None), P("atom", "tile", None))
    out_specs = (P(("tile", "atom"), None), P("atom", "tile", None))
    return jax.shard_map(
        on_device, mesh=mesh, in_specs=in_specs, out_specs=out_specs, check_vma=False
    )
```

time: 506 us -> 125 us (0.25)
  waiting for transfers between devices: 295 us -> 20.4 us
  local copies, waits for them, and re-layouts: 61.4 us -> 5.76 us
  matrix products: 104 us -> 49.6 us
  blocking collectives: 0 us -> 18.5 us
  starting transfers between devices: 4.99 us -> 20.1 us
  between operations: 16.9 us -> 3 us
  other arithmetic: 18.9 us -> 6.86 us
    psum x1 -> x0, waiting for transfers between devices: 142 us -> none  [on_device(): total = lax.psum(owner_sum, 'tile')]
    all_gather x1 -> x0, waiting for transfers between devices: 104 us -> none  [on_device(): every = lax.all_gather(own_spec, ('tile', 'atom'), axis=0, tiled=True)]
    dot_general x17 -> x9, matrix products: 104 us -> 49.6 us  [the longest x4 27.1 us: inverse(): lax.dot_general(spectra * weight, table, (((spectra.ndim - 1,), (1,)), ((...]
    reshape x9 -> x2, local copies, waits for them, and re-layouts: 31 us -> 0.97 us  [the longest x1 0.73 us: on_device(): arrived = arrived.reshape(tile_count, 1, pixels)]
    all_to_all x1 -> x3, waiting for transfers between devices: 48.2 us -> 20.4 us  [the longest x1 9.2 us: on_device(): lax.all_to_all(jnp.broadcast_to(step[None], (atom_count, tile_count, 1, p...]
    all_to_all x0 -> x1, blocking collectives: none -> 18.5 us  [on_device(): arrived = jnp.sum(lax.all_to_all(partial, 'atom', 0, 0, tiled=True), axis=0)]
    transpose x4 -> x0, local copies, waits for them, and re-layouts: 18 us -> none  [forward(): jnp.einsum('cpdu,...udq->...cpq', forward_left, across, precision=highest...]
    all_to_all x1 -> x3, starting transfers between devices: 4.95 us -> 20.1 us  [the longest x1 11.3 us: on_device(): lax.all_to_all(jnp.broadcast_to(own[None], (tile_count, 1, pixels)), 'til...]
  transfers between devices with their start and end apart: 3 -> 3, of which waited for: 3 -> 3; matrix products, arithmetic and copies ran while one was open for 1% -> 12% of each run, Pallas kernels for 0% -> 0%
where the time goes in v1:
time: 125 us; the launch traced here: 124 us
  matrix products  49.6 us (40%)
  waiting for transfers between devices  20.4 us (16%)
  starting transfers between devices  20.1 us (16%)
  blocking collectives  18.5 us (15%)
  other arithmetic  6.86 us (5%)
  local copies, waits for them, and re-layouts  5.76 us (5%)
  between operations  3 us (2%)
    dot_general x4, matrix products, inverse(): lax.dot_general(spectra * weight, table, (((spectra.ndim - 1,), (1,)), ((...  27.1 us
    dot_general x4, matrix products, forward(): jnp.dot(values, table, precision=highest, preferred_element_type=jnp.floa...  21.7 us
    all_to_all x1, blocking collectives, on_device(): arrived = jnp.sum(lax.all_to_all(partial, 'atom', 0, 0, tiled=True), axis=0)  18.5 us
    all_to_all x1, starting transfers between devices, on_device(): lax.all_to_all(jnp.broadcast_to(own[None], (tile_count, 1, pixels)), 'til...  11.3 us
    all_to_all x1, waiting for transfers between devices, on_device(): lax.all_to_all(jnp.broadcast_to(step[None], (atom_count, tile_count, 1, p...  9.2 us
    all_to_all x1, waiting for transfers between devices, on_device(): lax.all_to_all(jnp.broadcast_to(own[None], (tile_count, 1, pixels)), 'til...  8.36 us
    all_to_all x1, starting transfers between devices, on_device(): lax.all_to_all(jnp.broadcast_to(step[None], (atom_count, tile_count, 1, p...  4.92 us
    all_to_all x1, starting transfers between devices, on_device(): lax.all_to_all(arrived, 'tile', 0, 0, tiled=True)  3.85 us
  transfers between devices with their start and end apart: 3, of which 3 were waited for; matrix products, arithmetic and copies ran while one was open for 12% of the time, Pallas kernels for 0%

profile of v1, /device:TPU:8, one launch (start us, length us, event | category | flops | bytes accessed | tf_op | source)
XLA Modules:
  0.0 124.2 jit_solution(6338626375884624927)
XLA Ops:
  0.6 0.0 copy-start
  0.6 1.3 %multiply_reduce_fusion.1 = f32[]{:T(128)} fusion(f32[1,1,1024]{2,1,0:T(1,128)} %param.7), kind=kLoop, calls=%fused_computation.62 | loop fusion | flops 2047 | bytes 4100 | tf_op jit(solution)/shard_map/reduce_sum | solution.py:36
  2.6 0.7 broadcast_divide_fusion
  3.3 0.7 broadcast_in_dim.52
  4.1 11.3 %all-to-all-start = ((f32[32,1,1024]{2,1,0:T(1,128)}), f32[32,1,1024]{2,1,0:T(1,128)S(1)}, u32[]{:S(2)}, u32[]{:S(2)}) async-start(f32[32,1,1024]{2,1,0:T(1,128)} %broadcast_in_dim.52), calls=%async_computation | async-start | bytes 262144 | tf_op jit(solution)/shard_map/all_to_all | solution.py:96
  15.4 0.7 compare_and_fusion
  16.1 0.8 copy.18
  16.8 0.1 reshape.224
  16.9 0.1 reshape.223
  17.0 0.1 copy.17
  17.1 0.1 broadcast_in_dim.48
  17.2 0.1 broadcast_in_dim.49
  17.3 8.4 %all-to-all-done = f32[32,1,1024]{2,1,0:T(1,128)S(1)} async-done(((f32[32,1,1024]{2,1,0:T(1,128)}), f32[32,1,1024]{2,1,0:T(1,128)S(1)}, u32[]{:S(2)}, u32[]{:S(2)}) %all-to-all-start) | async-done | bytes 131104 | tf_op jit(solution)/shard_map/all_to_all | solution.py:96
  25.7 1.1 broadcast_in_dim.54
  26.8 4.9 %all-to-all-start.1 = ((f32[8,32,1,1024]{3,1,2,0:T(8,128)}), f32[8,32,1,1024]{3,1,2,0:T(8,128)S(1)}, u32[]{:S(2)}, u32[]{:S(2)}) async-start(f32[8,32,1,1024]{3,1,2,0:T(8,128)} %broadcast_in_dim.54), calls=%async_computation.1 | async-start | bytes 2097152 | tf_op jit(solution)/shard_map/all_to_all | solution.py:97
  31.7 5.2 %convolution_bitcast_fusion = f32[4,1280]{1,0:T(4,128)S(1)} fusion(f32[1024,1280]{1,0:T(8,128)} %constant.45.clone, f32[4,1024]{1,0:T(4,128)S(1)} %copy-done), kind=kOutput, calls=%fused_computation.2 | convolution fusion | flops 62914560 | bytes 5279744 | tf_op jit(solution)/shard_map/dot_general | solution.py:56
  37.0 9.2 %all-to-all-done.1 = f32[8,32,1,1024]{3,1,2,0:T(8,128)S(1)} async-done(((f32[8,32,1,1024]{3,1,2,0:T(8,128)}), f32[8,32,1,1024]{3,1,2,0:T(8,128)S(1)}, u32[]{:S(2)}, u32[]{:S(2)}) %all-to-all-start.1) | async-done | bytes 1048608 | tf_op jit(solution)/shard_map/all_to_all | solution.py:97
  46.2 0.6 copy.22
  46.8 0.9 gather_fusion
  47.7 0.2 gather.7
  47.9 7.0 %fusion.12 = f32[4,64,1280]{2,1,0:T(8,128)S(1)} fusion(f32[1024,1280,1]{1,0,2:T(8,128)} %constant.50, f32[4,64,1024]{2,1,0:T(8,128)S(1)} %gather.7, pred[4,64]{1,0:T(4,128)(4,1)S(1)} %broadcast_in_dim.49), kind=kOutput, calls=%fused_computation.21 | convolution fusion | flops 4026793984 | bytes 7602432 | tf_op jit(solution)/shard_map/dot_general | solution.py:56
  54.9 0.0 copy-start.1
  54.9 0.0 slice-start
  54.9 1.1 multiply_add_fusion.3
  56.0 0.1 reduce_max.9
  56.1 0.0 slice-start.1
  56.2 7.7 %multiply_add_fusion = f32[4,64,1024]{2,1,0:T(8,128)S(1)} fusion(f32[1024,1280,1]{1,0,2:T(8,128)} %constant.50, f32[4,64,640]{2,1,0:T(8,128)} %get-tuple-element.13, f32[4,64,640]{2,1,0:T(8,128)S(1)} %get-tuple-element.12, f32[1280]{0:T(1024)S(1)} %copy-done.1, f32[4]{0:T(128)S(1)} %fusion.34, f32[4]{0:T(128)S(1)} %get-tuple-element.6, ...), kind=kOutput, calls=%fused_computation.3 | convolution fusion | flops 4029022208 | bytes 7607344 | tf_op jit(solution)/shard_map/dot_general | solution.py:60
  63.9 4.6 %fusion.35 = f32[4,64,1280]{2,1,0:T(8,128)S(1)} fusion(f32[4,64,1024]{2,1,0:T(8,128)S(1)} %multiply_add_fusion, f32[1024,1280,1]{1,0,2:T(8,128)S(1)} %bitcast.57), kind=kOutput, calls=%fused_computation.78 | convolution fusion | flops 4026531840 | bytes 7602176 | tf_op jit(solution)/shard_map/dot_general | solution.py:56
  68.5 0.3 subtract_reduce_fusion.1
  68.8 0.1 multiply_add_fusion.2
  69.0 4.6 %fusion.1 = f32[4,64,1024]{2,1,0:T(8,128)S(1)} fusion(f32[4,64,1024]{2,1,0:T(8,128)S(1)} %multiply_add_fusion, f32[1024,1280,1]{1,0,2:T(8,128)S(1)} %bitcast.57, f32[4,64,640]{2,1,0:T(8,128)S(1)} %get-tuple-element.11, f32[4,64,640]{2,1,0:T(8,128)S(1)} %get-tuple-element.10, f32[1280]{0:T(1024)S(1)} %copy-done.1, f32[4]{0:T(128)S(1)} %get-tuple-element.7), kind=kOutput, calls=%fused_computation.7 | convolution fusion | flops 4027711488 | bytes 8655888 | tf_op jit(solution)/shard_map/dot_general | solution.py:60
  73.6 4.9 %fusion.8 = f32[4,64,1280]{2,1,0:T(8,128)S(1)} fusion(f32[1024,1280,1]{1,0,2:T(8,128)S(1)} %bitcast.57, f32[4,64,1024]{2,1,0:T(8,128)S(1)} %fusion.1, f32[4]{0:T(128)S(1)} %fusion.34, f32[4]{0:T(128)S(1)} %get-tuple-element.6), kind=kOutput, calls=%fused_computation.17 | convolution fusion | flops 4027318272 | bytes 7602208 | tf_op jit(solution)/shard_map/dot_general | solution.py:56
  78.4 0.3 subtract_reduce_fusion
  78.8 0.1 multiply_add_fusion.1
  78.9 0.1 pad_maximum_fusion
  79.0 0.2 reshape.225
  79.3 0.7 convolution_multiply_fusion
  80.0 7.4 %fusion.6 = f32[8,32,1024]{2,1,0:T(8,128)S(1)} fusion(f32[1024,1280,1]{1,0,2:T(8,128)} %constant.50, f32[8,32,1280]{2,0,1:T(8,128)S(1)} %convolution_multiply_fusion), kind=kOutput, calls=%fused_computation.15 | convolution fusion | flops 4026531840 | bytes 7602176 | tf_op jit(solution)/shard_map/dot_general | solution.py:60
  87.4 18.5 %all_to_all.20 = f32[8,32,1024]{2,1,0:T(8,128)S(1)} all-to-all(f32[8,32,1024]{2,1,0:T(8,128)S(1)} %fusion.6), channel_id=1, replica_groups=mesh['tile'=32,'atom'=8] {'atom'}, dimensions={0} | all-to-all | bytes 2097152 | tf_op jit(solution)/shard_map/all_to_all | solution.py:147
  105.9 0.1 reduce_sum.96
  106.0 0.7 reshape.226
  106.7 3.9 %all-to-all-start.3 = ((f32[32,1,1024]{2,1,0:T(1,128)}), f32[32,1,1024]{2,1,0:T(1,128)S(1)}, u32[]{:S(2)}, u32[]{:S(2)}) async-start(f32[32,1,1024]{2,1,0:T(1,128)} %reshape.226), calls=%async_computation.3 | async-start | bytes 262144 | tf_op jit(solution)/shard_map/all_to_all | solution.py:149
  110.6 7.4 %fusion.21 = f32[4,1024]{1,0:T(4,128)} fusion(f32[1024,1280]{1,0:T(8,128)} %constant.45.clone, f32[4,640]{1,0:T(4,128)S(1)} %get-tuple-element.3, f32[4,640]{1,0:T(4,128)S(1)} %get-tuple-element.2, f32[1280]{0:T(1024)S(1)} %copy-done.1), kind=kOutput, calls=%fused_computation.46 | convolution fusion | flops 62924800 | bytes 5284864 | tf_op jit(solution)/shard_map/dot_general | solution.py:60
  118.0 2.9 %all-to-all-done.3 = f32[32,1,1024]{2,1,0:T(1,128)S(1)} async-done(((f32[32,1,1024]{2,1,0:T(1,128)}), f32[32,1,1024]{2,1,0:T(1,128)S(1)}, u32[]{:S(2)}, u32[]{:S(2)}) %all-to-all-start.3) | async-done | bytes 131104 | tf_op jit(solution)/shard_map/all_to_all | solution.py:149
  120.8 0.1 reduce_sum.97
  120.9 0.6 multiply_reduce_fusion
  122.2 0.6 fusion.25
  123.5 0.6 subtract_divide_fusion
  (19 shorter events, 0.1 us)
Async XLA Ops:
  0.6 31.1 %copy-start = (f32[4,1024]{1,0:T(4,128)S(1)}, f32[4,1024]{1,0:T(4,128)}, u32[]{:S(2)}) copy-start(f32[4,1024]{1,0:T(4,128)} %param.5) | copy-start | bytes 49156
  4.1 21.6 %all-to-all-start = ((f32[32,1,1024]{2,1,0:T(1,128)}), f32[32,1,1024]{2,1,0:T(1,128)S(1)}, u32[]{:S(2)}, u32[]{:S(2)}) async-start(f32[32,1,1024]{2,1,0:T(1,128)} %broadcast_in_dim.52), calls=%async_computation | async-start | bytes 262144 | tf_op jit(solution)/shard_map/all_to_all | solution.py:96
  26.8 19.4 %all-to-all-start.1 = ((f32[8,32,1,1024]{3,1,2,0:T(8,128)}), f32[8,32,1,1024]{3,1,2,0:T(8,128)S(1)}, u32[]{:S(2)}, u32[]{:S(2)}) async-start(f32[8,32,1,1024]{3,1,2,0:T(8,128)} %broadcast_in_dim.54), calls=%async_computation.1 | async-start | bytes 2097152 | tf_op jit(solution)/shard_map/all_to_all | solution.py:97
  54.9 1.2 copy-start.1
  54.9 9.0 %slice-start = ((s8[5242880]{0:T(1024)(128)(4,1)}), s8[1048576]{0:T(1024)(128)(4,1)S(1)}, s32[]{:S(2)}) async-start(s8[5242880]{0:T(1024)(128)(4,1)} %bitcast.56), calls=%async_computation.4 | async-start | bytes 2097152
  56.1 7.8 %slice-start.1 = ((s8[5242880]{0:T(1024)(128)(4,1)}), s8[4194304]{0:T(1024)(128)(4,1)S(1)}, s32[]{:S(2)}) async-start(s8[5242880]{0:T(1024)(128)(4,1)} %bitcast.56), calls=%async_computation.5 | async-start | bytes 8388608
  106.7 14.1 %all-to-all-start.3 = ((f32[32,1,1024]{2,1,0:T(1,128)}), f32[32,1,1024]{2,1,0:T(1,128)S(1)}, u32[]{:S(2)}, u32[]{:S(2)}) async-start(f32[32,1,1024]{2,1,0:T(1,128)} %reshape.226), calls=%async_computation.3 | async-start | bytes 262144 | tf_op jit(solution)/shard_map/all_to_all | solution.py:149
  110.6 11.7 %copy-start.2 = (f32[1,1,1024]{2,1,0:T(1,128)S(1)}, f32[1,1,1024]{2,1,0:T(1,128)}, u32[]{:S(2)}) copy-start(f32[1,1,1024]{2,1,0:T(1,128)} %param.7) | copy-start | bytes 12292

commit v2 on v1

--- a/solution.py
+++ b/solution.py
@@ -16,6 +16,7 @@
 step_ratio = 0.5
 epsilon = 1e-06
 highest = lax.Precision.HIGHEST
+fast = lax.Precision.HIGH
 
 HALF = SIDE // 2 + 1
 USED = SIDE * HALF
@@ -53,13 +54,13 @@
 
 
 def forward(values, table):
-    return jnp.dot(values, table, precision=highest, preferred_element_type=jnp.float32)
+    return jnp.dot(values, table, precision=fast, preferred_element_type=jnp.float32)
 
 
 def inverse(spectra, table, weight):
     return lax.dot_general(
         spectra * weight, table, (((spectra.ndim - 1,), (1,)), ((), ())),
-        precision=highest, preferred_element_type=jnp.float32,
+        precision=fast, preferred_element_type=jnp.float32,
     )
 
 
@@ -90,6 +91,7 @@
     table_host, weight_host = half_table()
     table = jnp.asarray(table_host)
     weight = jnp.asarray(weight_host)
+    table, weight = lax.optimization_barrier((table, weight))
     width = table.shape[1]
 
     own = unit_rows(dictionary.reshape(1, pixels))
@@ -99,7 +101,7 @@
     )
     every = every.reshape(atom_count, tile_count * pixels)
 
-    image_spec = forward(images, table)
+    image_spec = forward(images.reshape(1, tiles_here, pixels), table).reshape(tiles_here, width)
     slot_count = tiles_here * ACT
     flat_ids = active.reshape(slot_count)
     chosen_atoms = jnp.take(every, flat_ids, axis=0).reshape(slot_count * BLK, pixels)
@@ -137,12 +139,13 @@
 
     code_spec = forward(prior.reshape(tiles_here * rows, pixels), table).reshape(tiles_here, rows, width)
     recon_spec = product_sum(chosen, code_spec)
-    recon = inverse(recon_spec, table, weight)
     residual_spec = recon_spec - image_spec
     slot_terms = conj_times(code_spec, residual_spec[:, None, :]).reshape(slot_count, BLK * width)
     member = (jnp.arange(NBLK, dtype=jnp.int32)[:, None] == flat_ids[None, :]).astype(jnp.float32)
     block_spec = jnp.dot(member, slot_terms, precision=highest, preferred_element_type=jnp.float32)
-    partial = inverse(block_spec.reshape(NBLK * BLK, width), table, weight).reshape(NBLK, BLK, pixels)
+    both = inverse(jnp.concatenate([block_spec.reshape(NBLK * BLK, width), recon_spec], axis=0), table, weight)
+    partial = both[:NBLK * BLK].reshape(NBLK, BLK, pixels)
+    recon = both[NBLK * BLK:]
 
     arrived = jnp.sum(lax.all_to_all(partial, "atom", 0, 0, tiled=True), axis=0)
     arrived = arrived.reshape(tile_count, 1, pixels)

time: 125 us -> 112 us (0.90)
  matrix products: 49.6 us -> 27.2 us
  waiting for transfers between devices: 20.4 us -> 28.8 us
    dot_general x4 -> x3, matrix products: 27.1 us -> 12.7 us  [inverse(): lax.dot_general(spectra * weight, table, (((spectra.ndim - 1,), (1,)), ((...]
    dot_general x4, matrix products: 21.7 us -> 13.9 us  [forward(): jnp.dot(values, table, precision=fast, preferred_element_type=jnp.float32)]
    all_to_all x1, waiting for transfers between devices: 2.86 us -> 9.66 us  [on_device(): lax.all_to_all(arrived, 'tile', 0, 0, tiled=True)]
    all_to_all x1, waiting for transfers between devices: 9.2 us -> 10.8 us  [on_device(): lax.all_to_all(jnp.broadcast_to(step[None], (atom_count, tile_count, 1, p...]
  transfers between devices with their start and end apart: 3 -> 3, of which waited for: 3 -> 3; matrix products, arithmetic and copies ran while one was open for 12% -> 6% of each run, Pallas kernels for 0% -> 0%
where the time goes in v2:
time: 112 us; the launch traced here: 111 us
  waiting for transfers between devices  28.8 us (26%)
  matrix products  27.2 us (24%)
  starting transfers between devices  20.1 us (18%)
  blocking collectives  18.5 us (17%)
  other arithmetic  6.84 us (6%)
  local copies, waits for them, and re-layouts  6.63 us (6%)
  between operations  3 us (3%)
    all_to_all x1, blocking collectives, on_device(): arrived = jnp.sum(lax.all_to_all(partial, 'atom', 0, 0, tiled=True), axis=0)  18.5 us
    dot_general x4, matrix products, forward(): jnp.dot(values, table, precision=fast, preferred_element_type=jnp.float32)  13.9 us
    dot_general x3, matrix products, inverse(): lax.dot_general(spectra * weight, table, (((spectra.ndim - 1,), (1,)), ((...  12.7 us
    all_to_all x1, starting transfers between devices, on_device(): lax.all_to_all(jnp.broadcast_to(own[None], (tile_count, 1, pixels)), 'til...  11.3 us
    all_to_all x1, waiting for transfers between devices, on_device(): lax.all_to_all(jnp.broadcast_to(step[None], (atom_count, tile_count, 1, p...  10.8 us
    all_to_all x1, waiting for transfers between devices, on_device(): lax.all_to_all(arrived, 'tile', 0, 0, tiled=True)  9.66 us
    all_to_all x1, waiting for transfers between devices, on_device(): lax.all_to_all(jnp.broadcast_to(own[None], (tile_count, 1, pixels)), 'til...  8.36 us
    all_to_all x1, starting transfers between devices, on_device(): lax.all_to_all(jnp.broadcast_to(step[None], (atom_count, tile_count, 1, p...  4.92 us
  transfers between devices with their start and end apart: 3, of which 3 were waited for; matrix products, arithmetic and copies ran while one was open for 6% of the time, Pallas kernels for 0%

profile of v2, /device:TPU:8, one launch (start us, length us, event | category | flops | bytes accessed | tf_op | source)
XLA Modules:
  0.0 111.1 jit_solution(15737159573557270499)
XLA Ops:
  0.6 0.0 copy-start
  0.6 1.3 %multiply_reduce_fusion.1 = f32[]{:T(128)} fusion(f32[1,1,1024]{2,1,0:T(1,128)} %param.7), kind=kLoop, calls=%fused_computation.70 | loop fusion | flops 2047 | bytes 4100 | tf_op jit(solution)/shard_map/reduce_sum | solution.py:37
  2.6 0.7 broadcast_divide_fusion
  3.3 0.7 broadcast_in_dim.51
  4.1 11.3 %all-to-all-start = ((f32[32,1,1024]{2,1,0:T(1,128)}), f32[32,1,1024]{2,1,0:T(1,128)S(1)}, u32[]{:S(2)}, u32[]{:S(2)}) async-start(f32[32,1,1024]{2,1,0:T(1,128)} %broadcast_in_dim.51), calls=%async_computation | async-start | bytes 262144 | tf_op jit(solution)/shard_map/all_to_all | solution.py:98
  15.4 0.7 compare_and_fusion
  16.1 0.8 copy.16
  16.8 0.1 reshape.224
  16.9 0.1 eq.16
  17.0 0.1 copy.17
  17.1 0.1 broadcast_in_dim.47
  17.2 0.1 broadcast_in_dim.48
  17.3 8.4 %all-to-all-done = f32[32,1,1024]{2,1,0:T(1,128)S(1)} async-done(((f32[32,1,1024]{2,1,0:T(1,128)}), f32[32,1,1024]{2,1,0:T(1,128)S(1)}, u32[]{:S(2)}, u32[]{:S(2)}) %all-to-all-start) | async-done | bytes 131104 | tf_op jit(solution)/shard_map/all_to_all | solution.py:98
  25.7 1.1 broadcast_in_dim.53
  26.8 4.9 %all-to-all-start.1 = ((f32[8,32,1,1024]{3,1,2,0:T(8,128)}), f32[8,32,1,1024]{3,1,2,0:T(8,128)S(1)}, u32[]{:S(2)}, u32[]{:S(2)}) async-start(f32[8,32,1,1024]{3,1,2,0:T(8,128)} %broadcast_in_dim.53), calls=%async_computation.1 | async-start | bytes 2097152 | tf_op jit(solution)/shard_map/all_to_all | solution.py:99
  31.7 3.7 %convolution_bitcast_fusion = f32[4,1280]{1,0:T(4,128)S(1)} fusion(f32[1024,1280]{1,0:T(8,128)} %constant.45.clone, f32[4,1024]{1,0:T(4,128)S(1)} %copy-done), kind=kOutput, calls=%fused_computation.11 | convolution fusion | flops 31457280 | bytes 5279744 | tf_op jit(solution)/shard_map/dot_general | solution.py:57
  35.4 10.8 %all-to-all-done.1 = f32[8,32,1,1024]{3,1,2,0:T(8,128)S(1)} async-done(((f32[8,32,1,1024]{3,1,2,0:T(8,128)}), f32[8,32,1,1024]{3,1,2,0:T(8,128)S(1)}, u32[]{:S(2)}, u32[]{:S(2)}) %all-to-all-start.1) | async-done | bytes 1048608 | tf_op jit(solution)/shard_map/all_to_all | solution.py:99
  46.2 0.6 copy.20
  46.8 0.9 gather_fusion
  47.7 0.2 gather.7
  47.9 5.0 %fusion.8 = f32[4,64,1280]{2,1,0:T(8,128)S(1)} fusion(f32[1024,1280]{1,0:T(8,128)} %constant.45.clone, f32[4,64,1024]{2,1,0:T(8,128)S(1)} %gather.7, pred[4,64]{1,0:T(4,128)(4,1)S(1)} %broadcast_in_dim.48), kind=kOutput, calls=%fused_computation.9 | convolution fusion | flops 2013528064 | bytes 7602432 | tf_op jit(solution)/shard_map/dot_general | solution.py:57
  52.9 0.0 slice-start
  52.9 1.1 multiply_add_fusion.3
  54.0 0.1 reduce_max.9
  54.1 5.2 %multiply_add_fusion = f32[4,64,1024]{2,1,0:T(8,128)S(1)} fusion(f32[1024,1280]{1,0:T(8,128)} %constant.45.clone, f32[4,64,640]{2,1,0:T(8,128)} %get-tuple-element.17, f32[4,64,640]{2,1,0:T(8,128)S(1)} %get-tuple-element.16, f32[1280]{0:T(1024)S(1)} %copy-done.1, f32[4]{0:T(128)S(1)} %fusion.55, f32[4]{0:T(128)S(1)} %get-tuple-element.10, ...), kind=kOutput, calls=%fused_computation.12 | convolution fusion | flops 2015756288 | bytes 7607344 | tf_op jit(solution)/shard_map/dot_general | solution.py:61
  59.4 2.6 %fusion.4 = f32[4,64,1280]{2,1,0:T(8,128)S(1)} fusion(f32[4,64,1024]{2,1,0:T(8,128)S(1)} %multiply_add_fusion, f32[1024,1280]{1,0:T(8,128)S(1)} %bitcast.66), kind=kOutput, calls=%fused_computation.5 | convolution fusion | flops 2013265920 | bytes 7602176 | tf_op jit(solution)/shard_map/dot_general | solution.py:57
  62.0 0.3 subtract_reduce_fusion.1
  62.3 0.1 multiply_add_fusion.2
  62.4 2.6 %fusion.19 = f32[4,64,1024]{2,1,0:T(8,128)S(1)} fusion(f32[4,64,1024]{2,1,0:T(8,128)S(1)} %multiply_add_fusion, f32[1024,1280]{1,0:T(8,128)S(1)} %bitcast.66, f32[4,64,640]{2,1,0:T(8,128)S(1)} %get-tuple-element.15, f32[4,64,640]{2,1,0:T(8,128)S(1)} %get-tuple-element.14, f32[1280]{0:T(1024)S(1)} %copy-done.1, f32[4]{0:T(128)S(1)} %get-tuple-element.11), kind=kOutput, calls=%fused_computation.16 | convolution fusion | flops 2014445568 | bytes 8655888 | tf_op jit(solution)/shard_map/dot_general | solution.py:61
  65.0 2.6 %fusion = f32[4,64,1280]{2,1,0:T(8,128)S(1)} fusion(f32[1024,1280]{1,0:T(8,128)S(1)} %bitcast.66, f32[4,64,1024]{2,1,0:T(8,128)S(1)} %fusion.19, f32[4]{0:T(128)S(1)} %fusion.55, f32[4]{0:T(128)S(1)} %get-tuple-element.10), kind=kOutput, calls=%fused_computation.1 | convolution fusion | flops 2014052352 | bytes 7602208 | tf_op jit(solution)/shard_map/dot_general | solution.py:57
  67.7 0.3 subtract_reduce_fusion
  68.0 0.1 multiply_add_fusion.1
  68.1 0.1 pad_maximum_fusion
  68.2 0.2 reshape.225
  68.5 0.7 fusion.48
  69.2 0.2 reshape.226
  69.4 4.9 %fusion.22 = f32[260,1024]{1,0:T(8,128)S(1)} fusion(f32[1024,1280]{1,0:T(8,128)} %constant.45.clone, f32[4,640]{1,0:T(4,128)S(1)} %get-tuple-element.7, f32[4,640]{1,0:T(4,128)S(1)} %get-tuple-element.6, f32[256,1280]{1,0:T(8,128)S(1)} %reshape.226, f32[1280]{0:T(1024)S(1)} %copy-done.1), kind=kOutput, calls=%fused_computation.18 | convolution fusion | flops 2045721600 | bytes 7644160 | tf_op jit(solution)/shard_map/dot_general | solution.py:61
  74.3 0.1 slice.81
  74.3 18.5 %all_to_all.20 = f32[8,32,1024]{2,1,0:T(8,128)S(1)} all-to-all(f32[8,32,1024]{2,1,0:T(8,128)S(1)} %bitcast.69), channel_id=1, replica_groups=mesh['tile'=32,'atom'=8] {'atom'}, dimensions={0} | all-to-all | bytes 2097152 | tf_op jit(solution)/shard_map/all_to_all | solution.py:150
  92.8 0.1 reduce_sum.96
  92.9 0.7 reshape.228
  93.6 3.9 %all-to-all-start.3 = ((f32[32,1,1024]{2,1,0:T(1,128)}), f32[32,1,1024]{2,1,0:T(1,128)S(1)}, u32[]{:S(2)}, u32[]{:S(2)}) async-start(f32[32,1,1024]{2,1,0:T(1,128)} %reshape.228), calls=%async_computation.3 | async-start | bytes 262144 | tf_op jit(solution)/shard_map/all_to_all | solution.py:152
  97.5 0.6 slice.80
  98.1 9.7 %all-to-all-done.3 = f32[32,1,1024]{2,1,0:T(1,128)S(1)} async-done(((f32[32,1,1024]{2,1,0:T(1,128)}), f32[32,1,1024]{2,1,0:T(1,128)S(1)}, u32[]{:S(2)}, u32[]{:S(2)}) %all-to-all-start.3) | async-done | bytes 131104 | tf_op jit(solution)/shard_map/all_to_all | solution.py:152
  107.7 0.1 reduce_sum.97
  107.8 0.6 multiply_reduce_fusion
  109.2 0.6 fusion.47
  110.5 0.6 subtract_divide_fusion
  (21 shorter events, 0.1 us)
Async XLA Ops:
  0.6 31.1 %copy-start = (f32[4,1024]{1,0:T(4,128)S(1)}, f32[4,1024]{1,0:T(4,128)}, u32[]{:S(2)}) copy-start(f32[4,1024]{1,0:T(4,128)} %param.5) | copy-start | bytes 49156
  4.1 21.6 %all-to-all-start = ((f32[32,1,1024]{2,1,0:T(1,128)}), f32[32,1,1024]{2,1,0:T(1,128)S(1)}, u32[]{:S(2)}, u32[]{:S(2)}) async-start(f32[32,1,1024]{2,1,0:T(1,128)} %broadcast_in_dim.51), calls=%async_computation | async-start | bytes 262144 | tf_op jit(solution)/shard_map/all_to_all | solution.py:98
  26.8 19.4 %all-to-all-start.1 = ((f32[8,32,1,1024]{3,1,2,0:T(8,128)}), f32[8,32,1,1024]{3,1,2,0:T(8,128)S(1)}, u32[]{:S(2)}, u32[]{:S(2)}) async-start(f32[8,32,1,1024]{3,1,2,0:T(8,128)} %broadcast_in_dim.53), calls=%async_computation.1 | async-start | bytes 2097152 | tf_op jit(solution)/shard_map/all_to_all | solution.py:99
  52.9 1.2 %copy-start.1 = (f32[1280]{0:T(1024)S(1)}, f32[1280]{0:T(1024)}, u32[]{:S(2)}) copy-start(f32[1280]{0:T(1024)} %constant.46.clone) | copy-start | bytes 15364
  52.9 6.5 %slice-start = ((s8[5242880]{0:T(1024)(128)(4,1)}), s8[1048576]{0:T(1024)(128)(4,1)S(1)}, s32[]{:S(2)}) async-start(s8[5242880]{0:T(1024)(128)(4,1)} %bitcast.65), calls=%async_computation.4 | async-start | bytes 2097152
  54.1 5.3 %slice-start.1 = ((s8[5242880]{0:T(1024)(128)(4,1)}), s8[4194304]{0:T(1024)(128)(4,1)S(1)}, s32[]{:S(2)}) async-start(s8[5242880]{0:T(1024)(128)(4,1)} %bitcast.65), calls=%async_computation.5 | async-start | bytes 8388608
  92.8 16.3 %copy-start.2 = (f32[1,1,1024]{2,1,0:T(1,128)S(1)}, f32[1,1,1024]{2,1,0:T(1,128)}, u32[]{:S(2)}) copy-start(f32[1,1,1024]{2,1,0:T(1,128)} %param.7) | copy-start | bytes 12292
  93.6 14.1 %all-to-all-start.3 = ((f32[32,1,1024]{2,1,0:T(1,128)}), f32[32,1,1024]{2,1,0:T(1,128)S(1)}, u32[]{:S(2)}, u32[]{:S(2)}) async-start(f32[32,1,1024]{2,1,0:T(1,128)} %reshape.228), calls=%async_computation.3 | async-start | bytes 262144 | tf_op jit(solution)/shard_map/all_to_all | solution.py:152

commit v3 on v2

--- a/solution.py
+++ b/solution.py
@@ -96,15 +96,23 @@
 
     own = unit_rows(dictionary.reshape(1, pixels))
     step = lax.all_to_all(jnp.broadcast_to(own[None], (tile_count, 1, pixels)), "tile", 0, 0, tiled=True)
-    every = lax.all_to_all(
-        jnp.broadcast_to(step[None], (atom_count, tile_count, 1, pixels)), "atom", 0, 0, tiled=True
-    )
-    every = every.reshape(atom_count, tile_count * pixels)
+    mine = step.reshape(1, tile_count * pixels)
+    place = lax.axis_index("atom")
+    core = place % 2
+    chips = atom_count // 2
+    chip = place // 2
+    other = lax.ppermute(mine, "atom", [(i, i ^ 1) for i in range(atom_count)])
+    pair = jnp.where(core == 0, jnp.concatenate([mine, other]), jnp.concatenate([other, mine]))
+    pieces = [pair]
+    for hop in range(1, chips):
+        pieces.append(lax.ppermute(pair, "atom", [(i, ((i // 2 + hop) % chips) * 2 + i % 2) for i in range(atom_count)]))
+    every = jnp.concatenate(pieces, axis=0)
 
     image_spec = forward(images.reshape(1, tiles_here, pixels), table).reshape(tiles_here, width)
     slot_count = tiles_here * ACT
     flat_ids = active.reshape(slot_count)
-    chosen_atoms = jnp.take(every, flat_ids, axis=0).reshape(slot_count * BLK, pixels)
+    where_held = ((chip - flat_ids // 2) % chips) * 2 + flat_ids % 2
+    chosen_atoms = jnp.take(every, where_held, axis=0).reshape(slot_count * BLK, pixels)
     rows = ACT * BLK
     chosen = forward(chosen_atoms, table).reshape(tiles_here, rows, width)
     chosen_real, chosen_imag = parts(chosen)
@@ -147,7 +155,14 @@
     partial = both[:NBLK * BLK].reshape(NBLK, BLK, pixels)
     recon = both[NBLK * BLK:]
 
-    arrived = jnp.sum(lax.all_to_all(partial, "atom", 0, 0, tiled=True), axis=0)
+    paired = partial.reshape(chips, 2, BLK, pixels)
+    keep = lax.dynamic_index_in_dim(paired, core, axis=1, keepdims=False)
+    give = lax.dynamic_index_in_dim(paired, 1 - core, axis=1, keepdims=False)
+    summed = keep + lax.ppermute(give, "atom", [(i, i ^ 1) for i in range(atom_count)])
+    arrived = lax.dynamic_index_in_dim(summed, chip, axis=0, keepdims=False)
+    for hop in range(1, chips):
+        sent = lax.dynamic_index_in_dim(summed, (chip + hop) % chips, axis=0, keepdims=False)
+        arrived = arrived + lax.ppermute(sent, "atom", [(i, ((i // 2 + hop) % chips) * 2 + i % 2) for i in range(atom_count)])
     arrived = arrived.reshape(tile_count, 1, pixels)
     atom_grad = jnp.sum(lax.all_to_all(arrived, "tile", 0, 0, tiled=True), axis=0)
 

time: 112 us -> 103 us (0.920)
  blocking collectives: 18.5 us -> 0 us
  waiting for transfers between devices: 28.8 us -> 36.4 us
  starting transfers between devices: 20.1 us -> 24.7 us
  local copies, waits for them, and re-layouts: 6.63 us -> 4.37 us
    ppermute x0 -> x8, waiting for transfers between devices: none -> 20.2 us  [the longest x3 10.8 us: on_device(): lax.ppermute(pair, 'atom', [(i, (i // 2 + hop) % chips * 2 + i % 2) for i...]
    all_to_all x1 -> x0, blocking collectives: 18.5 us -> none  [on_device(): arrived = jnp.sum(lax.all_to_all(partial, 'atom', 0, 0, tiled=True), axis=0)]
    all_to_all x1 -> x0, waiting for transfers between devices: 10.8 us -> none  [on_device(): lax.all_to_all(jnp.broadcast_to(step[None], (atom_count, tile_count, 1, p...]
    ppermute x0 -> x8, starting transfers between devices: none -> 9.59 us  [the longest x3 5 us: on_device(): lax.ppermute(pair, 'atom', [(i, (i // 2 + hop) % chips * 2 + i % 2) for i...]
    all_to_all x1 -> x0, starting transfers between devices: 4.92 us -> none  [on_device(): lax.all_to_all(jnp.broadcast_to(step[None], (atom_count, tile_count, 1, p...]
    all_to_all x1, waiting for transfers between devices: 8.36 us -> 6.32 us  [on_device(): lax.all_to_all(jnp.broadcast_to(own[None], (tile_count, 1, pixels)), 'til...]
    unnamed x13, local copies, waits for them, and re-layouts: 1.43 us -> 0.14 us
  transfers between devices with their start and end apart: 3 -> 10, of which waited for: 3 -> 10; matrix products, arithmetic and copies ran while one was open for 6% -> 5% of each run, Pallas kernels for 0% -> 0%
where the time goes in v3:
time: 103 us
  waiting for transfers between devices  36.4 us (35%)
  matrix products  27.3 us (27%)
  starting transfers between devices  24.7 us (24%)
  other arithmetic  7.1 us (7%)
  local copies, waits for them, and re-layouts  4.37 us (4%)
  between operations  3.15 us (3%)
    dot_general x4, matrix products, forward(): jnp.dot(values, table, precision=fast, preferred_element_type=jnp.float32)  14.1 us
    dot_general x3, matrix products, inverse(): lax.dot_general(spectra * weight, table, (((spectra.ndim - 1,), (1,)), ((...  12.5 us
    all_to_all x1, starting transfers between devices, on_device(): lax.all_to_all(jnp.broadcast_to(own[None], (tile_count, 1, pixels)), 'til...  11.3 us
    ppermute x3, waiting for transfers between devices, on_device(): lax.ppermute(pair, 'atom', [(i, (i // 2 + hop) % chips * 2 + i % 2) for i...  10.8 us
    all_to_all x1, waiting for transfers between devices, on_device(): lax.all_to_all(arrived, 'tile', 0, 0, tiled=True)  9.93 us
    all_to_all x1, waiting for transfers between devices, on_device(): lax.all_to_all(jnp.broadcast_to(own[None], (tile_count, 1, pixels)), 'til...  6.32 us
    ppermute x3, waiting for transfers between devices, on_device(): lax.ppermute(sent, 'atom', [(i, (i // 2 + hop) % chips * 2 + i % 2) for i...  6.24 us
    ppermute x3, starting transfers between devices, on_device(): lax.ppermute(pair, 'atom', [(i, (i // 2 + hop) % chips * 2 + i % 2) for i...  5 us
  transfers between devices with their start and end apart: 10, of which 10 were waited for; matrix products, arithmetic and copies ran while one was open for 5% of the time, Pallas kernels for 0%

profile of v3, /device:TPU:8, one launch (start us, length us, event | category | flops | bytes accessed | tf_op | source)
XLA Modules:
  0.0 103.1 jit_solution(4468801643857288005)
XLA Ops:
  0.6 1.3 %multiply_reduce_fusion.1 = f32[]{:T(128)} fusion(f32[1,1,1024]{2,1,0:T(1,128)} %param.7), kind=kLoop, calls=%fused_computation.79 | loop fusion | flops 2047 | bytes 4100 | tf_op jit(solution)/shard_map/reduce_sum | solution.py:37
  2.6 0.7 broadcast_divide_fusion
  3.3 0.7 broadcast_in_dim.43
  4.1 11.3 %all-to-all-start = ((f32[32,1,1024]{2,1,0:T(1,128)}), f32[32,1,1024]{2,1,0:T(1,128)S(1)}, u32[]{:S(2)}, u32[]{:S(2)}) async-start(f32[32,1,1024]{2,1,0:T(1,128)} %broadcast_in_dim.43), calls=%async_computation | async-start | bytes 262144 | tf_op jit(solution)/shard_map/all_to_all | solution.py:98
  15.4 3.7 %convolution_bitcast_fusion = f32[4,1280]{1,0:T(4,128)S(1)} fusion(f32[1024,1280]{1,0:T(8,128)} %constant.137.clone, f32[4,1024]{1,0:T(4,128)S(1)} %copy-done), kind=kOutput, calls=%fused_computation.11 | convolution fusion | flops 31457280 | bytes 5279744 | tf_op jit(solution)/shard_map/dot_general | solution.py:57
  19.3 6.3 %all-to-all-done = f32[32,1,1024]{2,1,0:T(1,128)S(1)} async-done(((f32[32,1,1024]{2,1,0:T(1,128)}), f32[32,1,1024]{2,1,0:T(1,128)S(1)}, u32[]{:S(2)}, u32[]{:S(2)}) %all-to-all-start) | async-done | bytes 131104 | tf_op jit(solution)/shard_map/all_to_all | solution.py:98
  25.7 1.3 %collective-permute-done = f32[1,32768]{1,0:T(1,128)S(1)} collective-permute-done((f32[1,32768]{1,0:T(1,128)S(1)}, f32[1,32768]{1,0:T(1,128)S(1)}, u32[]{:S(2)}, u32[]{:S(2)}) %collective-permute-start) | collective-permute-done | bytes 131104 | tf_op jit(solution)/shard_map/ppermute | solution.py:104
  27.0 0.4 maximum_select_fusion
  27.4 1.7 %collective-permute-start.1 = (f32[2,32768]{1,0:T(2,128)S(1)}, f32[2,32768]{1,0:T(2,128)S(1)}, u32[]{:S(2)}, u32[]{:S(2)}) collective-permute-start(f32[2,32768]{1,0:T(2,128)S(1)} %maximum_select_fusion), channel_id=1, source_target_pairs={{0,2},{1,3},{2,4},{3,5},{4,6},{5,7},{6,0},{7,1},{8,10},{9,11},{10,... | collective-permute-start | bytes 786440 | tf_op jit(solution)/shard_map/ppermute | solution.py:108
  29.0 0.9 collective-permute-start.2
  30.0 2.4 %collective-permute-start.3 = (f32[2,32768]{1,0:T(2,128)S(1)}, f32[2,32768]{1,0:T(2,128)S(1)}, u32[]{:S(2)}, u32[]{:S(2)}) collective-permute-start(f32[2,32768]{1,0:T(2,128)S(1)} %maximum_select_fusion), channel_id=1, source_target_pairs={{0,6},{1,7},{2,0},{3,1},{4,2},{5,3},{6,4},{7,5},{8,14},{9,15},{10,... | collective-permute-start | bytes 786440 | tf_op jit(solution)/shard_map/ppermute | solution.py:108
  32.5 0.1 copy.17
  32.8 3.9 %collective-permute-done.1 = f32[2,32768]{1,0:T(2,128)S(1)} collective-permute-done((f32[2,32768]{1,0:T(2,128)S(1)}, f32[2,32768]{1,0:T(2,128)S(1)}, u32[]{:S(2)}, u32[]{:S(2)}) %collective-permute-start.1) | collective-permute-done | bytes 262176 | tf_op jit(solution)/shard_map/ppermute | solution.py:108
  36.6 3.1 %collective-permute-done.2 = f32[2,32768]{1,0:T(2,128)S(1)} collective-permute-done((f32[2,32768]{1,0:T(2,128)S(1)}, f32[2,32768]{1,0:T(2,128)S(1)}, u32[]{:S(2)}, u32[]{:S(2)}) %collective-permute-start.2) | collective-permute-done | bytes 262176 | tf_op jit(solution)/shard_map/ppermute | solution.py:108
  39.7 3.8 %collective-permute-done.3 = f32[2,32768]{1,0:T(2,128)S(1)} collective-permute-done((f32[2,32768]{1,0:T(2,128)S(1)}, f32[2,32768]{1,0:T(2,128)S(1)}, u32[]{:S(2)}, u32[]{:S(2)}) %collective-permute-start.3) | collective-permute-done | bytes 262176 | tf_op jit(solution)/shard_map/ppermute | solution.py:108
  43.6 0.5 pad_maximum_fusion.1
  44.0 0.9 gather_fusion
  44.9 0.2 gather.7
  45.1 5.0 %fusion.8 = f32[4,64,1280]{2,1,0:T(8,128)S(1)} fusion(f32[1024,1280]{1,0:T(8,128)} %constant.137.clone, f32[4,64,1024]{2,1,0:T(8,128)S(1)} %gather.7, pred[4,64]{1,0:T(4,128)(4,1)S(1)} %broadcast_in_dim.40), kind=kOutput, calls=%fused_computation.9 | convolution fusion | flops 2013528064 | bytes 7602432 | tf_op jit(solution)/shard_map/dot_general | solution.py:57
  50.2 1.1 %multiply_add_fusion.3 = (f32[4,64,640]{2,1,0:T(8,128)S(1)}, f32[4,64,640]{2,1,0:T(8,128)}, f32[4,640]{1,0:T(4,128)S(1)}) fusion(f32[4,64,1280]{2,1,0:T(8,128)S(1)} %fusion.8, f32[4,640]{1,0:T(4,128)S(1)} %get-tuple-element.27, f32[4,640]{1,0:T(4,128)S(1)} %get-tuple-element.26), kind=kLoop, calls=%fused_computation.47 | loop fusion | flops 1635840 | bytes 2652160 | tf_op jit(solution)/shard_map/add | solution.py:74
  51.2 0.1 reduce_max.9
  51.4 5.2 %multiply_add_fusion = f32[4,64,1024]{2,1,0:T(8,128)S(1)} fusion(f32[1024,1280]{1,0:T(8,128)} %constant.137.clone, f32[4,64,640]{2,1,0:T(8,128)} %get-tuple-element.17, f32[4,64,640]{2,1,0:T(8,128)S(1)} %get-tuple-element.16, f32[1280]{0:T(1024)S(1)} %copy-done.1, f32[4]{0:T(128)S(1)} %fusion.63, f32[4]{0:T(128)S(1)} %get-tuple-element.10, ...), kind=kOutput, calls=%fused_computation.12 | convolution fusion | flops 2015756288 | bytes 7607344 | tf_op jit(solution)/shard_map/dot_general | solution.py:61
  56.7 2.6 %fusion.4 = f32[4,64,1280]{2,1,0:T(8,128)S(1)} fusion(f32[4,64,1024]{2,1,0:T(8,128)S(1)} %multiply_add_fusion, f32[1024,1280]{1,0:T(8,128)S(1)} %bitcast.76), kind=kOutput, calls=%fused_computation.5 | convolution fusion | flops 2013265920 | bytes 7602176 | tf_op jit(solution)/shard_map/dot_general | solution.py:57
  59.2 0.3 subtract_reduce_fusion.1
  59.5 0.1 multiply_add_fusion.2
  59.7 2.4 %fusion.19 = f32[4,64,1024]{2,1,0:T(8,128)S(1)} fusion(f32[4,64,1024]{2,1,0:T(8,128)S(1)} %multiply_add_fusion, f32[1024,1280]{1,0:T(8,128)S(1)} %bitcast.76, f32[4,64,640]{2,1,0:T(8,128)S(1)} %get-tuple-element.15, f32[4,64,640]{2,1,0:T(8,128)S(1)} %get-tuple-element.14, f32[1280]{0:T(1024)S(1)} %copy-done.1, f32[4]{0:T(128)S(1)} %get-tuple-element.11), kind=kOutput, calls=%fused_computation.16 | convolution fusion | flops 2014445568 | bytes 8655888 | tf_op jit(solution)/shard_map/dot_general | solution.py:61
  62.1 2.8 %fusion = f32[4,64,1280]{2,1,0:T(8,128)S(1)} fusion(f32[1024,1280]{1,0:T(8,128)S(1)} %bitcast.76, f32[4,64,1024]{2,1,0:T(8,128)S(1)} %fusion.19, f32[4]{0:T(128)S(1)} %fusion.63, f32[4]{0:T(128)S(1)} %get-tuple-element.10), kind=kOutput, calls=%fused_computation.1 | convolution fusion | flops 2014052352 | bytes 7602208 | tf_op jit(solution)/shard_map/dot_general | solution.py:57
  64.9 0.3 subtract_reduce_fusion
  65.2 0.1 multiply_add_fusion.1
  65.5 0.2 reshape.337
  65.7 0.7 fusion.50
  66.5 0.2 reshape.338
  66.7 4.9 %fusion.22 = f32[260,1024]{1,0:T(8,128)S(1)} fusion(f32[1024,1280]{1,0:T(8,128)} %constant.137.clone, f32[4,640]{1,0:T(4,128)S(1)} %get-tuple-element.7, f32[4,640]{1,0:T(4,128)S(1)} %get-tuple-element.6, f32[256,1280]{1,0:T(8,128)S(1)} %reshape.338, f32[1280]{0:T(1024)S(1)} %copy-done.1), kind=kOutput, calls=%fused_computation.18 | convolution fusion | flops 2045721600 | bytes 7644160 | tf_op jit(solution)/shard_map/dot_general | solution.py:61
  71.5 0.1 slice.81
  71.9 1.8 %collective-permute-done.4 = f32[4,32,1024]{2,1,0:T(8,128)S(1)} collective-permute-done((f32[4,32,1024]{2,1,0:T(8,128)S(1)}, f32[4,32,1024]{2,1,0:T(8,128)S(1)}, u32[]{:S(2)}, u32[]{:S(2)}) %collective-permute-start.4) | collective-permute-done | bytes 524320 | tf_op jit(solution)/shard_map/ppermute | solution.py:161
  73.8 1.4 %collective-permute-start.5 = (f32[32,1024]{1,0:T(8,128)S(1)}, f32[32,1024]{1,0:T(8,128)S(1)}, u32[]{:S(2)}, u32[]{:S(2)}) collective-permute-start(f32[32,1024]{1,0:T(8,128)S(1)} %get-tuple-element.19), channel_id=1, source_target_pairs={{0,2},{1,3},{2,4},{3,5},{4,6},{5,7},{6,0},{7,1},{8,10},{9,11},{10,... | collective-permute-start | bytes 393224 | tf_op jit(solution)/shard_map/ppermute | solution.py:165
  75.2 1.6 %collective-permute-start.6 = (f32[32,1024]{1,0:T(8,128)S(1)}, f32[32,1024]{1,0:T(8,128)S(1)}, u32[]{:S(2)}, u32[]{:S(2)}) collective-permute-start(f32[32,1024]{1,0:T(8,128)S(1)} %get-tuple-element.21), channel_id=1, source_target_pairs={{0,4},{1,5},{2,6},{3,7},{4,0},{5,1},{6,2},{7,3},{8,12},{9,13},{10,... | collective-permute-start | bytes 393224 | tf_op jit(solution)/shard_map/ppermute | solution.py:165
  76.8 1.5 %collective-permute-start.7 = (f32[32,1024]{1,0:T(8,128)S(1)}, f32[32,1024]{1,0:T(8,128)S(1)}, u32[]{:S(2)}, u32[]{:S(2)}) collective-permute-start(f32[32,1024]{1,0:T(8,128)S(1)} %get-tuple-element.20), channel_id=1, source_target_pairs={{0,6},{1,7},{2,0},{3,1},{4,2},{5,3},{6,4},{7,5},{8,14},{9,15},{10,... | collective-permute-start | bytes 393224 | tf_op jit(solution)/shard_map/ppermute | solution.py:165
  78.3 1.8 %collective-permute-done.5 = f32[32,1024]{1,0:T(8,128)S(1)} collective-permute-done((f32[32,1024]{1,0:T(8,128)S(1)}, f32[32,1024]{1,0:T(8,128)S(1)}, u32[]{:S(2)}, u32[]{:S(2)}) %collective-permute-start.5) | collective-permute-done | bytes 131104 | tf_op jit(solution)/shard_map/ppermute | solution.py:165
  80.2 2.9 %collective-permute-done.6 = f32[32,1024]{1,0:T(8,128)S(1)} collective-permute-done((f32[32,1024]{1,0:T(8,128)S(1)}, f32[32,1024]{1,0:T(8,128)S(1)}, u32[]{:S(2)}, u32[]{:S(2)}) %collective-permute-start.6) | collective-permute-done | bytes 131104 | tf_op jit(solution)/shard_map/ppermute | solution.py:165
  83.1 1.5 %collective-permute-done.7 = f32[32,1024]{1,0:T(8,128)S(1)} collective-permute-done((f32[32,1024]{1,0:T(8,128)S(1)}, f32[32,1024]{1,0:T(8,128)S(1)}, u32[]{:S(2)}, u32[]{:S(2)}) %collective-permute-start.7) | collective-permute-done | bytes 131104 | tf_op jit(solution)/shard_map/ppermute | solution.py:165
  84.6 0.7 reshape.339
  85.3 3.8 %all-to-all-start.1 = ((f32[32,1,1024]{2,1,0:T(1,128)}), f32[32,1,1024]{2,1,0:T(1,128)S(1)}, u32[]{:S(2)}, u32[]{:S(2)}) async-start(f32[32,1,1024]{2,1,0:T(1,128)} %reshape.339), calls=%async_computation.1 | async-start | bytes 262144 | tf_op jit(solution)/shard_map/all_to_all | solution.py:167
  89.2 0.6 slice.80
  89.8 9.9 %all-to-all-done.1 = f32[32,1,1024]{2,1,0:T(1,128)S(1)} async-done(((f32[32,1,1024]{2,1,0:T(1,128)}), f32[32,1,1024]{2,1,0:T(1,128)S(1)}, u32[]{:S(2)}, u32[]{:S(2)}) %all-to-all-start.1) | async-done | bytes 131104 | tf_op jit(solution)/shard_map/all_to_all | solution.py:167
  99.8 0.6 multiply_reduce_fusion
  101.2 0.6 fusion.49
  102.5 0.6 subtract_divide_fusion
  (38 shorter events, 1.1 us)
Async XLA Ops:
  0.6 14.8 %copy-start = (f32[4,1024]{1,0:T(4,128)S(1)}, f32[4,1024]{1,0:T(4,128)}, u32[]{:S(2)}) copy-start(f32[4,1024]{1,0:T(4,128)} %param.5) | copy-start | bytes 49156
  4.1 21.6 %all-to-all-start = ((f32[32,1,1024]{2,1,0:T(1,128)}), f32[32,1,1024]{2,1,0:T(1,128)S(1)}, u32[]{:S(2)}, u32[]{:S(2)}) async-start(f32[32,1,1024]{2,1,0:T(1,128)} %broadcast_in_dim.43), calls=%async_computation | async-start | bytes 262144 | tf_op jit(solution)/shard_map/all_to_all | solution.py:98
  15.4 3.7 %copy-start.3 = (s32[4,2]{0,1:T(2,128)S(1)}, s32[4,2]{0,1:T(2,128)}, u32[]{:S(2)}) copy-start(s32[4,2]{0,1:T(2,128)} %param.6) | copy-start | bytes 100
  25.7 1.3 %collective-permute-start = (f32[1,32768]{1,0:T(1,128)S(1)}, f32[1,32768]{1,0:T(1,128)S(1)}, u32[]{:S(2)}, u32[]{:S(2)}) collective-permute-start(f32[1,32768]{1,0:T(1,128)S(1)} %bitcast.79), channel_id=1, source_target_pairs={{0,1},{1,0},{2,3},{3,2},{4,5},{5,4},{6,7},{7,6},{8,9},{9,8},{10,11... | collective-permute-start | bytes 393224 | tf_op jit(solution)/shard_map/ppermute | solution.py:104
  27.4 9.3 %collective-permute-start.1 = (f32[2,32768]{1,0:T(2,128)S(1)}, f32[2,32768]{1,0:T(2,128)S(1)}, u32[]{:S(2)}, u32[]{:S(2)}) collective-permute-start(f32[2,32768]{1,0:T(2,128)S(1)} %maximum_select_fusion), channel_id=1, source_target_pairs={{0,2},{1,3},{2,4},{3,5},{4,6},{5,7},{6,0},{7,1},{8,10},{9,11},{10,... | collective-permute-start | bytes 786440 | tf_op jit(solution)/shard_map/ppermute | solution.py:108
  29.0 10.7 %collective-permute-start.2 = (f32[2,32768]{1,0:T(2,128)S(1)}, f32[2,32768]{1,0:T(2,128)S(1)}, u32[]{:S(2)}, u32[]{:S(2)}) collective-permute-start(f32[2,32768]{1,0:T(2,128)S(1)} %maximum_select_fusion), channel_id=1, source_target_pairs={{0,4},{1,5},{2,6},{3,7},{4,0},{5,1},{6,2},{7,3},{8,12},{9,13},{10,... | collective-permute-start | bytes 786440 | tf_op jit(solution)/shard_map/ppermute | solution.py:108
  30.0 13.6 %collective-permute-start.3 = (f32[2,32768]{1,0:T(2,128)S(1)}, f32[2,32768]{1,0:T(2,128)S(1)}, u32[]{:S(2)}, u32[]{:S(2)}) collective-permute-start(f32[2,32768]{1,0:T(2,128)S(1)} %maximum_select_fusion), channel_id=1, source_target_pairs={{0,6},{1,7},{2,0},{3,1},{4,2},{5,3},{6,4},{7,5},{8,14},{9,15},{10,... | collective-permute-start | bytes 786440 | tf_op jit(solution)/shard_map/ppermute | solution.py:108
  50.1 1.2 %copy-start.1 = (f32[1280]{0:T(1024)S(1)}, f32[1280]{0:T(1024)}, u32[]{:S(2)}) copy-start(f32[1280]{0:T(1024)} %constant.138.clone) | copy-start | bytes 15364
  50.1 6.5 %slice-start = ((s8[5242880]{0:T(1024)(128)(4,1)}), s8[1048576]{0:T(1024)(128)(4,1)S(1)}, s32[]{:S(2)}) async-start(s8[5242880]{0:T(1024)(128)(4,1)} %bitcast.75), calls=%async_computation.2 | async-start | bytes 2097152
  51.4 5.3 %slice-start.1 = ((s8[5242880]{0:T(1024)(128)(4,1)}), s8[4194304]{0:T(1024)(128)(4,1)S(1)}, s32[]{:S(2)}) async-start(s8[5242880]{0:T(1024)(128)(4,1)} %bitcast.75), calls=%async_computation.3 | async-start | bytes 8388608
  71.7 2.0 %collective-permute-start.4 = (f32[4,32,1024]{2,1,0:T(8,128)S(1)}, f32[4,32,1024]{2,1,0:T(8,128)S(1)}, u32[]{:S(2)}, u32[]{:S(2)}) collective-permute-start(f32[4,32,1024]{2,1,0:T(8,128)S(1)} %dynamic-slice_bitcast_fusion), channel_id=1, source_target_pairs={{0,1},{1,0},{2,3},{3,2},{4,5},{5,4},{6,7},{7,6},{8,9},{9,8},{10,11... | collective-permute-start | bytes 1572872 | tf_op jit(solution)/shard_map/ppermute | solution.py:161
  73.8 27.4 %copy-start.2 = (f32[1,1,1024]{2,1,0:T(1,128)S(1)}, f32[1,1,1024]{2,1,0:T(1,128)}, u32[]{:S(2)}) copy-start(f32[1,1,1024]{2,1,0:T(1,128)} %param.7) | copy-start | bytes 12292
  73.8 6.3 %collective-permute-start.5 = (f32[32,1024]{1,0:T(8,128)S(1)}, f32[32,1024]{1,0:T(8,128)S(1)}, u32[]{:S(2)}, u32[]{:S(2)}) collective-permute-start(f32[32,1024]{1,0:T(8,128)S(1)} %get-tuple-element.19), channel_id=1, source_target_pairs={{0,2},{1,3},{2,4},{3,5},{4,6},{5,7},{6,0},{7,1},{8,10},{9,11},{10,... | collective-permute-start | bytes 393224 | tf_op jit(solution)/shard_map/ppermute | solution.py:165
  75.2 7.9 %collective-permute-start.6 = (f32[32,1024]{1,0:T(8,128)S(1)}, f32[32,1024]{1,0:T(8,128)S(1)}, u32[]{:S(2)}, u32[]{:S(2)}) collective-permute-start(f32[32,1024]{1,0:T(8,128)S(1)} %get-tuple-element.21), channel_id=1, source_target_pairs={{0,4},{1,5},{2,6},{3,7},{4,0},{5,1},{6,2},{7,3},{8,12},{9,13},{10,... | collective-permute-start | bytes 393224 | tf_op jit(solution)/shard_map/ppermute | solution.py:165
  76.8 7.8 %collective-permute-start.7 = (f32[32,1024]{1,0:T(8,128)S(1)}, f32[32,1024]{1,0:T(8,128)S(1)}, u32[]{:S(2)}, u32[]{:S(2)}) collective-permute-start(f32[32,1024]{1,0:T(8,128)S(1)} %get-tuple-element.20), channel_id=1, source_target_pairs={{0,6},{1,7},{2,0},{3,1},{4,2},{5,3},{6,4},{7,5},{8,14},{9,15},{10,... | collective-permute-start | bytes 393224 | tf_op jit(solution)/shard_map/ppermute | solution.py:165
  85.3 14.4 %all-to-all-start.1 = ((f32[32,1,1024]{2,1,0:T(1,128)}), f32[32,1,1024]{2,1,0:T(1,128)S(1)}, u32[]{:S(2)}, u32[]{:S(2)}) async-start(f32[32,1,1024]{2,1,0:T(1,128)} %reshape.339), calls=%async_computation.1 | async-start | bytes 262144 | tf_op jit(solution)/shard_map/all_to_all | solution.py:167

commit v4 on v3

--- a/solution.py
+++ b/solution.py
@@ -94,25 +94,26 @@
     table, weight = lax.optimization_barrier((table, weight))
     width = table.shape[1]
 
-    own = unit_rows(dictionary.reshape(1, pixels))
-    step = lax.all_to_all(jnp.broadcast_to(own[None], (tile_count, 1, pixels)), "tile", 0, 0, tiled=True)
-    mine = step.reshape(1, tile_count * pixels)
+    raw = dictionary.reshape(1, pixels)
+    step = lax.all_to_all(jnp.broadcast_to(raw[None], (tile_count, 1, pixels)), "tile", 0, 0, tiled=True)
+    mine = step.reshape(tile_count, pixels)
+    own = unit_rows(raw)
     place = lax.axis_index("atom")
     core = place % 2
     chips = atom_count // 2
     chip = place // 2
     other = lax.ppermute(mine, "atom", [(i, i ^ 1) for i in range(atom_count)])
-    pair = jnp.where(core == 0, jnp.concatenate([mine, other]), jnp.concatenate([other, mine]))
+    pair = jnp.concatenate([mine, other])
     pieces = [pair]
     for hop in range(1, chips):
         pieces.append(lax.ppermute(pair, "atom", [(i, ((i // 2 + hop) % chips) * 2 + i % 2) for i in range(atom_count)]))
-    every = jnp.concatenate(pieces, axis=0)
+    every = jnp.concatenate(pieces, axis=0).reshape(atom_count, tile_count * pixels)
 
     image_spec = forward(images.reshape(1, tiles_here, pixels), table).reshape(tiles_here, width)
     slot_count = tiles_here * ACT
     flat_ids = active.reshape(slot_count)
-    where_held = ((chip - flat_ids // 2) % chips) * 2 + flat_ids % 2
-    chosen_atoms = jnp.take(every, where_held, axis=0).reshape(slot_count * BLK, pixels)
+    where_held = ((chip - flat_ids // 2) % chips) * 2 + (flat_ids % 2 != core).astype(jnp.int32)
+    chosen_atoms = unit_rows(jnp.take(every, where_held, axis=0).reshape(slot_count * BLK, pixels))
     rows = ACT * BLK
     chosen = forward(chosen_atoms, table).reshape(tiles_here, rows, width)
     chosen_real, chosen_imag = parts(chosen)

time: 103 us -> 102 us (level)
  waiting for transfers between devices: 36.4 us -> 33.9 us
  local copies, waits for them, and re-layouts: 4.37 us -> 6.44 us
  other arithmetic: 7.1 us -> 5.14 us
    all_to_all x1, waiting for transfers between devices: 9.93 us -> 8.35 us  [on_device(): lax.all_to_all(arrived, 'tile', 0, 0, tiled=True)]
  transfers between devices with their start and end apart: 10 -> 10, of which waited for: 10 -> 10; matrix products, arithmetic and copies ran while one was open for 5% -> 6% of each run, Pallas kernels for 0% -> 0%
where the time goes in v4:
time: 102 us; the launch traced here: 101 us
  waiting for transfers between devices  33.9 us (33%)
  matrix products  27.3 us (27%)
  starting transfers between devices  25.2 us (25%)
  local copies, waits for them, and re-layouts  6.44 us (6%)
  other arithmetic  5.14 us (5%)
  between operations  3.2 us (3%)
    dot_general x4, matrix products, forward(): jnp.dot(values, table, precision=fast, preferred_element_type=jnp.float32)  14.1 us
    dot_general x3, matrix products, inverse(): lax.dot_general(spectra * weight, table, (((spectra.ndim - 1,), (1,)), ((...  12.5 us
    all_to_all x1, starting transfers between devices, on_device(): lax.all_to_all(jnp.broadcast_to(raw[None], (tile_count, 1, pixels)), 'til...  11.3 us
    ppermute x3, waiting for transfers between devices, on_device(): lax.ppermute(pair, 'atom', [(i, (i // 2 + hop) % chips * 2 + i % 2) for i...  11.1 us
    all_to_all x1, waiting for transfers between devices, on_device(): lax.all_to_all(arrived, 'tile', 0, 0, tiled=True)  8.35 us
    ppermute x3, waiting for transfers between devices, on_device(): lax.ppermute(sent, 'atom', [(i, (i // 2 + hop) % chips * 2 + i % 2) for i...  6.26 us
    all_to_all x1, waiting for transfers between devices, on_device(): lax.all_to_all(jnp.broadcast_to(raw[None], (tile_count, 1, pixels)), 'til...  5.53 us
    ppermute x3, starting transfers between devices, on_device(): lax.ppermute(pair, 'atom', [(i, (i // 2 + hop) % chips * 2 + i % 2) for i...  5.26 us
  transfers between devices with their start and end apart: 10, of which 10 were waited for; matrix products, arithmetic and copies ran while one was open for 6% of the time, Pallas kernels for 0%

profile of v4, /device:TPU:8, one launch (start us, length us, event | category | flops | bytes accessed | tf_op | source)
XLA Modules:
  0.0 101.3 jit_solution(12028240395463235750)
XLA Ops:
  0.6 1.4 %broadcast_in_dim.51 = f32[32,1,1024]{2,1,0:T(1,128)} broadcast(f32[1024]{0:T(1024)} %bitcast.85), dimensions={2} | broadcast | bytes 135168 | tf_op jit(solution)/shard_map/broadcast_in_dim | solution.py:98
  2.0 11.3 %all-to-all-start = ((f32[32,1,1024]{2,1,0:T(1,128)}), f32[32,1,1024]{2,1,0:T(1,128)S(1)}, u32[]{:S(2)}, u32[]{:S(2)}) async-start(f32[32,1,1024]{2,1,0:T(1,128)} %broadcast_in_dim.51), calls=%async_computation | async-start | bytes 262144 | tf_op jit(solution)/shard_map/all_to_all | solution.py:98
  13.4 0.8 copy.16
  14.2 3.7 %convolution_bitcast_fusion = f32[4,1280]{1,0:T(4,128)S(1)} fusion(f32[1024,1280]{1,0:T(8,128)} %constant.139.clone, f32[4,1024]{1,0:T(4,128)S(1)} %copy-done), kind=kOutput, calls=%fused_computation.11 | convolution fusion | flops 31457280 | bytes 5279744 | tf_op jit(solution)/shard_map/dot_general | solution.py:57
  18.1 5.5 %all-to-all-done = f32[32,1,1024]{2,1,0:T(1,128)S(1)} async-done(((f32[32,1,1024]{2,1,0:T(1,128)}), f32[32,1,1024]{2,1,0:T(1,128)S(1)}, u32[]{:S(2)}, u32[]{:S(2)}) %all-to-all-start) | async-done | bytes 131104 | tf_op jit(solution)/shard_map/all_to_all | solution.py:98
  24.0 0.1 copy.17
  24.2 0.9 collective-permute-done
  25.1 1.7 %collective-permute-start.1 = (f32[64,1024]{1,0:T(8,128)S(1)}, f32[64,1024]{1,0:T(8,128)S(1)}, u32[]{:S(2)}, u32[]{:S(2)}) collective-permute-start(f32[64,1024]{1,0:T(8,128)S(1)} %pad_maximum_fusion.1), channel_id=1, source_target_pairs={{0,2},{1,3},{2,4},{3,5},{4,6},{5,7},{6,0},{7,1},{8,10},{9,11},{10,... | collective-permute-start | bytes 786440 | tf_op jit(solution)/shard_map/ppermute | solution.py:109
  26.8 0.9 collective-permute-start.2
  27.7 2.7 %collective-permute-start.3 = (f32[64,1024]{1,0:T(8,128)S(1)}, f32[64,1024]{1,0:T(8,128)S(1)}, u32[]{:S(2)}, u32[]{:S(2)}) collective-permute-start(f32[64,1024]{1,0:T(8,128)S(1)} %pad_maximum_fusion.1), channel_id=1, source_target_pairs={{0,6},{1,7},{2,0},{3,1},{4,2},{5,3},{6,4},{7,5},{8,14},{9,15},{10,... | collective-permute-start | bytes 786440 | tf_op jit(solution)/shard_map/ppermute | solution.py:109
  30.4 3.9 %collective-permute-done.1 = f32[64,1024]{1,0:T(8,128)S(1)} collective-permute-done((f32[64,1024]{1,0:T(8,128)S(1)}, f32[64,1024]{1,0:T(8,128)S(1)}, u32[]{:S(2)}, u32[]{:S(2)}) %collective-permute-start.1) | collective-permute-done | bytes 262176 | tf_op jit(solution)/shard_map/ppermute | solution.py:109
  34.4 3.1 %collective-permute-done.2 = f32[64,1024]{1,0:T(8,128)S(1)} collective-permute-done((f32[64,1024]{1,0:T(8,128)S(1)}, f32[64,1024]{1,0:T(8,128)S(1)}, u32[]{:S(2)}, u32[]{:S(2)}) %collective-permute-start.2) | collective-permute-done | bytes 262176 | tf_op jit(solution)/shard_map/ppermute | solution.py:109
  37.5 4.1 %collective-permute-done.3 = f32[64,1024]{1,0:T(8,128)S(1)} collective-permute-done((f32[64,1024]{1,0:T(8,128)S(1)}, f32[64,1024]{1,0:T(8,128)S(1)}, u32[]{:S(2)}, u32[]{:S(2)}) %collective-permute-start.3) | collective-permute-done | bytes 262176 | tf_op jit(solution)/shard_map/ppermute | solution.py:109
  41.6 0.2 reshape.363
  41.8 0.9 gather_fusion
  42.7 0.2 gather.10
  42.9 0.2 gather.9
  43.1 0.3 multiply_reduce_fusion
  43.4 5.0 %fusion.8 = f32[4,64,1280]{2,1,0:T(8,128)S(1)} fusion(f32[1024,1280]{1,0:T(8,128)} %constant.139.clone, f32[4,64,1024]{2,1,0:T(8,128)S(1)} %gather.9, f32[4,64]{1,0:T(4,128)S(1)} %sqrt.24, pred[4,64]{1,0:T(4,128)(4,1)S(1)} %broadcast_in_dim.48), kind=kOutput, calls=%fused_computation.9 | convolution fusion | flops 2013790208 | bytes 7603456 | tf_op jit(solution)/shard_map/dot_general | solution.py:57
  48.5 1.1 %multiply_add_fusion.3 = (f32[4,64,640]{2,1,0:T(8,128)S(1)}, f32[4,64,640]{2,1,0:T(8,128)}, f32[4,640]{1,0:T(4,128)S(1)}) fusion(f32[4,64,1280]{2,1,0:T(8,128)S(1)} %fusion.8, f32[4,640]{1,0:T(4,128)S(1)} %get-tuple-element.29, f32[4,640]{1,0:T(4,128)S(1)} %get-tuple-element.28), kind=kLoop, calls=%fused_computation.48 | loop fusion | flops 1635840 | bytes 2652160 | tf_op jit(solution)/shard_map/add | solution.py:74
  49.6 0.1 reduce_max.9
  49.7 5.2 %multiply_add_fusion = f32[4,64,1024]{2,1,0:T(8,128)S(1)} fusion(f32[1024,1280]{1,0:T(8,128)} %constant.139.clone, f32[4,64,640]{2,1,0:T(8,128)} %get-tuple-element.19, f32[4,64,640]{2,1,0:T(8,128)S(1)} %get-tuple-element.18, f32[1280]{0:T(1024)S(1)} %copy-done.1, f32[4]{0:T(128)S(1)} %fusion.68, f32[4]{0:T(128)S(1)} %get-tuple-element.12, ...), kind=kOutput, calls=%fused_computation.12 | convolution fusion | flops 2015756288 | bytes 7607344 | tf_op jit(solution)/shard_map/dot_general | solution.py:61
  55.0 2.6 %fusion.4 = f32[4,64,1280]{2,1,0:T(8,128)S(1)} fusion(f32[4,64,1024]{2,1,0:T(8,128)S(1)} %multiply_add_fusion, f32[1024,1280]{1,0:T(8,128)S(1)} %bitcast.80), kind=kOutput, calls=%fused_computation.5 | convolution fusion | flops 2013265920 | bytes 7602176 | tf_op jit(solution)/shard_map/dot_general | solution.py:57
  57.6 0.3 subtract_reduce_fusion.1
  57.9 0.1 multiply_add_fusion.2
  58.0 2.4 %fusion.19 = f32[4,64,1024]{2,1,0:T(8,128)S(1)} fusion(f32[4,64,1024]{2,1,0:T(8,128)S(1)} %multiply_add_fusion, f32[1024,1280]{1,0:T(8,128)S(1)} %bitcast.80, f32[4,64,640]{2,1,0:T(8,128)S(1)} %get-tuple-element.17, f32[4,64,640]{2,1,0:T(8,128)S(1)} %get-tuple-element.16, f32[1280]{0:T(1024)S(1)} %copy-done.1, f32[4]{0:T(128)S(1)} %get-tuple-element.13), kind=kOutput, calls=%fused_computation.16 | convolution fusion | flops 2014445568 | bytes 8655888 | tf_op jit(solution)/shard_map/dot_general | solution.py:61
  60.4 2.9 %fusion = f32[4,64,1280]{2,1,0:T(8,128)S(1)} fusion(f32[1024,1280]{1,0:T(8,128)S(1)} %bitcast.80, f32[4,64,1024]{2,1,0:T(8,128)S(1)} %fusion.19, f32[4]{0:T(128)S(1)} %fusion.68, f32[4]{0:T(128)S(1)} %get-tuple-element.12), kind=kOutput, calls=%fused_computation.1 | convolution fusion | flops 2014052352 | bytes 7602208 | tf_op jit(solution)/shard_map/dot_general | solution.py:57
  63.3 0.3 subtract_reduce_fusion
  63.6 0.1 multiply_add_fusion.1
  63.8 0.2 reshape.365
  64.1 0.7 fusion.52
  64.8 0.2 reshape.366
  65.0 4.9 %fusion.22 = f32[260,1024]{1,0:T(8,128)S(1)} fusion(f32[1024,1280]{1,0:T(8,128)} %constant.139.clone, f32[4,640]{1,0:T(4,128)S(1)} %get-tuple-element.7, f32[4,640]{1,0:T(4,128)S(1)} %get-tuple-element.6, f32[256,1280]{1,0:T(8,128)S(1)} %reshape.366, f32[1280]{0:T(1024)S(1)} %copy-done.1), kind=kOutput, calls=%fused_computation.18 | convolution fusion | flops 2045721600 | bytes 7644160 | tf_op jit(solution)/shard_map/dot_general | solution.py:61
  70.2 1.8 %collective-permute-done.4 = f32[4,32,1024]{2,1,0:T(8,128)S(1)} collective-permute-done((f32[4,32,1024]{2,1,0:T(8,128)S(1)}, f32[4,32,1024]{2,1,0:T(8,128)S(1)}, u32[]{:S(2)}, u32[]{:S(2)}) %collective-permute-start.4) | collective-permute-done | bytes 524320 | tf_op jit(solution)/shard_map/ppermute | solution.py:162
  72.2 1.1 %collective-permute-start.5 = (f32[32,1024]{1,0:T(8,128)S(1)}, f32[32,1024]{1,0:T(8,128)S(1)}, u32[]{:S(2)}, u32[]{:S(2)}) collective-permute-start(f32[32,1024]{1,0:T(8,128)S(1)} %get-tuple-element.21), channel_id=1, source_target_pairs={{0,2},{1,3},{2,4},{3,5},{4,6},{5,7},{6,0},{7,1},{8,10},{9,11},{10,... | collective-permute-start | bytes 393224 | tf_op jit(solution)/shard_map/ppermute | solution.py:166
  73.3 1.6 %collective-permute-start.6 = (f32[32,1024]{1,0:T(8,128)S(1)}, f32[32,1024]{1,0:T(8,128)S(1)}, u32[]{:S(2)}, u32[]{:S(2)}) collective-permute-start(f32[32,1024]{1,0:T(8,128)S(1)} %get-tuple-element.23), channel_id=1, source_target_pairs={{0,4},{1,5},{2,6},{3,7},{4,0},{5,1},{6,2},{7,3},{8,12},{9,13},{10,... | collective-permute-start | bytes 393224 | tf_op jit(solution)/shard_map/ppermute | solution.py:166
  74.9 1.5 %collective-permute-start.7 = (f32[32,1024]{1,0:T(8,128)S(1)}, f32[32,1024]{1,0:T(8,128)S(1)}, u32[]{:S(2)}, u32[]{:S(2)}) collective-permute-start(f32[32,1024]{1,0:T(8,128)S(1)} %get-tuple-element.22), channel_id=1, source_target_pairs={{0,6},{1,7},{2,0},{3,1},{4,2},{5,3},{6,4},{7,5},{8,14},{9,15},{10,... | collective-permute-start | bytes 393224 | tf_op jit(solution)/shard_map/ppermute | solution.py:166
  76.4 2.2 %collective-permute-done.5 = f32[32,1024]{1,0:T(8,128)S(1)} collective-permute-done((f32[32,1024]{1,0:T(8,128)S(1)}, f32[32,1024]{1,0:T(8,128)S(1)}, u32[]{:S(2)}, u32[]{:S(2)}) %collective-permute-start.5) | collective-permute-done | bytes 131104 | tf_op jit(solution)/shard_map/ppermute | solution.py:166
  78.6 2.5 %collective-permute-done.6 = f32[32,1024]{1,0:T(8,128)S(1)} collective-permute-done((f32[32,1024]{1,0:T(8,128)S(1)}, f32[32,1024]{1,0:T(8,128)S(1)}, u32[]{:S(2)}, u32[]{:S(2)}) %collective-permute-start.6) | collective-permute-done | bytes 131104 | tf_op jit(solution)/shard_map/ppermute | solution.py:166
  81.1 1.5 %collective-permute-done.7 = f32[32,1024]{1,0:T(8,128)S(1)} collective-permute-done((f32[32,1024]{1,0:T(8,128)S(1)}, f32[32,1024]{1,0:T(8,128)S(1)}, u32[]{:S(2)}, u32[]{:S(2)}) %collective-permute-start.7) | collective-permute-done | bytes 131104 | tf_op jit(solution)/shard_map/ppermute | solution.py:166
  82.7 0.7 reshape.367
  83.4 4.3 %all-to-all-start.1 = ((f32[32,1,1024]{2,1,0:T(1,128)}), f32[32,1,1024]{2,1,0:T(1,128)S(1)}, u32[]{:S(2)}, u32[]{:S(2)}) async-start(f32[32,1,1024]{2,1,0:T(1,128)} %reshape.367), calls=%async_computation.1 | async-start | bytes 262144 | tf_op jit(solution)/shard_map/all_to_all | solution.py:168
  87.7 0.6 multiply_reduce_fusion.2
  89.0 0.6 slice.80
  89.6 8.3 %all-to-all-done.1 = f32[32,1,1024]{2,1,0:T(1,128)S(1)} async-done(((f32[32,1,1024]{2,1,0:T(1,128)}), f32[32,1,1024]{2,1,0:T(1,128)S(1)}, u32[]{:S(2)}, u32[]{:S(2)}) %all-to-all-start.1) | async-done | bytes 131104 | tf_op jit(solution)/shard_map/all_to_all | solution.py:168
  98.1 0.6 multiply_reduce_fusion.1
  99.4 0.6 fusion.51
  100.7 0.6 subtract_divide_fusion
  (50 shorter events, 1.6 us)
Async XLA Ops:
  0.6 13.6 %copy-start = (f32[4,1024]{1,0:T(4,128)S(1)}, f32[4,1024]{1,0:T(4,128)}, u32[]{:S(2)}) copy-start(f32[4,1024]{1,0:T(4,128)} %param.5) | copy-start | bytes 49156
  2.0 21.6 %all-to-all-start = ((f32[32,1,1024]{2,1,0:T(1,128)}), f32[32,1,1024]{2,1,0:T(1,128)S(1)}, u32[]{:S(2)}, u32[]{:S(2)}) async-start(f32[32,1,1024]{2,1,0:T(1,128)} %broadcast_in_dim.51), calls=%async_computation | async-start | bytes 262144 | tf_op jit(solution)/shard_map/all_to_all | solution.py:98
  14.2 3.7 %copy-start.3 = (s32[4,2]{0,1:T(2,128)S(1)}, s32[4,2]{0,1:T(2,128)}, u32[]{:S(2)}) copy-start(s32[4,2]{0,1:T(2,128)} %param.6) | copy-start | bytes 100
  23.7 1.4 %collective-permute-start = (f32[32,1024]{1,0:T(8,128)S(1)}, f32[32,1024]{1,0:T(8,128)S(1)}, u32[]{:S(2)}, u32[]{:S(2)}) collective-permute-start(f32[32,1024]{1,0:T(8,128)S(1)} %bitcast.83), channel_id=1, source_target_pairs={{0,1},{1,0},{2,3},{3,2},{4,5},{5,4},{6,7},{7,6},{8,9},{9,8},{10,11... | collective-permute-start | bytes 393224 | tf_op jit(solution)/shard_map/ppermute | solution.py:105
  25.1 9.3 %collective-permute-start.1 = (f32[64,1024]{1,0:T(8,128)S(1)}, f32[64,1024]{1,0:T(8,128)S(1)}, u32[]{:S(2)}, u32[]{:S(2)}) collective-permute-start(f32[64,1024]{1,0:T(8,128)S(1)} %pad_maximum_fusion.1), channel_id=1, source_target_pairs={{0,2},{1,3},{2,4},{3,5},{4,6},{5,7},{6,0},{7,1},{8,10},{9,11},{10,... | collective-permute-start | bytes 786440 | tf_op jit(solution)/shard_map/ppermute | solution.py:109
  26.8 10.7 %collective-permute-start.2 = (f32[64,1024]{1,0:T(8,128)S(1)}, f32[64,1024]{1,0:T(8,128)S(1)}, u32[]{:S(2)}, u32[]{:S(2)}) collective-permute-start(f32[64,1024]{1,0:T(8,128)S(1)} %pad_maximum_fusion.1), channel_id=1, source_target_pairs={{0,4},{1,5},{2,6},{3,7},{4,0},{5,1},{6,2},{7,3},{8,12},{9,13},{10,... | collective-permute-start | bytes 786440 | tf_op jit(solution)/shard_map/ppermute | solution.py:109
  27.7 13.8 %collective-permute-start.3 = (f32[64,1024]{1,0:T(8,128)S(1)}, f32[64,1024]{1,0:T(8,128)S(1)}, u32[]{:S(2)}, u32[]{:S(2)}) collective-permute-start(f32[64,1024]{1,0:T(8,128)S(1)} %pad_maximum_fusion.1), channel_id=1, source_target_pairs={{0,6},{1,7},{2,0},{3,1},{4,2},{5,3},{6,4},{7,5},{8,14},{9,15},{10,... | collective-permute-start | bytes 786440 | tf_op jit(solution)/shard_map/ppermute | solution.py:109
  48.5 1.2 %copy-start.1 = (f32[1280]{0:T(1024)S(1)}, f32[1280]{0:T(1024)}, u32[]{:S(2)}) copy-start(f32[1280]{0:T(1024)} %constant.140.clone) | copy-start | bytes 15364
  48.5 6.5 %slice-start = ((s8[5242880]{0:T(1024)(128)(4,1)}), s8[1048576]{0:T(1024)(128)(4,1)S(1)}, s32[]{:S(2)}) async-start(s8[5242880]{0:T(1024)(128)(4,1)} %bitcast.79), calls=%async_computation.2 | async-start | bytes 2097152
  49.7 5.3 %slice-start.1 = ((s8[5242880]{0:T(1024)(128)(4,1)}), s8[4194304]{0:T(1024)(128)(4,1)S(1)}, s32[]{:S(2)}) async-start(s8[5242880]{0:T(1024)(128)(4,1)} %bitcast.79), calls=%async_computation.3 | async-start | bytes 8388608
  70.0 2.0 %collective-permute-start.4 = (f32[4,32,1024]{2,1,0:T(8,128)S(1)}, f32[4,32,1024]{2,1,0:T(8,128)S(1)}, u32[]{:S(2)}, u32[]{:S(2)}) collective-permute-start(f32[4,32,1024]{2,1,0:T(8,128)S(1)} %dynamic-slice_bitcast_fusion), channel_id=1, source_target_pairs={{0,1},{1,0},{2,3},{3,2},{4,5},{5,4},{6,7},{7,6},{8,9},{9,8},{10,11... | collective-permute-start | bytes 1572872 | tf_op jit(solution)/shard_map/ppermute | solution.py:162
  72.1 15.6 %copy-start.2 = (f32[1,1,1024]{2,1,0:T(1,128)S(1)}, f32[1,1,1024]{2,1,0:T(1,128)}, u32[]{:S(2)}) copy-start(f32[1,1,1024]{2,1,0:T(1,128)} %param.7) | copy-start | bytes 12292
  72.2 6.4 %collective-permute-start.5 = (f32[32,1024]{1,0:T(8,128)S(1)}, f32[32,1024]{1,0:T(8,128)S(1)}, u32[]{:S(2)}, u32[]{:S(2)}) collective-permute-start(f32[32,1024]{1,0:T(8,128)S(1)} %get-tuple-element.21), channel_id=1, source_target_pairs={{0,2},{1,3},{2,4},{3,5},{4,6},{5,7},{6,0},{7,1},{8,10},{9,11},{10,... | collective-permute-start | bytes 393224 | tf_op jit(solution)/shard_map/ppermute | solution.py:166
  73.3 7.9 %collective-permute-start.6 = (f32[32,1024]{1,0:T(8,128)S(1)}, f32[32,1024]{1,0:T(8,128)S(1)}, u32[]{:S(2)}, u32[]{:S(2)}) collective-permute-start(f32[32,1024]{1,0:T(8,128)S(1)} %get-tuple-element.23), channel_id=1, source_target_pairs={{0,4},{1,5},{2,6},{3,7},{4,0},{5,1},{6,2},{7,3},{8,12},{9,13},{10,... | collective-permute-start | bytes 393224 | tf_op jit(solution)/shard_map/ppermute | solution.py:166
  74.9 7.8 %collective-permute-start.7 = (f32[32,1024]{1,0:T(8,128)S(1)}, f32[32,1024]{1,0:T(8,128)S(1)}, u32[]{:S(2)}, u32[]{:S(2)}) collective-permute-start(f32[32,1024]{1,0:T(8,128)S(1)} %get-tuple-element.22), channel_id=1, source_target_pairs={{0,6},{1,7},{2,0},{3,1},{4,2},{5,3},{6,4},{7,5},{8,14},{9,15},{10,... | collective-permute-start | bytes 393224 | tf_op jit(solution)/shard_map/ppermute | solution.py:166
  83.4 14.5 %all-to-all-start.1 = ((f32[32,1,1024]{2,1,0:T(1,128)}), f32[32,1,1024]{2,1,0:T(1,128)S(1)}, u32[]{:S(2)}, u32[]{:S(2)}) async-start(f32[32,1,1024]{2,1,0:T(1,128)} %reshape.367), calls=%async_computation.1 | async-start | bytes 262144 | tf_op jit(solution)/shard_map/all_to_all | solution.py:168

commit v5 on v4

--- a/solution.py
+++ b/solution.py
@@ -16,7 +16,6 @@
 step_ratio = 0.5
 epsilon = 1e-06
 highest = lax.Precision.HIGHEST
-fast = lax.Precision.HIGH
 
 HALF = SIDE // 2 + 1
 USED = SIDE * HALF
@@ -45,23 +44,37 @@
     table = np.zeros((SIDE * SIDE, 2 * PART), np.float32)
     table[:, :USED] = np.cos(angle).reshape(SIDE * SIDE, USED)
     table[:, PART:PART + USED] = -np.sin(angle).reshape(SIDE * SIDE, USED)
+    high = table.astype(jnp.bfloat16)
+    low = (table - high.astype(np.float32)).astype(jnp.bfloat16)
     column = np.arange(HALF)
     pair = np.where((column == 0) | (column == SIDE // 2), 1.0, 2.0) / (SIDE * SIDE)
     weight = np.zeros((2 * PART,), np.float32)
     weight[:USED] = np.tile(pair, SIDE)
     weight[PART:PART + USED] = np.tile(pair, SIDE)
-    return table, weight
+    return high, low, weight
+
+
+def halves(values):
+    rounded = lax.reduce_precision(values, exponent_bits=8, mantissa_bits=7)
+    return rounded.astype(jnp.bfloat16), (values - rounded).astype(jnp.bfloat16)
+
+
+def three_products(values, table, dims):
+    value_high, value_low = halves(values)
+    table_high, table_low = table
+
+    def product(first, second):
+        return lax.dot_general(first, second, dims, preferred_element_type=jnp.float32)
+
+    return product(value_high, table_high) + product(value_high, table_low) + product(value_low, table_high)
 
 
 def forward(values, table):
-    return jnp.dot(values, table, precision=fast, preferred_element_type=jnp.float32)
+    return three_products(values, table, (((values.ndim - 1,), (0,)), ((), ())))
 
 
 def inverse(spectra, table, weight):
-    return lax.dot_general(
-        spectra * weight, table, (((spectra.ndim - 1,), (1,)), ((), ())),
-        precision=fast, preferred_element_type=jnp.float32,
-    )
+    return three_products(spectra * weight, table, (((spectra.ndim - 1,), (1,)), ((), ())))
 
 
 def parts(packed):
@@ -88,11 +101,10 @@
     tiles_here, pixels = images.shape
     tile_count = lax.axis_size("tile")
     atom_count = lax.axis_size("atom")
-    table_host, weight_host = half_table()
-    table = jnp.asarray(table_host)
+    high_host, low_host, weight_host = half_table()
+    table = lax.optimization_barrier((jnp.asarray(high_host), jnp.asarray(low_host)))
     weight = jnp.asarray(weight_host)
-    table, weight = lax.optimization_barrier((table, weight))
-    width = table.shape[1]
+    width = weight.shape[0]
 
     raw = dictionary.reshape(1, pixels)
     step = lax.all_to_all(jnp.broadcast_to(raw[None], (tile_count, 1, pixels)), "tile", 0, 0, tiled=True)

time: 102 us -> 122 us (1.20)
  local copies, waits for them, and re-layouts: 6.44 us -> 26.7 us
  waiting for transfers between devices: 33.9 us -> 30.9 us
  other arithmetic: 5.14 us -> 7.19 us
    unnamed x18 -> x32, local copies, waits for them, and re-layouts: 0.91 us -> 8.01 us
    gather x3 -> x2, local copies, waits for them, and re-layouts: 1.27 us -> 5.91 us  [on_device(): jnp.take(every, where_held, axis=0).reshape(slot_count * BLK, pixels)]
    dot_general x1, matrix products: 0.72 us -> 3.1 us  [on_device(): jnp.dot(member, slot_terms, precision=highest, preferred_element_type=jnp...]
    reshape x1, local copies, waits for them, and re-layouts: 0.24 us -> 2.62 us  [on_device(): conj_times(code_spec, residual_spec[:, None, :])]
    reshape x1, local copies, waits for them, and re-layouts: 0.2 us -> 2.58 us  [on_device(): block_spec.reshape(NBLK * BLK, width)]
    reshape x1, local copies, waits for them, and re-layouts: 0.19 us -> 2.39 us  [on_device(): jnp.concatenate(pieces, axis=0).reshape(atom_count, tile_count * pixels)]
    ppermute x3, waiting for transfers between devices: 11.1 us -> 9.08 us  [on_device(): lax.ppermute(pair, 'atom', [(i, (i // 2 + hop) % chips * 2 + i % 2) for i...]
    dot_general x7 -> x21, matrix products: 26.6 us -> 24.8 us  [product(): lax.dot_general(first, second, dims, preferred_element_type=jnp.float32)]
  transfers between devices with their start and end apart: 10 -> 10, of which waited for: 10 -> 10; matrix products, arithmetic and copies ran while one was open for 6% -> 8% of each run, Pallas kernels for 0% -> 0%
where the time goes in v5:
time: 122 us; the launch traced here: 121 us
  waiting for transfers between devices  30.9 us (25%)
  matrix products  27.9 us (23%)
  local copies, waits for them, and re-layouts  26.7 us (22%)
  starting transfers between devices  25.5 us (21%)
  other arithmetic  7.19 us (6%)
  between operations  3.14 us (3%)
    dot_general x21, matrix products, product(): lax.dot_general(first, second, dims, preferred_element_type=jnp.float32)  24.8 us
    all_to_all x1, starting transfers between devices, on_device(): lax.all_to_all(jnp.broadcast_to(raw[None], (tile_count, 1, pixels)), 'til...  11.3 us
    ppermute x3, waiting for transfers between devices, on_device(): lax.ppermute(pair, 'atom', [(i, (i // 2 + hop) % chips * 2 + i % 2) for i...  9.08 us
    unnamed x32, local copies, waits for them, and re-layouts  8.01 us
    all_to_all x1, waiting for transfers between devices, on_device(): lax.all_to_all(arrived, 'tile', 0, 0, tiled=True)  7.76 us
    ppermute x3, waiting for transfers between devices, on_device(): lax.ppermute(sent, 'atom', [(i, (i // 2 + hop) % chips * 2 + i % 2) for i...  6.45 us
    gather x2, local copies, waits for them, and re-layouts, on_device(): jnp.take(every, where_held, axis=0).reshape(slot_count * BLK, pixels)  5.91 us
    all_to_all x1, starting transfers between devices, on_device(): lax.all_to_all(arrived, 'tile', 0, 0, tiled=True)  5.25 us
  transfers between devices with their start and end apart: 10, of which 10 were waited for; matrix products, arithmetic and copies ran while one was open for 8% of the time, Pallas kernels for 0%

profile of v5, /device:TPU:8, one launch (start us, length us, event | category | flops | bytes accessed | tf_op | source)
XLA Modules:
  0.0 121.2 jit_solution(10951258464976764084)
XLA Ops:
  0.6 1.4 %broadcast_in_dim.37 = f32[32,1,1024]{2,1,0:T(1,128)} broadcast(f32[1024]{0:T(1024)} %bitcast.107), dimensions={2} | broadcast | bytes 135168 | tf_op jit(solution)/shard_map/broadcast_in_dim | solution.py:110
  2.0 11.3 %all-to-all-start = ((f32[32,1,1024]{2,1,0:T(1,128)}), f32[32,1,1024]{2,1,0:T(1,128)S(1)}, u32[]{:S(2)}, u32[]{:S(2)}) async-start(f32[32,1,1024]{2,1,0:T(1,128)} %broadcast_in_dim.37), calls=%async_computation | async-start | bytes 262144 | tf_op jit(solution)/shard_map/all_to_all | solution.py:110
  14.2 2.3 %fusion.28 = f32[1280,4]{0,1:T(4,128)S(1)} fusion(bf16[1024,1280]{1,0:T(8,128)(2,1)} %constant.141.clone, f32[4,1024]{1,0:T(4,128)} %param.6), kind=kOutput, calls=%fused_computation.104 | convolution fusion | flops 10493952 | bytes 2658304 | tf_op jit(solution)/shard_map/dot_general | solution.py:67
  17.2 1.3 %copy-done = bf16[1024,1280]{1,0:T(8,128)(2,1)S(1)} copy-done((bf16[1024,1280]{1,0:T(8,128)(2,1)S(1)}, bf16[1024,1280]{1,0:T(8,128)(2,1)}, u32[]{:S(2)}) %copy-start) | copy-done | bytes 2621464
  19.1 4.5 %all-to-all-done = f32[32,1,1024]{2,1,0:T(1,128)S(1)} async-done(((f32[32,1,1024]{2,1,0:T(1,128)}), f32[32,1,1024]{2,1,0:T(1,128)S(1)}, u32[]{:S(2)}, u32[]{:S(2)}) %all-to-all-start) | async-done | bytes 131104 | tf_op jit(solution)/shard_map/all_to_all | solution.py:110
  23.9 1.1 collective-permute-done
  25.1 1.7 %collective-permute-start.1 = (f32[64,1024]{1,0:T(8,128)S(1)}, f32[64,1024]{1,0:T(8,128)S(1)}, u32[]{:S(2)}, u32[]{:S(2)}) collective-permute-start(f32[64,1024]{1,0:T(8,128)S(1)} %pad_maximum_fusion.3), channel_id=1, source_target_pairs={{0,2},{1,3},{2,4},{3,5},{4,6},{5,7},{6,0},{7,1},{8,10},{9,11},{10,... | collective-permute-start | bytes 786440 | tf_op jit(solution)/shard_map/ppermute | solution.py:121
  26.8 0.9 collective-permute-start.2
  28.4 2.4 %collective-permute-start.3 = (f32[64,1024]{1,0:T(8,128)S(1)}, f32[64,1024]{1,0:T(8,128)S(1)}, u32[]{:S(2)}, u32[]{:S(2)}) collective-permute-start(f32[64,1024]{1,0:T(8,128)S(1)} %pad_maximum_fusion.3), channel_id=1, source_target_pairs={{0,6},{1,7},{2,0},{3,1},{4,2},{5,3},{6,4},{7,5},{8,14},{9,15},{10,... | collective-permute-start | bytes 786440 | tf_op jit(solution)/shard_map/ppermute | solution.py:121
  31.4 2.9 %collective-permute-done.1 = f32[64,1024]{1,0:T(8,128)S(1)} collective-permute-done((f32[64,1024]{1,0:T(8,128)S(1)}, f32[64,1024]{1,0:T(8,128)S(1)}, u32[]{:S(2)}, u32[]{:S(2)}) %collective-permute-start.1) | collective-permute-done | bytes 262176 | tf_op jit(solution)/shard_map/ppermute | solution.py:121
  35.1 2.4 %collective-permute-done.2 = f32[64,1024]{1,0:T(8,128)S(1)} collective-permute-done((f32[64,1024]{1,0:T(8,128)S(1)}, f32[64,1024]{1,0:T(8,128)S(1)}, u32[]{:S(2)}, u32[]{:S(2)}) %collective-permute-start.2) | collective-permute-done | bytes 262176 | tf_op jit(solution)/shard_map/ppermute | solution.py:121
  38.2 3.8 %collective-permute-done.3 = f32[64,1024]{1,0:T(8,128)S(1)} collective-permute-done((f32[64,1024]{1,0:T(8,128)S(1)}, f32[64,1024]{1,0:T(8,128)S(1)}, u32[]{:S(2)}, u32[]{:S(2)}) %collective-permute-start.3) | collective-permute-done | bytes 262176 | tf_op jit(solution)/shard_map/ppermute | solution.py:121
  42.7 2.4 %reshape.379 = f32[8,32768]{1,0:T(8,128)} reshape(f32[256,1024]{1,0:T(8,128)} %constant_dynamic-update-slice_fusion) | data formatting | bytes 2097152 | tf_op jit(solution)/shard_map/reshape | solution.py:122
  45.0 3.5 %gather_fusion = f32[8,32768]{1,0:T(8,128)} fusion(f32[8,32768]{1,0:T(8,128)} %reshape.379, s32[1024]{0:T(1024)S(1)} %pad_clamp_fusion), kind=kCustom, calls=%fused_computation | custom fusion | bytes 2097184 | tf_op jit(solution)/shard_map/jit(_take)/gather | solution.py:128
  48.6 2.4 %gather.7 = f32[256,1024]{1,0:T(8,128)} reshape(f32[8,32768]{1,0:T(8,128)} %gather_fusion) | data formatting | bytes 2097152 | tf_op jit(solution)/shard_map/jit(_take)/gather | solution.py:128
  51.0 1.5 %multiply_reduce_fusion = f32[256]{0:T(256)S(1)} fusion(f32[256,1024]{1,0:T(8,128)} %gather.7, pred[256]{0:T(512)(128)(4,1)S(1)} %broadcast_in_dim.19), kind=kLoop, calls=%fused_computation.46 | loop fusion | flops 786176 | bytes 1049856 | tf_op jit(solution)/shard_map/reduce_sum | solution.py:36
  52.5 2.3 %fusion.16 = f32[256,1280]{1,0:T(8,128)S(1)} fusion(bf16[1024,1280]{1,0:T(8,128)(2,1)S(1)} %copy-done, f32[256,1024]{1,0:T(8,128)} %gather.7, f32[256]{0:T(256)S(1)} %add_sqrt_fusion, pred[256]{0:T(512)(128)(4,1)S(1)} %broadcast_in_dim.19), kind=kOutput, calls=%fused_computation.63 | convolution fusion | flops 672137216 | bytes 4982016 | tf_op jit(solution)/shard_map/dot_general | solution.py:67
  54.8 0.9 convolution_add_fusion.5
  55.7 1.0 convolution_add_fusion.4
  58.0 0.9 fusion.40
  58.8 1.9 %convolution_add_fusion.13 = f32[256,1024]{1,0:T(8,128)} fusion(f32[256,1024]{1,0:T(8,128)S(1)} %fusion.40, bf16[256,1280]{1,0:T(8,128)(2,1)S(1)} %get-tuple-element.23, bf16[1024,1280]{1,0:T(8,128)(2,1)S(1)} %copy-done.2), kind=kOutput, calls=%fused_computation.28 | convolution fusion | flops 671350784 | bytes 5373952 | tf_op jit(solution)/shard_map/dot_general | solution.py:67
  61.3 2.2 %multiply_add_fusion = f32[256,1024]{1,0:T(8,128)S(1)} fusion(f32[256,1024]{1,0:T(8,128)} %convolution_add_fusion.13, bf16[256,1280]{1,0:T(8,128)(2,1)S(1)} %get-tuple-element.22, bf16[1024,1280]{1,0:T(8,128)(2,1)S(1)} %copy-done, f32[256]{0:T(256)S(1)} %max.26, f32[256]{0:T(256)S(1)} %min.26, f32[256]{0:T(256)S(1)} %mul.266), kind=kOutput, calls=%fused_computation.16 | convolution fusion | flops 673185792 | bytes 5377024 | tf_op jit(solution)/shard_map/dot_general | solution.py:67
  63.5 0.9 fusion.17
  64.4 0.9 copy-done.3
  65.2 0.9 convolution_add_fusion.3
  66.1 0.9 convolution_add_fusion.2
  68.2 0.9 fusion.41
  69.1 0.9 convolution_add_fusion.11
  69.9 1.0 minimum_subtract_fusion
  70.9 0.9 fusion.18
  71.8 0.9 convolution_add_fusion.1
  72.7 1.1 convolution_add_fusion
  74.3 1.2 pad_maximum_fusion.2
  75.4 2.6 %reshape.386 = f32[8,40960]{1,0:T(8,128)} reshape(f32[4,64,1280]{2,1,0:T(8,128)} %pad_maximum_fusion.2) | data formatting | bytes 2621440 | tf_op jit(solution)/shard_map/reshape | solution.py:164
  78.1 3.1 %fusion.27 = f32[8,40960]{1,0:T(8,128)} fusion(f32[8,40960]{1,0:T(8,128)} %reshape.386, s32[8]{0:T(128)S(1)} %eq.24), kind=kOutput, calls=%fused_computation.101 | convolution fusion | flops 31457344 | bytes 2621472 | tf_op jit(solution)/shard_map/dot_general | solution.py:166
  81.2 2.6 %reshape.387 = f32[256,1280]{1,0:T(8,128)} reshape(f32[8,40960]{1,0:T(8,128)} %fusion.27) | data formatting | bytes 2621440 | tf_op jit(solution)/shard_map/reshape | solution.py:167
  83.8 2.4 %fusion.39 = f32[260,1024]{1,0:T(8,128)S(1)} fusion(bf16[1024,1280]{1,0:T(8,128)(2,1)S(1)} %copy-done, f32[4,640]{1,0:T(4,128)S(1)} %get-tuple-element.7, f32[4,640]{1,0:T(4,128)S(1)} %get-tuple-element.6, f32[256,1280]{1,0:T(8,128)} %reshape.387, f32[1280]{0:T(1024)S(1)} %copy-done.12), kind=kOutput, calls=%fused_computation.138 | convolution fusion | flops 683238400 | bytes 5022720 | tf_op jit(solution)/shard_map/dot_general | solution.py:67
  86.2 0.9 convolution_add_fusion.9
  87.2 0.9 convolution_add_fusion.8
  89.1 1.9 %collective-permute-done.4 = f32[4,32,1024]{2,1,0:T(8,128)S(1)} collective-permute-done((f32[4,32,1024]{2,1,0:T(8,128)S(1)}, f32[4,32,1024]{2,1,0:T(8,128)S(1)}, u32[]{:S(2)}, u32[]{:S(2)}) %collective-permute-start.4) | collective-permute-done | bytes 524320 | tf_op jit(solution)/shard_map/ppermute | solution.py:174
  91.9 2.3 %collective-permute-start.6 = (f32[32,1024]{1,0:T(8,128)S(1)}, f32[32,1024]{1,0:T(8,128)S(1)}, u32[]{:S(2)}, u32[]{:S(2)}) collective-permute-start(f32[32,1024]{1,0:T(8,128)S(1)} %get-tuple-element.27), channel_id=1, source_target_pairs={{0,4},{1,5},{2,6},{3,7},{4,0},{5,1},{6,2},{7,3},{8,12},{9,13},{10,... | collective-permute-start | bytes 393224 | tf_op jit(solution)/shard_map/ppermute | solution.py:178
  94.1 0.8 collective-permute-start.7
  95.0 2.6 %collective-permute-done.5 = f32[32,1024]{1,0:T(8,128)S(1)} collective-permute-done((f32[32,1024]{1,0:T(8,128)S(1)}, f32[32,1024]{1,0:T(8,128)S(1)}, u32[]{:S(2)}, u32[]{:S(2)}) %collective-permute-start.5) | collective-permute-done | bytes 131104 | tf_op jit(solution)/shard_map/ppermute | solution.py:178
  97.6 2.1 %collective-permute-done.6 = f32[32,1024]{1,0:T(8,128)S(1)} collective-permute-done((f32[32,1024]{1,0:T(8,128)S(1)}, f32[32,1024]{1,0:T(8,128)S(1)}, u32[]{:S(2)}, u32[]{:S(2)}) %collective-permute-start.6) | collective-permute-done | bytes 131104 | tf_op jit(solution)/shard_map/ppermute | solution.py:178
  99.8 1.7 %collective-permute-done.7 = f32[32,1024]{1,0:T(8,128)S(1)} collective-permute-done((f32[32,1024]{1,0:T(8,128)S(1)}, f32[32,1024]{1,0:T(8,128)S(1)}, u32[]{:S(2)}, u32[]{:S(2)}) %collective-permute-start.7) | collective-permute-done | bytes 131104 | tf_op jit(solution)/shard_map/ppermute | solution.py:178
  102.2 5.2 %all-to-all-start.1 = ((f32[32,1,1024]{2,1,0:T(1,128)}), f32[32,1,1024]{2,1,0:T(1,128)S(1)}, u32[]{:S(2)}, u32[]{:S(2)}) async-start(f32[32,1,1024]{2,1,0:T(1,128)} %reshape.388), calls=%async_computation.1 | async-start | bytes 262144 | tf_op jit(solution)/shard_map/all_to_all | solution.py:180
  108.8 1.4 %slice.80 = f32[4,1024]{1,0:T(4,128)} slice(f32[260,1024]{1,0:T(8,128)} %copy-done.9), slice={[256:260], [0:1024]} | slice | bytes 32768 | tf_op jit(solution)/shard_map/slice | solution.py:169
  110.2 7.8 %all-to-all-done.1 = f32[32,1,1024]{2,1,0:T(1,128)S(1)} async-done(((f32[32,1,1024]{2,1,0:T(1,128)}), f32[32,1,1024]{2,1,0:T(1,128)S(1)}, u32[]{:S(2)}, u32[]{:S(2)}) %all-to-all-start.1) | async-done | bytes 131104 | tf_op jit(solution)/shard_map/all_to_all | solution.py:180
  (81 shorter events, 14.5 us)
Async XLA Ops:
  2.0 21.6 %all-to-all-start = ((f32[32,1,1024]{2,1,0:T(1,128)}), f32[32,1,1024]{2,1,0:T(1,128)S(1)}, u32[]{:S(2)}, u32[]{:S(2)}) async-start(f32[32,1,1024]{2,1,0:T(1,128)} %broadcast_in_dim.37), calls=%async_computation | async-start | bytes 262144 | tf_op jit(solution)/shard_map/all_to_all | solution.py:110
  14.2 2.5 %copy-start.1 = (bf16[1024,1280]{1,0:T(8,128)(2,1)S(1)}, bf16[1024,1280]{1,0:T(8,128)(2,1)}, u32[]{:S(2)}) copy-start(bf16[1024,1280]{1,0:T(8,128)(2,1)} %constant.142.clone) | copy-start | bytes 7864324
  14.2 2.5 %copy-start.10 = (f32[4,1024]{1,0:T(4,128)S(1)}, f32[4,1024]{1,0:T(4,128)}, u32[]{:S(2)}) copy-start(f32[4,1024]{1,0:T(4,128)} %param.6) | copy-start | bytes 49156
  16.8 1.7 %copy-start = (bf16[1024,1280]{1,0:T(8,128)(2,1)S(1)}, bf16[1024,1280]{1,0:T(8,128)(2,1)}, u32[]{:S(2)}) copy-start(bf16[1024,1280]{1,0:T(8,128)(2,1)} %constant.141.clone) | copy-start | bytes 7864324
  23.7 1.4 %collective-permute-start = (f32[32,1024]{1,0:T(8,128)S(1)}, f32[32,1024]{1,0:T(8,128)S(1)}, u32[]{:S(2)}, u32[]{:S(2)}) collective-permute-start(f32[32,1024]{1,0:T(8,128)S(1)} %bitcast.105), channel_id=1, source_target_pairs={{0,1},{1,0},{2,3},{3,2},{4,5},{5,4},{6,7},{7,6},{8,9},{9,8},{10,11... | collective-permute-start | bytes 393224 | tf_op jit(solution)/shard_map/ppermute | solution.py:117
  25.1 9.3 %collective-permute-start.1 = (f32[64,1024]{1,0:T(8,128)S(1)}, f32[64,1024]{1,0:T(8,128)S(1)}, u32[]{:S(2)}, u32[]{:S(2)}) collective-permute-start(f32[64,1024]{1,0:T(8,128)S(1)} %pad_maximum_fusion.3), channel_id=1, source_target_pairs={{0,2},{1,3},{2,4},{3,5},{4,6},{5,7},{6,0},{7,1},{8,10},{9,11},{10,... | collective-permute-start | bytes 786440 | tf_op jit(solution)/shard_map/ppermute | solution.py:121
  26.8 10.7 %collective-permute-start.2 = (f32[64,1024]{1,0:T(8,128)S(1)}, f32[64,1024]{1,0:T(8,128)S(1)}, u32[]{:S(2)}, u32[]{:S(2)}) collective-permute-start(f32[64,1024]{1,0:T(8,128)S(1)} %pad_maximum_fusion.3), channel_id=1, source_target_pairs={{0,4},{1,5},{2,6},{3,7},{4,0},{5,1},{6,2},{7,3},{8,12},{9,13},{10,... | collective-permute-start | bytes 786440 | tf_op jit(solution)/shard_map/ppermute | solution.py:121
  28.4 13.6 %collective-permute-start.3 = (f32[64,1024]{1,0:T(8,128)S(1)}, f32[64,1024]{1,0:T(8,128)S(1)}, u32[]{:S(2)}, u32[]{:S(2)}) collective-permute-start(f32[64,1024]{1,0:T(8,128)S(1)} %pad_maximum_fusion.3), channel_id=1, source_target_pairs={{0,6},{1,7},{2,0},{3,1},{4,2},{5,3},{6,4},{7,5},{8,14},{9,15},{10,... | collective-permute-start | bytes 786440 | tf_op jit(solution)/shard_map/ppermute | solution.py:121
  52.4 2.3 %copy-start.2 = (bf16[1024,1280]{1,0:T(8,128)(2,1)S(1)}, bf16[1024,1280]{1,0:T(8,128)(2,1)}, u32[]{:S(2)}) copy-start(bf16[1024,1280]{1,0:T(8,128)(2,1)} %constant.142.clone) | copy-start | bytes 7864324
  52.5 2.3 %copy-start.7 = (f32[256,1024]{1,0:T(8,128)S(1)}, f32[256,1024]{1,0:T(8,128)}, u32[]{:S(2)}) copy-start(f32[256,1024]{1,0:T(8,128)} %gather.7) | copy-start | bytes 3145732
  56.7 1.1 copy-start.5
  56.9 0.8 copy-start.12
  63.5 1.7 %copy-start.3 = (bf16[1024,1280]{1,0:T(8,128)(2,1)S(1)}, bf16[1024,1280]{1,0:T(8,128)(2,1)}, u32[]{:S(2)}) copy-start(bf16[1024,1280]{1,0:T(8,128)(2,1)} %constant.142.clone) | copy-start | bytes 7864324
  66.1 1.3 %copy-start.6 = (f32[256,1280]{1,0:T(8,128)S(1)}, f32[256,1280]{1,0:T(8,128)}, u32[]{:S(2)}) copy-start(f32[256,1280]{1,0:T(8,128)} %copy-done.5) | copy-start | bytes 3932164
  83.7 2.4 %copy-start.4 = (bf16[1024,1280]{1,0:T(8,128)(2,1)S(1)}, bf16[1024,1280]{1,0:T(8,128)(2,1)}, u32[]{:S(2)}) copy-start(bf16[1024,1280]{1,0:T(8,128)(2,1)} %constant.142.clone) | copy-start | bytes 7864324
  83.8 2.5 %copy-start.8 = (f32[256,1280]{1,0:T(8,128)S(1)}, f32[256,1280]{1,0:T(8,128)}, u32[]{:S(2)}) copy-start(f32[256,1280]{1,0:T(8,128)} %reshape.387) | copy-start | bytes 3932164
  88.2 1.0 copy-start.9
  89.1 1.9 %collective-permute-start.4 = (f32[4,32,1024]{2,1,0:T(8,128)S(1)}, f32[4,32,1024]{2,1,0:T(8,128)S(1)}, u32[]{:S(2)}, u32[]{:S(2)}) collective-permute-start(f32[4,32,1024]{2,1,0:T(8,128)S(1)} %dynamic-slice_bitcast_fusion), channel_id=1, source_target_pairs={{0,1},{1,0},{2,3},{3,2},{4,5},{5,4},{6,7},{7,6},{8,9},{9,8},{10,11... | collective-permute-start | bytes 1572872 | tf_op jit(solution)/shard_map/ppermute | solution.py:174
  91.1 16.4 %copy-start.11 = (f32[1,1,1024]{2,1,0:T(1,128)S(1)}, f32[1,1,1024]{2,1,0:T(1,128)}, u32[]{:S(2)}) copy-start(f32[1,1,1024]{2,1,0:T(1,128)} %param.8) | copy-start | bytes 12292
  91.2 6.4 %collective-permute-start.5 = (f32[32,1024]{1,0:T(8,128)S(1)}, f32[32,1024]{1,0:T(8,128)S(1)}, u32[]{:S(2)}, u32[]{:S(2)}) collective-permute-start(f32[32,1024]{1,0:T(8,128)S(1)} %get-tuple-element.25), channel_id=1, source_target_pairs={{0,2},{1,3},{2,4},{3,5},{4,6},{5,7},{6,0},{7,1},{8,10},{9,11},{10,... | collective-permute-start | bytes 393224 | tf_op jit(solution)/shard_map/ppermute | solution.py:178
  91.9 7.9 %collective-permute-start.6 = (f32[32,1024]{1,0:T(8,128)S(1)}, f32[32,1024]{1,0:T(8,128)S(1)}, u32[]{:S(2)}, u32[]{:S(2)}) collective-permute-start(f32[32,1024]{1,0:T(8,128)S(1)} %get-tuple-element.27), channel_id=1, source_target_pairs={{0,4},{1,5},{2,6},{3,7},{4,0},{5,1},{6,2},{7,3},{8,12},{9,13},{10,... | collective-permute-start | bytes 393224 | tf_op jit(solution)/shard_map/ppermute | solution.py:178
  94.1 7.3 %collective-permute-start.7 = (f32[32,1024]{1,0:T(8,128)S(1)}, f32[32,1024]{1,0:T(8,128)S(1)}, u32[]{:S(2)}, u32[]{:S(2)}) collective-permute-start(f32[32,1024]{1,0:T(8,128)S(1)} %get-tuple-element.26), channel_id=1, source_target_pairs={{0,6},{1,7},{2,0},{3,1},{4,2},{5,3},{6,4},{7,5},{8,14},{9,15},{10,... | collective-permute-start | bytes 393224 | tf_op jit(solution)/shard_map/ppermute | solution.py:178
  102.2 15.7 %all-to-all-start.1 = ((f32[32,1,1024]{2,1,0:T(1,128)}), f32[32,1,1024]{2,1,0:T(1,128)S(1)}, u32[]{:S(2)}, u32[]{:S(2)}) async-start(f32[32,1,1024]{2,1,0:T(1,128)} %reshape.388), calls=%async_computation.1 | async-start | bytes 262144 | tf_op jit(solution)/shard_map/all_to_all | solution.py:180

commit v6 on v4

--- a/solution.py
+++ b/solution.py
@@ -107,7 +107,7 @@
     pieces = [pair]
     for hop in range(1, chips):
         pieces.append(lax.ppermute(pair, "atom", [(i, ((i // 2 + hop) % chips) * 2 + i % 2) for i in range(atom_count)]))
-    every = jnp.concatenate(pieces, axis=0).reshape(atom_count, tile_count * pixels)
+    every = jnp.concatenate(pieces, axis=0).reshape(atom_count, tile_count, pixels)
 
     image_spec = forward(images.reshape(1, tiles_here, pixels), table).reshape(tiles_here, width)
     slot_count = tiles_here * ACT
@@ -149,9 +149,9 @@
     code_spec = forward(prior.reshape(tiles_here * rows, pixels), table).reshape(tiles_here, rows, width)
     recon_spec = product_sum(chosen, code_spec)
     residual_spec = recon_spec - image_spec
-    slot_terms = conj_times(code_spec, residual_spec[:, None, :]).reshape(slot_count, BLK * width)
+    slot_terms = conj_times(code_spec, residual_spec[:, None, :]).reshape(slot_count, BLK, width)
     member = (jnp.arange(NBLK, dtype=jnp.int32)[:, None] == flat_ids[None, :]).astype(jnp.float32)
-    block_spec = jnp.dot(member, slot_terms, precision=highest, preferred_element_type=jnp.float32)
+    block_spec = jnp.einsum("bs,skx->bkx", member, slot_terms, precision=highest, preferred_element_type=jnp.float32)
     both = inverse(jnp.concatenate([block_spec.reshape(NBLK * BLK, width), recon_spec], axis=0), table, weight)
     partial = both[:NBLK * BLK].reshape(NBLK, BLK, pixels)
     recon = both[NBLK * BLK:]

time: 102 us -> 99.2 us (0.973)
  matrix products: 27.3 us -> 25.6 us
  local copies, waits for them, and re-layouts: 6.44 us -> 5.41 us
    dot_general x3, matrix products: 12.5 us -> 10 us  [inverse(): lax.dot_general(spectra * weight, table, (((spectra.ndim - 1,), (1,)), ((...]
where the time goes in v6:
time: 99.2 us; the launch traced here: 98.8 us
  waiting for transfers between devices  34.1 us (34%)
  matrix products  25.6 us (26%)
  starting transfers between devices  25.2 us (25%)
  local copies, waits for them, and re-layouts  5.41 us (5%)
  other arithmetic  5.3 us (5%)
  between operations  3.18 us (3%)
    dot_general x4, matrix products, forward(): jnp.dot(values, table, precision=fast, preferred_element_type=jnp.float32)  14.1 us
    all_to_all x1, starting transfers between devices, on_device(): lax.all_to_all(jnp.broadcast_to(raw[None], (tile_count, 1, pixels)), 'til...  11.3 us
    ppermute x3, waiting for transfers between devices, on_device(): lax.ppermute(pair, 'atom', [(i, (i // 2 + hop) % chips * 2 + i % 2) for i...  11.1 us
    dot_general x3, matrix products, inverse(): lax.dot_general(spectra * weight, table, (((spectra.ndim - 1,), (1,)), ((...  10 us
    all_to_all x1, waiting for transfers between devices, on_device(): lax.all_to_all(arrived, 'tile', 0, 0, tiled=True)  8.35 us
    ppermute x3, waiting for transfers between devices, on_device(): lax.ppermute(sent, 'atom', [(i, (i // 2 + hop) % chips * 2 + i % 2) for i...  6.27 us
    all_to_all x1, waiting for transfers between devices, on_device(): lax.all_to_all(jnp.broadcast_to(raw[None], (tile_count, 1, pixels)), 'til...  5.53 us
    ppermute x3, starting transfers between devices, on_device(): lax.ppermute(pair, 'atom', [(i, (i // 2 + hop) % chips * 2 + i % 2) for i...  5.26 us
  transfers between devices with their start and end apart: 10, of which 10 were waited for; matrix products, arithmetic and copies ran while one was open for 6% of the time, Pallas kernels for 0%

profile of v6, /device:TPU:8, one launch (start us, length us, event | category | flops | bytes accessed | tf_op | source)
XLA Modules:
  0.0 98.8 jit_solution(14171923638457763355)
XLA Ops:
  0.6 1.4 %broadcast_in_dim.47 = f32[32,1,1024]{2,1,0:T(1,128)} broadcast(f32[1024]{0:T(1024)} %bitcast.100), dimensions={2} | broadcast | bytes 135168 | tf_op jit(solution)/shard_map/broadcast_in_dim | solution.py:98
  2.0 11.3 %all-to-all-start = ((f32[32,1,1024]{2,1,0:T(1,128)}), f32[32,1,1024]{2,1,0:T(1,128)S(1)}, u32[]{:S(2)}, u32[]{:S(2)}) async-start(f32[32,1,1024]{2,1,0:T(1,128)} %broadcast_in_dim.47), calls=%async_computation | async-start | bytes 262144 | tf_op jit(solution)/shard_map/all_to_all | solution.py:98
  13.4 0.8 copy.21
  14.2 3.7 %convolution_bitcast_fusion = f32[4,1280]{1,0:T(4,128)S(1)} fusion(f32[1024,1280]{1,0:T(8,128)} %constant.139.clone, f32[4,1024]{1,0:T(4,128)S(1)} %copy-done), kind=kOutput, calls=%fused_computation.11 | convolution fusion | flops 31457280 | bytes 5279744 | tf_op jit(solution)/shard_map/dot_general | solution.py:57
  18.1 5.5 %all-to-all-done = f32[32,1,1024]{2,1,0:T(1,128)S(1)} async-done(((f32[32,1,1024]{2,1,0:T(1,128)}), f32[32,1,1024]{2,1,0:T(1,128)S(1)}, u32[]{:S(2)}, u32[]{:S(2)}) %all-to-all-start) | async-done | bytes 131104 | tf_op jit(solution)/shard_map/all_to_all | solution.py:98
  23.8 0.1 copy.22
  24.1 1.0 %collective-permute-done = f32[32,1024]{1,0:T(8,128)S(1)} collective-permute-done((f32[32,1024]{1,0:T(8,128)S(1)}, f32[32,1024]{1,0:T(8,128)S(1)}, u32[]{:S(2)}, u32[]{:S(2)}) %collective-permute-start) | collective-permute-done | bytes 131104 | tf_op jit(solution)/shard_map/ppermute | solution.py:105
  25.1 1.7 %collective-permute-start.1 = (f32[64,1024]{1,0:T(8,128)S(1)}, f32[64,1024]{1,0:T(8,128)S(1)}, u32[]{:S(2)}, u32[]{:S(2)}) collective-permute-start(f32[64,1024]{1,0:T(8,128)S(1)} %pad_maximum_fusion.1), channel_id=1, source_target_pairs={{0,2},{1,3},{2,4},{3,5},{4,6},{5,7},{6,0},{7,1},{8,10},{9,11},{10,... | collective-permute-start | bytes 786440 | tf_op jit(solution)/shard_map/ppermute | solution.py:109
  26.8 0.9 collective-permute-start.2
  27.7 2.7 %collective-permute-start.3 = (f32[64,1024]{1,0:T(8,128)S(1)}, f32[64,1024]{1,0:T(8,128)S(1)}, u32[]{:S(2)}, u32[]{:S(2)}) collective-permute-start(f32[64,1024]{1,0:T(8,128)S(1)} %pad_maximum_fusion.1), channel_id=1, source_target_pairs={{0,6},{1,7},{2,0},{3,1},{4,2},{5,3},{6,4},{7,5},{8,14},{9,15},{10,... | collective-permute-start | bytes 786440 | tf_op jit(solution)/shard_map/ppermute | solution.py:109
  30.4 3.9 %collective-permute-done.1 = f32[64,1024]{1,0:T(8,128)S(1)} collective-permute-done((f32[64,1024]{1,0:T(8,128)S(1)}, f32[64,1024]{1,0:T(8,128)S(1)}, u32[]{:S(2)}, u32[]{:S(2)}) %collective-permute-start.1) | collective-permute-done | bytes 262176 | tf_op jit(solution)/shard_map/ppermute | solution.py:109
  34.4 3.1 %collective-permute-done.2 = f32[64,1024]{1,0:T(8,128)S(1)} collective-permute-done((f32[64,1024]{1,0:T(8,128)S(1)}, f32[64,1024]{1,0:T(8,128)S(1)}, u32[]{:S(2)}, u32[]{:S(2)}) %collective-permute-start.2) | collective-permute-done | bytes 262176 | tf_op jit(solution)/shard_map/ppermute | solution.py:109
  37.5 4.1 %collective-permute-done.3 = f32[64,1024]{1,0:T(8,128)S(1)} collective-permute-done((f32[64,1024]{1,0:T(8,128)S(1)}, f32[64,1024]{1,0:T(8,128)S(1)}, u32[]{:S(2)}, u32[]{:S(2)}) %collective-permute-start.3) | collective-permute-done | bytes 262176 | tf_op jit(solution)/shard_map/ppermute | solution.py:109
  41.6 0.6 gather_fusion
  42.2 0.2 multiply_reduce_fusion
  42.6 0.2 fusion.33
  42.7 5.0 %fusion.8 = f32[4,64,1280]{2,1,0:T(8,128)S(1)} fusion(f32[4,64,1024]{2,1,0:T(8,128)S(1)} %fusion.33, f32[1024,1280]{1,0:T(8,128)} %constant.139.clone), kind=kOutput, calls=%fused_computation.9 | convolution fusion | flops 2013265920 | bytes 7602176 | tf_op jit(solution)/shard_map/dot_general | solution.py:57
  47.8 1.1 %multiply_add_fusion.3 = (f32[4,64,640]{2,1,0:T(8,128)S(1)}, f32[4,64,640]{2,1,0:T(8,128)}, f32[4,640]{1,0:T(4,128)S(1)}) fusion(f32[4,64,1280]{2,1,0:T(8,128)S(1)} %fusion.8, f32[4,640]{1,0:T(4,128)S(1)} %get-tuple-element.29, f32[4,640]{1,0:T(4,128)S(1)} %get-tuple-element.28), kind=kLoop, calls=%fused_computation.50 | loop fusion | flops 1635840 | bytes 2652160 | tf_op jit(solution)/shard_map/add | solution.py:74
  48.8 0.1 reduce_max.9
  49.0 5.2 %multiply_add_fusion = f32[4,64,1024]{2,1,0:T(8,128)S(1)} fusion(f32[1024,1280]{1,0:T(8,128)} %constant.139.clone, f32[4,64,640]{2,1,0:T(8,128)} %get-tuple-element.19, f32[4,64,640]{2,1,0:T(8,128)S(1)} %get-tuple-element.18, f32[1280]{0:T(1024)S(1)} %copy-done.1, f32[4]{0:T(128)S(1)} %fusion.66, f32[4]{0:T(128)S(1)} %get-tuple-element.12, ...), kind=kOutput, calls=%fused_computation.12 | convolution fusion | flops 2015756288 | bytes 7607344 | tf_op jit(solution)/shard_map/dot_general | solution.py:61
  54.2 2.6 %fusion.4 = f32[4,64,1280]{2,1,0:T(8,128)S(1)} fusion(f32[4,64,1024]{2,1,0:T(8,128)S(1)} %multiply_add_fusion, f32[1024,1280]{1,0:T(8,128)S(1)} %bitcast.91), kind=kOutput, calls=%fused_computation.5 | convolution fusion | flops 2013265920 | bytes 7602176 | tf_op jit(solution)/shard_map/dot_general | solution.py:57
  56.8 0.3 subtract_reduce_fusion.1
  57.1 0.1 multiply_add_fusion.2
  57.3 2.4 %fusion.19 = f32[4,64,1024]{2,1,0:T(8,128)S(1)} fusion(f32[4,64,1024]{2,1,0:T(8,128)S(1)} %multiply_add_fusion, f32[1024,1280]{1,0:T(8,128)S(1)} %bitcast.91, f32[4,64,640]{2,1,0:T(8,128)S(1)} %get-tuple-element.17, f32[4,64,640]{2,1,0:T(8,128)S(1)} %get-tuple-element.16, f32[1280]{0:T(1024)S(1)} %copy-done.1, f32[4]{0:T(128)S(1)} %get-tuple-element.13), kind=kOutput, calls=%fused_computation.16 | convolution fusion | flops 2014445568 | bytes 8655888 | tf_op jit(solution)/shard_map/dot_general | solution.py:61
  59.7 2.9 %fusion = f32[4,64,1280]{2,1,0:T(8,128)S(1)} fusion(f32[1024,1280]{1,0:T(8,128)S(1)} %bitcast.91, f32[4,64,1024]{2,1,0:T(8,128)S(1)} %fusion.19, f32[4]{0:T(128)S(1)} %fusion.66, f32[4]{0:T(128)S(1)} %get-tuple-element.12), kind=kOutput, calls=%fused_computation.1 | convolution fusion | flops 2014052352 | bytes 7602208 | tf_op jit(solution)/shard_map/dot_general | solution.py:57
  62.5 0.3 subtract_reduce_fusion
  62.8 0.1 multiply_add_fusion.1
  63.0 0.1 pad_maximum_fusion
  63.1 1.4 %fusion.31 = f32[8,32,1280]{2,0,1:T(8,128)S(1)} fusion(f32[8,32,1280]{2,1,0:T(8,128)S(1)} %bitcast.93, s32[8]{0:T(128)S(1)} %eq.24), kind=kOutput, calls=%fused_computation.30 | convolution fusion | flops 31457344 | bytes 2621472 | tf_op jit(solution)/shard_map/bs,skx->bkx/dot_general | solution.py:154
  64.5 0.4 copy.25
  65.0 2.4 %fusion.22 = f32[260,1024]{1,0:T(8,128)S(1)} fusion(f32[1024,1280]{1,0:T(8,128)S(1)} %bitcast.91, f32[4,640]{1,0:T(4,128)S(1)} %get-tuple-element.7, f32[4,640]{1,0:T(4,128)S(1)} %get-tuple-element.6, f32[256,1280]{1,0:T(8,128)S(1)} %bitcast.94, f32[1280]{0:T(1024)S(1)} %copy-done.1), kind=kOutput, calls=%fused_computation.18 | convolution fusion | flops 2045721600 | bytes 7644160 | tf_op jit(solution)/shard_map/dot_general | solution.py:61
  67.4 0.1 slice.81
  67.7 1.8 %collective-permute-done.4 = f32[4,32,1024]{2,1,0:T(8,128)S(1)} collective-permute-done((f32[4,32,1024]{2,1,0:T(8,128)S(1)}, f32[4,32,1024]{2,1,0:T(8,128)S(1)}, u32[]{:S(2)}, u32[]{:S(2)}) %collective-permute-start.4) | collective-permute-done | bytes 524320 | tf_op jit(solution)/shard_map/ppermute | solution.py:162
  69.7 1.1 %collective-permute-start.5 = (f32[32,1024]{1,0:T(8,128)S(1)}, f32[32,1024]{1,0:T(8,128)S(1)}, u32[]{:S(2)}, u32[]{:S(2)}) collective-permute-start(f32[32,1024]{1,0:T(8,128)S(1)} %get-tuple-element.21), channel_id=1, source_target_pairs={{0,2},{1,3},{2,4},{3,5},{4,6},{5,7},{6,0},{7,1},{8,10},{9,11},{10,... | collective-permute-start | bytes 393224 | tf_op jit(solution)/shard_map/ppermute | solution.py:166
  70.8 1.6 %collective-permute-start.6 = (f32[32,1024]{1,0:T(8,128)S(1)}, f32[32,1024]{1,0:T(8,128)S(1)}, u32[]{:S(2)}, u32[]{:S(2)}) collective-permute-start(f32[32,1024]{1,0:T(8,128)S(1)} %get-tuple-element.23), channel_id=1, source_target_pairs={{0,4},{1,5},{2,6},{3,7},{4,0},{5,1},{6,2},{7,3},{8,12},{9,13},{10,... | collective-permute-start | bytes 393224 | tf_op jit(solution)/shard_map/ppermute | solution.py:166
  72.4 1.5 %collective-permute-start.7 = (f32[32,1024]{1,0:T(8,128)S(1)}, f32[32,1024]{1,0:T(8,128)S(1)}, u32[]{:S(2)}, u32[]{:S(2)}) collective-permute-start(f32[32,1024]{1,0:T(8,128)S(1)} %get-tuple-element.22), channel_id=1, source_target_pairs={{0,6},{1,7},{2,0},{3,1},{4,2},{5,3},{6,4},{7,5},{8,14},{9,15},{10,... | collective-permute-start | bytes 393224 | tf_op jit(solution)/shard_map/ppermute | solution.py:166
  73.9 2.2 %collective-permute-done.5 = f32[32,1024]{1,0:T(8,128)S(1)} collective-permute-done((f32[32,1024]{1,0:T(8,128)S(1)}, f32[32,1024]{1,0:T(8,128)S(1)}, u32[]{:S(2)}, u32[]{:S(2)}) %collective-permute-start.5) | collective-permute-done | bytes 131104 | tf_op jit(solution)/shard_map/ppermute | solution.py:166
  76.1 2.5 %collective-permute-done.6 = f32[32,1024]{1,0:T(8,128)S(1)} collective-permute-done((f32[32,1024]{1,0:T(8,128)S(1)}, f32[32,1024]{1,0:T(8,128)S(1)}, u32[]{:S(2)}, u32[]{:S(2)}) %collective-permute-start.6) | collective-permute-done | bytes 131104 | tf_op jit(solution)/shard_map/ppermute | solution.py:166
  78.7 1.5 %collective-permute-done.7 = f32[32,1024]{1,0:T(8,128)S(1)} collective-permute-done((f32[32,1024]{1,0:T(8,128)S(1)}, f32[32,1024]{1,0:T(8,128)S(1)}, u32[]{:S(2)}, u32[]{:S(2)}) %collective-permute-start.7) | collective-permute-done | bytes 131104 | tf_op jit(solution)/shard_map/ppermute | solution.py:166
  80.2 0.7 reshape.375
  80.9 4.3 %all-to-all-start.1 = ((f32[32,1,1024]{2,1,0:T(1,128)}), f32[32,1,1024]{2,1,0:T(1,128)S(1)}, u32[]{:S(2)}, u32[]{:S(2)}) async-start(f32[32,1,1024]{2,1,0:T(1,128)} %reshape.375), calls=%async_computation.1 | async-start | bytes 262144 | tf_op jit(solution)/shard_map/all_to_all | solution.py:168
  85.2 0.6 multiply_reduce_fusion.2
  86.5 0.6 slice.80
  87.1 8.3 %all-to-all-done.1 = f32[32,1,1024]{2,1,0:T(1,128)S(1)} async-done(((f32[32,1,1024]{2,1,0:T(1,128)}), f32[32,1,1024]{2,1,0:T(1,128)S(1)}, u32[]{:S(2)}, u32[]{:S(2)}) %all-to-all-start.1) | async-done | bytes 131104 | tf_op jit(solution)/shard_map/all_to_all | solution.py:168
  95.5 0.1 reduce_sum.97
  95.6 0.6 multiply_reduce_fusion.1
  96.9 0.6 fusion.49
  98.2 0.6 subtract_divide_fusion
  (45 shorter events, 1.1 us)
Async XLA Ops:
  0.6 13.6 %copy-start = (f32[4,1024]{1,0:T(4,128)S(1)}, f32[4,1024]{1,0:T(4,128)}, u32[]{:S(2)}) copy-start(f32[4,1024]{1,0:T(4,128)} %param.5) | copy-start | bytes 49156
  2.0 21.6 %all-to-all-start = ((f32[32,1,1024]{2,1,0:T(1,128)}), f32[32,1,1024]{2,1,0:T(1,128)S(1)}, u32[]{:S(2)}, u32[]{:S(2)}) async-start(f32[32,1,1024]{2,1,0:T(1,128)} %broadcast_in_dim.47), calls=%async_computation | async-start | bytes 262144 | tf_op jit(solution)/shard_map/all_to_all | solution.py:98
  14.2 3.7 %copy-start.3 = (s32[4,2]{0,1:T(2,128)S(1)}, s32[4,2]{0,1:T(2,128)}, u32[]{:S(2)}) copy-start(s32[4,2]{0,1:T(2,128)} %param.6) | copy-start | bytes 100
  23.7 1.4 %collective-permute-start = (f32[32,1024]{1,0:T(8,128)S(1)}, f32[32,1024]{1,0:T(8,128)S(1)}, u32[]{:S(2)}, u32[]{:S(2)}) collective-permute-start(f32[32,1024]{1,0:T(8,128)S(1)} %bitcast.98), channel_id=1, source_target_pairs={{0,1},{1,0},{2,3},{3,2},{4,5},{5,4},{6,7},{7,6},{8,9},{9,8},{10,11... | collective-permute-start | bytes 393224 | tf_op jit(solution)/shard_map/ppermute | solution.py:105
  25.1 9.3 %collective-permute-start.1 = (f32[64,1024]{1,0:T(8,128)S(1)}, f32[64,1024]{1,0:T(8,128)S(1)}, u32[]{:S(2)}, u32[]{:S(2)}) collective-permute-start(f32[64,1024]{1,0:T(8,128)S(1)} %pad_maximum_fusion.1), channel_id=1, source_target_pairs={{0,2},{1,3},{2,4},{3,5},{4,6},{5,7},{6,0},{7,1},{8,10},{9,11},{10,... | collective-permute-start | bytes 786440 | tf_op jit(solution)/shard_map/ppermute | solution.py:109
  26.8 10.7 %collective-permute-start.2 = (f32[64,1024]{1,0:T(8,128)S(1)}, f32[64,1024]{1,0:T(8,128)S(1)}, u32[]{:S(2)}, u32[]{:S(2)}) collective-permute-start(f32[64,1024]{1,0:T(8,128)S(1)} %pad_maximum_fusion.1), channel_id=1, source_target_pairs={{0,4},{1,5},{2,6},{3,7},{4,0},{5,1},{6,2},{7,3},{8,12},{9,13},{10,... | collective-permute-start | bytes 786440 | tf_op jit(solution)/shard_map/ppermute | solution.py:109
  27.7 13.8 %collective-permute-start.3 = (f32[64,1024]{1,0:T(8,128)S(1)}, f32[64,1024]{1,0:T(8,128)S(1)}, u32[]{:S(2)}, u32[]{:S(2)}) collective-permute-start(f32[64,1024]{1,0:T(8,128)S(1)} %pad_maximum_fusion.1), channel_id=1, source_target_pairs={{0,6},{1,7},{2,0},{3,1},{4,2},{5,3},{6,4},{7,5},{8,14},{9,15},{10,... | collective-permute-start | bytes 786440 | tf_op jit(solution)/shard_map/ppermute | solution.py:109
  47.7 1.2 %copy-start.1 = (f32[1280]{0:T(1024)S(1)}, f32[1280]{0:T(1024)}, u32[]{:S(2)}) copy-start(f32[1280]{0:T(1024)} %constant.140.clone) | copy-start | bytes 15364
  47.7 6.5 %slice-start = ((s8[5242880]{0:T(1024)(128)(4,1)}), s8[1048576]{0:T(1024)(128)(4,1)S(1)}, s32[]{:S(2)}) async-start(s8[5242880]{0:T(1024)(128)(4,1)} %bitcast.90), calls=%async_computation.2 | async-start | bytes 2097152
  49.0 5.3 %slice-start.1 = ((s8[5242880]{0:T(1024)(128)(4,1)}), s8[4194304]{0:T(1024)(128)(4,1)S(1)}, s32[]{:S(2)}) async-start(s8[5242880]{0:T(1024)(128)(4,1)} %bitcast.90), calls=%async_computation.3 | async-start | bytes 8388608
  67.6 2.0 %collective-permute-start.4 = (f32[4,32,1024]{2,1,0:T(8,128)S(1)}, f32[4,32,1024]{2,1,0:T(8,128)S(1)}, u32[]{:S(2)}, u32[]{:S(2)}) collective-permute-start(f32[4,32,1024]{2,1,0:T(8,128)S(1)} %dynamic-slice_bitcast_fusion), channel_id=1, source_target_pairs={{0,1},{1,0},{2,3},{3,2},{4,5},{5,4},{6,7},{7,6},{8,9},{9,8},{10,11... | collective-permute-start | bytes 1572872 | tf_op jit(solution)/shard_map/ppermute | solution.py:162
  69.6 15.6 %copy-start.2 = (f32[1,1,1024]{2,1,0:T(1,128)S(1)}, f32[1,1,1024]{2,1,0:T(1,128)}, u32[]{:S(2)}) copy-start(f32[1,1,1024]{2,1,0:T(1,128)} %param.7) | copy-start | bytes 12292
  69.7 6.4 %collective-permute-start.5 = (f32[32,1024]{1,0:T(8,128)S(1)}, f32[32,1024]{1,0:T(8,128)S(1)}, u32[]{:S(2)}, u32[]{:S(2)}) collective-permute-start(f32[32,1024]{1,0:T(8,128)S(1)} %get-tuple-element.21), channel_id=1, source_target_pairs={{0,2},{1,3},{2,4},{3,5},{4,6},{5,7},{6,0},{7,1},{8,10},{9,11},{10,... | collective-permute-start | bytes 393224 | tf_op jit(solution)/shard_map/ppermute | solution.py:166
  70.8 7.9 %collective-permute-start.6 = (f32[32,1024]{1,0:T(8,128)S(1)}, f32[32,1024]{1,0:T(8,128)S(1)}, u32[]{:S(2)}, u32[]{:S(2)}) collective-permute-start(f32[32,1024]{1,0:T(8,128)S(1)} %get-tuple-element.23), channel_id=1, source_target_pairs={{0,4},{1,5},{2,6},{3,7},{4,0},{5,1},{6,2},{7,3},{8,12},{9,13},{10,... | collective-permute-start | bytes 393224 | tf_op jit(solution)/shard_map/ppermute | solution.py:166
  72.4 7.8 %collective-permute-start.7 = (f32[32,1024]{1,0:T(8,128)S(1)}, f32[32,1024]{1,0:T(8,128)S(1)}, u32[]{:S(2)}, u32[]{:S(2)}) collective-permute-start(f32[32,1024]{1,0:T(8,128)S(1)} %get-tuple-element.22), channel_id=1, source_target_pairs={{0,6},{1,7},{2,0},{3,1},{4,2},{5,3},{6,4},{7,5},{8,14},{9,15},{10,... | collective-permute-start | bytes 393224 | tf_op jit(solution)/shard_map/ppermute | solution.py:166
  80.9 14.5 %all-to-all-start.1 = ((f32[32,1,1024]{2,1,0:T(1,128)}), f32[32,1,1024]{2,1,0:T(1,128)S(1)}, u32[]{:S(2)}, u32[]{:S(2)}) async-start(f32[32,1,1024]{2,1,0:T(1,128)} %reshape.375), calls=%async_computation.1 | async-start | bytes 262144 | tf_op jit(solution)/shard_map/all_to_all | solution.py:168

commit v7 on v6

--- a/solution.py
+++ b/solution.py
@@ -95,7 +95,8 @@
     width = table.shape[1]
 
     raw = dictionary.reshape(1, pixels)
-    step = lax.all_to_all(jnp.broadcast_to(raw[None], (tile_count, 1, pixels)), "tile", 0, 0, tiled=True)
+    dense = raw.reshape(1, 8, pixels // 8)
+    step = lax.all_to_all(jnp.broadcast_to(dense, (tile_count, 8, pixels // 8)), "tile", 0, 0, tiled=True)
     mine = step.reshape(tile_count, pixels)
     own = unit_rows(raw)
     place = lax.axis_index("atom")

time: 99.2 us -> 99.1 us (level)
  no operation moved by 1% of the time
where the time goes in v7:
time: 99.1 us; the launch traced here: 98.8 us
  waiting for transfers between devices  34.1 us (34%)
  matrix products  25.6 us (26%)
  starting transfers between devices  25.2 us (25%)
  local copies, waits for them, and re-layouts  5.39 us (5%)
  other arithmetic  5.29 us (5%)
  between operations  3.18 us (3%)
    dot_general x4, matrix products, forward(): jnp.dot(values, table, precision=fast, preferred_element_type=jnp.float32)  14.1 us
    all_to_all x1, starting transfers between devices, on_device(): lax.all_to_all(jnp.broadcast_to(dense, (tile_count, 8, pixels // 8)), 'ti...  11.3 us
    ppermute x3, waiting for transfers between devices, on_device(): lax.ppermute(pair, 'atom', [(i, (i // 2 + hop) % chips * 2 + i % 2) for i...  10.8 us
    dot_general x3, matrix products, inverse(): lax.dot_general(spectra * weight, table, (((spectra.ndim - 1,), (1,)), ((...  10 us
    all_to_all x1, waiting for transfers between devices, on_device(): lax.all_to_all(arrived, 'tile', 0, 0, tiled=True)  8.35 us
    ppermute x3, waiting for transfers between devices, on_device(): lax.ppermute(sent, 'atom', [(i, (i // 2 + hop) % chips * 2 + i % 2) for i...  6.26 us
    all_to_all x1, waiting for transfers between devices, on_device(): lax.all_to_all(jnp.broadcast_to(dense, (tile_count, 8, pixels // 8)), 'ti...  5.53 us
    ppermute x3, starting transfers between devices, on_device(): lax.ppermute(pair, 'atom', [(i, (i // 2 + hop) % chips * 2 + i % 2) for i...  5.26 us
  transfers between devices with their start and end apart: 10, of which 10 were waited for; matrix products, arithmetic and copies ran while one was open for 6% of the time, Pallas kernels for 0%

profile of v7, /device:TPU:8, one launch (start us, length us, event | category | flops | bytes accessed | tf_op | source)
XLA Modules:
  0.0 98.8 jit_solution(14355560690483048113)
XLA Ops:
  0.6 1.4 %broadcast_in_dim.47 = f32[32,8,128]{2,1,0:T(8,128)} broadcast(f32[8,128]{1,0:T(8,128)} %bitcast.104), dimensions={1,2} | broadcast | bytes 135168 | tf_op jit(solution)/shard_map/broadcast_in_dim | solution.py:99
  2.0 11.3 %all-to-all-start = ((f32[32,8,128]{2,1,0:T(8,128)}), f32[32,8,128]{2,1,0:T(8,128)S(1)}, u32[]{:S(2)}, u32[]{:S(2)}) async-start(f32[32,8,128]{2,1,0:T(8,128)} %broadcast_in_dim.47), calls=%async_computation | async-start | bytes 262144 | tf_op jit(solution)/shard_map/all_to_all | solution.py:99
  13.3 0.8 copy.21
  14.2 3.7 %convolution_bitcast_fusion = f32[4,1280]{1,0:T(4,128)S(1)} fusion(f32[1024,1280]{1,0:T(8,128)} %constant.139.clone, f32[4,1024]{1,0:T(4,128)S(1)} %copy-done), kind=kOutput, calls=%fused_computation.11 | convolution fusion | flops 31457280 | bytes 5279744 | tf_op jit(solution)/shard_map/dot_general | solution.py:57
  18.1 5.5 %all-to-all-done = f32[32,8,128]{2,1,0:T(8,128)S(1)} async-done(((f32[32,8,128]{2,1,0:T(8,128)}), f32[32,8,128]{2,1,0:T(8,128)S(1)}, u32[]{:S(2)}, u32[]{:S(2)}) %all-to-all-start) | async-done | bytes 131104 | tf_op jit(solution)/shard_map/all_to_all | solution.py:99
  23.8 1.3 %collective-permute-done = f32[32,1024]{1,0:T(8,128)S(1)} collective-permute-done((f32[32,1024]{1,0:T(8,128)S(1)}, f32[32,1024]{1,0:T(8,128)S(1)}, u32[]{:S(2)}, u32[]{:S(2)}) %collective-permute-start) | collective-permute-done | bytes 131104 | tf_op jit(solution)/shard_map/ppermute | solution.py:106
  25.1 1.7 %collective-permute-start.1 = (f32[64,1024]{1,0:T(8,128)S(1)}, f32[64,1024]{1,0:T(8,128)S(1)}, u32[]{:S(2)}, u32[]{:S(2)}) collective-permute-start(f32[64,1024]{1,0:T(8,128)S(1)} %get-tuple-element.24), channel_id=1, source_target_pairs={{0,2},{1,3},{2,4},{3,5},{4,6},{5,7},{6,0},{7,1},{8,10},{9,11},{10,... | collective-permute-start | bytes 786440 | tf_op jit(solution)/shard_map/ppermute | solution.py:110
  26.7 0.9 collective-permute-start.2
  27.7 2.7 %collective-permute-start.3 = (f32[64,1024]{1,0:T(8,128)S(1)}, f32[64,1024]{1,0:T(8,128)S(1)}, u32[]{:S(2)}, u32[]{:S(2)}) collective-permute-start(f32[64,1024]{1,0:T(8,128)S(1)} %get-tuple-element.24), channel_id=1, source_target_pairs={{0,6},{1,7},{2,0},{3,1},{4,2},{5,3},{6,4},{7,5},{8,14},{9,15},{10,... | collective-permute-start | bytes 786440 | tf_op jit(solution)/shard_map/ppermute | solution.py:110
  30.4 0.1 copy.22
  30.6 3.7 %collective-permute-done.1 = f32[64,1024]{1,0:T(8,128)S(1)} collective-permute-done((f32[64,1024]{1,0:T(8,128)S(1)}, f32[64,1024]{1,0:T(8,128)S(1)}, u32[]{:S(2)}, u32[]{:S(2)}) %collective-permute-start.1) | collective-permute-done | bytes 262176 | tf_op jit(solution)/shard_map/ppermute | solution.py:110
  34.4 3.1 %collective-permute-done.2 = f32[64,1024]{1,0:T(8,128)S(1)} collective-permute-done((f32[64,1024]{1,0:T(8,128)S(1)}, f32[64,1024]{1,0:T(8,128)S(1)}, u32[]{:S(2)}, u32[]{:S(2)}) %collective-permute-start.2) | collective-permute-done | bytes 262176 | tf_op jit(solution)/shard_map/ppermute | solution.py:110
  37.4 4.1 %collective-permute-done.3 = f32[64,1024]{1,0:T(8,128)S(1)} collective-permute-done((f32[64,1024]{1,0:T(8,128)S(1)}, f32[64,1024]{1,0:T(8,128)S(1)}, u32[]{:S(2)}, u32[]{:S(2)}) %collective-permute-start.3) | collective-permute-done | bytes 262176 | tf_op jit(solution)/shard_map/ppermute | solution.py:110
  41.6 0.6 gather_fusion
  42.2 0.2 multiply_reduce_fusion
  42.5 0.2 fusion.33
  42.7 5.0 %fusion.8 = f32[4,64,1280]{2,1,0:T(8,128)S(1)} fusion(f32[4,64,1024]{2,1,0:T(8,128)S(1)} %fusion.33, f32[1024,1280]{1,0:T(8,128)} %constant.139.clone), kind=kOutput, calls=%fused_computation.9 | convolution fusion | flops 2013265920 | bytes 7602176 | tf_op jit(solution)/shard_map/dot_general | solution.py:57
  47.7 1.1 %multiply_add_fusion.3 = (f32[4,64,640]{2,1,0:T(8,128)S(1)}, f32[4,64,640]{2,1,0:T(8,128)}, f32[4,640]{1,0:T(4,128)S(1)}) fusion(f32[4,64,1280]{2,1,0:T(8,128)S(1)} %fusion.8, f32[4,640]{1,0:T(4,128)S(1)} %get-tuple-element.33, f32[4,640]{1,0:T(4,128)S(1)} %get-tuple-element.32), kind=kLoop, calls=%fused_computation.50 | loop fusion | flops 1635840 | bytes 2652160 | tf_op jit(solution)/shard_map/add | solution.py:74
  48.8 0.1 reduce_max.9
  48.9 5.2 %multiply_add_fusion = f32[4,64,1024]{2,1,0:T(8,128)S(1)} fusion(f32[1024,1280]{1,0:T(8,128)} %constant.139.clone, f32[4,64,640]{2,1,0:T(8,128)} %get-tuple-element.19, f32[4,64,640]{2,1,0:T(8,128)S(1)} %get-tuple-element.18, f32[1280]{0:T(1024)S(1)} %copy-done.1, f32[4]{0:T(128)S(1)} %fusion.66, f32[4]{0:T(128)S(1)} %get-tuple-element.12, ...), kind=kOutput, calls=%fused_computation.12 | convolution fusion | flops 2015756288 | bytes 7607344 | tf_op jit(solution)/shard_map/dot_general | solution.py:61
  54.2 2.6 %fusion.4 = f32[4,64,1280]{2,1,0:T(8,128)S(1)} fusion(f32[4,64,1024]{2,1,0:T(8,128)S(1)} %multiply_add_fusion, f32[1024,1280]{1,0:T(8,128)S(1)} %bitcast.94), kind=kOutput, calls=%fused_computation.5 | convolution fusion | flops 2013265920 | bytes 7602176 | tf_op jit(solution)/shard_map/dot_general | solution.py:57
  56.8 0.3 subtract_reduce_fusion.1
  57.1 0.1 multiply_add_fusion.2
  57.3 2.4 %fusion.19 = f32[4,64,1024]{2,1,0:T(8,128)S(1)} fusion(f32[4,64,1024]{2,1,0:T(8,128)S(1)} %multiply_add_fusion, f32[1024,1280]{1,0:T(8,128)S(1)} %bitcast.94, f32[4,64,640]{2,1,0:T(8,128)S(1)} %get-tuple-element.17, f32[4,64,640]{2,1,0:T(8,128)S(1)} %get-tuple-element.16, f32[1280]{0:T(1024)S(1)} %copy-done.1, f32[4]{0:T(128)S(1)} %get-tuple-element.13), kind=kOutput, calls=%fused_computation.16 | convolution fusion | flops 2014445568 | bytes 8655888 | tf_op jit(solution)/shard_map/dot_general | solution.py:61
  59.6 2.8 %fusion = f32[4,64,1280]{2,1,0:T(8,128)S(1)} fusion(f32[1024,1280]{1,0:T(8,128)S(1)} %bitcast.94, f32[4,64,1024]{2,1,0:T(8,128)S(1)} %fusion.19, f32[4]{0:T(128)S(1)} %fusion.66, f32[4]{0:T(128)S(1)} %get-tuple-element.12), kind=kOutput, calls=%fused_computation.1 | convolution fusion | flops 2014052352 | bytes 7602208 | tf_op jit(solution)/shard_map/dot_general | solution.py:57
  62.5 0.3 subtract_reduce_fusion
  62.8 0.1 multiply_add_fusion.1
  63.0 0.1 pad_maximum_fusion
  63.1 1.4 %fusion.31 = f32[8,32,1280]{2,0,1:T(8,128)S(1)} fusion(f32[8,32,1280]{2,1,0:T(8,128)S(1)} %bitcast.96, s32[8]{0:T(128)S(1)} %eq.24), kind=kOutput, calls=%fused_computation.30 | convolution fusion | flops 31457344 | bytes 2621472 | tf_op jit(solution)/shard_map/bs,skx->bkx/dot_general | solution.py:155
  64.5 0.4 copy.25
  64.9 2.4 %fusion.22 = f32[260,1024]{1,0:T(8,128)S(1)} fusion(f32[1024,1280]{1,0:T(8,128)S(1)} %bitcast.94, f32[4,640]{1,0:T(4,128)S(1)} %get-tuple-element.7, f32[4,640]{1,0:T(4,128)S(1)} %get-tuple-element.6, f32[256,1280]{1,0:T(8,128)S(1)} %bitcast.97, f32[1280]{0:T(1024)S(1)} %copy-done.1), kind=kOutput, calls=%fused_computation.18 | convolution fusion | flops 2045721600 | bytes 7644160 | tf_op jit(solution)/shard_map/dot_general | solution.py:61
  67.4 0.1 slice.81
  67.7 1.8 %collective-permute-done.4 = f32[4,32,1024]{2,1,0:T(8,128)S(1)} collective-permute-done((f32[4,32,1024]{2,1,0:T(8,128)S(1)}, f32[4,32,1024]{2,1,0:T(8,128)S(1)}, u32[]{:S(2)}, u32[]{:S(2)}) %collective-permute-start.4) | collective-permute-done | bytes 524320 | tf_op jit(solution)/shard_map/ppermute | solution.py:163
  69.7 1.1 %collective-permute-start.5 = (f32[32,1024]{1,0:T(8,128)S(1)}, f32[32,1024]{1,0:T(8,128)S(1)}, u32[]{:S(2)}, u32[]{:S(2)}) collective-permute-start(f32[32,1024]{1,0:T(8,128)S(1)} %get-tuple-element.21), channel_id=1, source_target_pairs={{0,2},{1,3},{2,4},{3,5},{4,6},{5,7},{6,0},{7,1},{8,10},{9,11},{10,... | collective-permute-start | bytes 393224 | tf_op jit(solution)/shard_map/ppermute | solution.py:167
  70.7 1.6 %collective-permute-start.6 = (f32[32,1024]{1,0:T(8,128)S(1)}, f32[32,1024]{1,0:T(8,128)S(1)}, u32[]{:S(2)}, u32[]{:S(2)}) collective-permute-start(f32[32,1024]{1,0:T(8,128)S(1)} %get-tuple-element.23), channel_id=1, source_target_pairs={{0,4},{1,5},{2,6},{3,7},{4,0},{5,1},{6,2},{7,3},{8,12},{9,13},{10,... | collective-permute-start | bytes 393224 | tf_op jit(solution)/shard_map/ppermute | solution.py:167
  72.3 1.5 %collective-permute-start.7 = (f32[32,1024]{1,0:T(8,128)S(1)}, f32[32,1024]{1,0:T(8,128)S(1)}, u32[]{:S(2)}, u32[]{:S(2)}) collective-permute-start(f32[32,1024]{1,0:T(8,128)S(1)} %get-tuple-element.22), channel_id=1, source_target_pairs={{0,6},{1,7},{2,0},{3,1},{4,2},{5,3},{6,4},{7,5},{8,14},{9,15},{10,... | collective-permute-start | bytes 393224 | tf_op jit(solution)/shard_map/ppermute | solution.py:167
  73.9 2.2 %collective-permute-done.5 = f32[32,1024]{1,0:T(8,128)S(1)} collective-permute-done((f32[32,1024]{1,0:T(8,128)S(1)}, f32[32,1024]{1,0:T(8,128)S(1)}, u32[]{:S(2)}, u32[]{:S(2)}) %collective-permute-start.5) | collective-permute-done | bytes 131104 | tf_op jit(solution)/shard_map/ppermute | solution.py:167
  76.1 2.5 %collective-permute-done.6 = f32[32,1024]{1,0:T(8,128)S(1)} collective-permute-done((f32[32,1024]{1,0:T(8,128)S(1)}, f32[32,1024]{1,0:T(8,128)S(1)}, u32[]{:S(2)}, u32[]{:S(2)}) %collective-permute-start.6) | collective-permute-done | bytes 131104 | tf_op jit(solution)/shard_map/ppermute | solution.py:167
  78.6 1.5 %collective-permute-done.7 = f32[32,1024]{1,0:T(8,128)S(1)} collective-permute-done((f32[32,1024]{1,0:T(8,128)S(1)}, f32[32,1024]{1,0:T(8,128)S(1)}, u32[]{:S(2)}, u32[]{:S(2)}) %collective-permute-start.7) | collective-permute-done | bytes 131104 | tf_op jit(solution)/shard_map/ppermute | solution.py:167
  80.2 0.7 reshape.374
  80.9 4.3 %all-to-all-start.1 = ((f32[32,1,1024]{2,1,0:T(1,128)}), f32[32,1,1024]{2,1,0:T(1,128)S(1)}, u32[]{:S(2)}, u32[]{:S(2)}) async-start(f32[32,1,1024]{2,1,0:T(1,128)} %reshape.374), calls=%async_computation.1 | async-start | bytes 262144 | tf_op jit(solution)/shard_map/all_to_all | solution.py:169
  85.2 0.6 multiply_reduce_fusion.2
  86.5 0.6 slice.80
  87.1 8.3 %all-to-all-done.1 = f32[32,1,1024]{2,1,0:T(1,128)S(1)} async-done(((f32[32,1,1024]{2,1,0:T(1,128)}), f32[32,1,1024]{2,1,0:T(1,128)S(1)}, u32[]{:S(2)}, u32[]{:S(2)}) %all-to-all-start.1) | async-done | bytes 131104 | tf_op jit(solution)/shard_map/all_to_all | solution.py:169
  95.4 0.1 reduce_sum.97
  95.5 0.6 multiply_reduce_fusion.1
  96.9 0.6 fusion.49
  98.2 0.6 subtract_divide_fusion
  (44 shorter events, 1.1 us)
Async XLA Ops:
  0.6 13.6 %copy-start = (f32[4,1024]{1,0:T(4,128)S(1)}, f32[4,1024]{1,0:T(4,128)}, u32[]{:S(2)}) copy-start(f32[4,1024]{1,0:T(4,128)} %param.5) | copy-start | bytes 49156
  2.0 21.6 %all-to-all-start = ((f32[32,8,128]{2,1,0:T(8,128)}), f32[32,8,128]{2,1,0:T(8,128)S(1)}, u32[]{:S(2)}, u32[]{:S(2)}) async-start(f32[32,8,128]{2,1,0:T(8,128)} %broadcast_in_dim.47), calls=%async_computation | async-start | bytes 262144 | tf_op jit(solution)/shard_map/all_to_all | solution.py:99
  14.2 3.7 %copy-start.3 = (s32[4,2]{0,1:T(2,128)S(1)}, s32[4,2]{0,1:T(2,128)}, u32[]{:S(2)}) copy-start(s32[4,2]{0,1:T(2,128)} %param.6) | copy-start | bytes 100
  23.6 1.4 %collective-permute-start = (f32[32,1024]{1,0:T(8,128)S(1)}, f32[32,1024]{1,0:T(8,128)S(1)}, u32[]{:S(2)}, u32[]{:S(2)}) collective-permute-start(f32[32,1024]{1,0:T(8,128)S(1)} %bitcast.103), channel_id=1, source_target_pairs={{0,1},{1,0},{2,3},{3,2},{4,5},{5,4},{6,7},{7,6},{8,9},{9,8},{10,11... | collective-permute-start | bytes 393224 | tf_op jit(solution)/shard_map/ppermute | solution.py:106
  25.1 9.3 %collective-permute-start.1 = (f32[64,1024]{1,0:T(8,128)S(1)}, f32[64,1024]{1,0:T(8,128)S(1)}, u32[]{:S(2)}, u32[]{:S(2)}) collective-permute-start(f32[64,1024]{1,0:T(8,128)S(1)} %get-tuple-element.24), channel_id=1, source_target_pairs={{0,2},{1,3},{2,4},{3,5},{4,6},{5,7},{6,0},{7,1},{8,10},{9,11},{10,... | collective-permute-start | bytes 786440 | tf_op jit(solution)/shard_map/ppermute | solution.py:110
  26.7 10.7 %collective-permute-start.2 = (f32[64,1024]{1,0:T(8,128)S(1)}, f32[64,1024]{1,0:T(8,128)S(1)}, u32[]{:S(2)}, u32[]{:S(2)}) collective-permute-start(f32[64,1024]{1,0:T(8,128)S(1)} %get-tuple-element.24), channel_id=1, source_target_pairs={{0,4},{1,5},{2,6},{3,7},{4,0},{5,1},{6,2},{7,3},{8,12},{9,13},{10,... | collective-permute-start | bytes 786440 | tf_op jit(solution)/shard_map/ppermute | solution.py:110
  27.7 13.8 %collective-permute-start.3 = (f32[64,1024]{1,0:T(8,128)S(1)}, f32[64,1024]{1,0:T(8,128)S(1)}, u32[]{:S(2)}, u32[]{:S(2)}) collective-permute-start(f32[64,1024]{1,0:T(8,128)S(1)} %get-tuple-element.24), channel_id=1, source_target_pairs={{0,6},{1,7},{2,0},{3,1},{4,2},{5,3},{6,4},{7,5},{8,14},{9,15},{10,... | collective-permute-start | bytes 786440 | tf_op jit(solution)/shard_map/ppermute | solution.py:110
  47.7 1.2 %copy-start.1 = (f32[1280]{0:T(1024)S(1)}, f32[1280]{0:T(1024)}, u32[]{:S(2)}) copy-start(f32[1280]{0:T(1024)} %constant.140.clone) | copy-start | bytes 15364
  47.7 6.5 %slice-start = ((s8[5242880]{0:T(1024)(128)(4,1)}), s8[1048576]{0:T(1024)(128)(4,1)S(1)}, s32[]{:S(2)}) async-start(s8[5242880]{0:T(1024)(128)(4,1)} %bitcast.93), calls=%async_computation.2 | async-start | bytes 2097152
  48.9 5.3 %slice-start.1 = ((s8[5242880]{0:T(1024)(128)(4,1)}), s8[4194304]{0:T(1024)(128)(4,1)S(1)}, s32[]{:S(2)}) async-start(s8[5242880]{0:T(1024)(128)(4,1)} %bitcast.93), calls=%async_computation.3 | async-start | bytes 8388608
  67.5 2.0 %collective-permute-start.4 = (f32[4,32,1024]{2,1,0:T(8,128)S(1)}, f32[4,32,1024]{2,1,0:T(8,128)S(1)}, u32[]{:S(2)}, u32[]{:S(2)}) collective-permute-start(f32[4,32,1024]{2,1,0:T(8,128)S(1)} %dynamic-slice_bitcast_fusion), channel_id=1, source_target_pairs={{0,1},{1,0},{2,3},{3,2},{4,5},{5,4},{6,7},{7,6},{8,9},{9,8},{10,11... | collective-permute-start | bytes 1572872 | tf_op jit(solution)/shard_map/ppermute | solution.py:163
  69.6 15.6 %copy-start.2 = (f32[1,1,1024]{2,1,0:T(1,128)S(1)}, f32[1,1,1024]{2,1,0:T(1,128)}, u32[]{:S(2)}) copy-start(f32[1,1,1024]{2,1,0:T(1,128)} %param.7) | copy-start | bytes 12292
  69.7 6.4 %collective-permute-start.5 = (f32[32,1024]{1,0:T(8,128)S(1)}, f32[32,1024]{1,0:T(8,128)S(1)}, u32[]{:S(2)}, u32[]{:S(2)}) collective-permute-start(f32[32,1024]{1,0:T(8,128)S(1)} %get-tuple-element.21), channel_id=1, source_target_pairs={{0,2},{1,3},{2,4},{3,5},{4,6},{5,7},{6,0},{7,1},{8,10},{9,11},{10,... | collective-permute-start | bytes 393224 | tf_op jit(solution)/shard_map/ppermute | solution.py:167
  70.7 7.9 %collective-permute-start.6 = (f32[32,1024]{1,0:T(8,128)S(1)}, f32[32,1024]{1,0:T(8,128)S(1)}, u32[]{:S(2)}, u32[]{:S(2)}) collective-permute-start(f32[32,1024]{1,0:T(8,128)S(1)} %get-tuple-element.23), channel_id=1, source_target_pairs={{0,4},{1,5},{2,6},{3,7},{4,0},{5,1},{6,2},{7,3},{8,12},{9,13},{10,... | collective-permute-start | bytes 393224 | tf_op jit(solution)/shard_map/ppermute | solution.py:167
  72.3 7.8 %collective-permute-start.7 = (f32[32,1024]{1,0:T(8,128)S(1)}, f32[32,1024]{1,0:T(8,128)S(1)}, u32[]{:S(2)}, u32[]{:S(2)}) collective-permute-start(f32[32,1024]{1,0:T(8,128)S(1)} %get-tuple-element.22), channel_id=1, source_target_pairs={{0,6},{1,7},{2,0},{3,1},{4,2},{5,3},{6,4},{7,5},{8,14},{9,15},{10,... | collective-permute-start | bytes 393224 | tf_op jit(solution)/shard_map/ppermute | solution.py:167
  80.9 14.5 %all-to-all-start.1 = ((f32[32,1,1024]{2,1,0:T(1,128)}), f32[32,1,1024]{2,1,0:T(1,128)S(1)}, u32[]{:S(2)}, u32[]{:S(2)}) async-start(f32[32,1,1024]{2,1,0:T(1,128)} %reshape.374), calls=%async_computation.1 | async-start | bytes 262144 | tf_op jit(solution)/shard_map/all_to_all | solution.py:169

commit v8 on v7

--- a/solution.py
+++ b/solution.py
@@ -168,8 +168,13 @@
     arrived = arrived.reshape(tile_count, 1, pixels)
     atom_grad = jnp.sum(lax.all_to_all(arrived, "tile", 0, 0, tiled=True), axis=0)
 
-    scale = jnp.sqrt(jnp.mean(atom_grad * atom_grad, axis=-1, keepdims=True) + epsilon)
-    atoms = unit_rows(own - step_ratio * atom_grad / scale)
+    grad_square = jnp.mean(atom_grad * atom_grad, axis=-1, keepdims=True)
+    cross = jnp.mean(own * atom_grad, axis=-1, keepdims=True)
+    own_square = jnp.mean(own * own, axis=-1, keepdims=True)
+    scale = jnp.sqrt(grad_square + epsilon)
+    shift = step_ratio / scale
+    moved_square = own_square - 2.0 * shift * cross + shift * shift * grad_square
+    atoms = (own - shift * atom_grad) / jnp.sqrt(moved_square + epsilon)
     return (recon, atoms.reshape(dictionary.shape))
 
 

time: 99.1 us -> 99.3 us (level)
  between operations: 3.18 us -> 4.57 us
  waiting for transfers between devices: 34.1 us -> 32.8 us
    all_to_all x1, waiting for transfers between devices: 8.35 us -> 7.08 us  [on_device(): lax.all_to_all(arrived, 'tile', 0, 0, tiled=True)]
  transfers between devices with their start and end apart: 10 -> 10, of which waited for: 10 -> 10; matrix products, arithmetic and copies ran while one was open for 6% -> 7% of each run, Pallas kernels for 0% -> 0%
where the time goes in v8:
time: 99.3 us; the launch traced here: 98.9 us
  waiting for transfers between devices  32.8 us (33%)
  matrix products  25.6 us (26%)
  starting transfers between devices  25.2 us (25%)
  local copies, waits for them, and re-layouts  5.36 us (5%)
  other arithmetic  5.36 us (5%)
  between operations  4.57 us (5%)
    dot_general x4, matrix products, forward(): jnp.dot(values, table, precision=fast, preferred_element_type=jnp.float32)  14.1 us
    all_to_all x1, starting transfers between devices, on_device(): lax.all_to_all(jnp.broadcast_to(dense, (tile_count, 8, pixels // 8)), 'ti...  11.3 us
    ppermute x3, waiting for transfers between devices, on_device(): lax.ppermute(pair, 'atom', [(i, (i // 2 + hop) % chips * 2 + i % 2) for i...  10.8 us
    dot_general x3, matrix products, inverse(): lax.dot_general(spectra * weight, table, (((spectra.ndim - 1,), (1,)), ((...  10.1 us
    all_to_all x1, waiting for transfers between devices, on_device(): lax.all_to_all(arrived, 'tile', 0, 0, tiled=True)  7.08 us
    ppermute x3, waiting for transfers between devices, on_device(): lax.ppermute(sent, 'atom', [(i, (i // 2 + hop) % chips * 2 + i % 2) for i...  6.27 us
    all_to_all x1, waiting for transfers between devices, on_device(): lax.all_to_all(jnp.broadcast_to(dense, (tile_count, 8, pixels // 8)), 'ti...  5.53 us
    ppermute x3, starting transfers between devices, on_device(): lax.ppermute(pair, 'atom', [(i, (i // 2 + hop) % chips * 2 + i % 2) for i...  5.26 us
  transfers between devices with their start and end apart: 10, of which 10 were waited for; matrix products, arithmetic and copies ran while one was open for 7% of the time, Pallas kernels for 0%

profile of v8, /device:TPU:8, one launch (start us, length us, event | category | flops | bytes accessed | tf_op | source)
XLA Modules:
  0.0 98.9 jit_solution(10950633567865215624)
XLA Ops:
  0.6 1.3 %broadcast_in_dim.50 = f32[32,8,128]{2,1,0:T(8,128)} broadcast(f32[8,128]{1,0:T(8,128)} %bitcast.103), dimensions={1,2} | broadcast | bytes 135168 | tf_op jit(solution)/shard_map/broadcast_in_dim | solution.py:99
  2.0 11.3 %all-to-all-start = ((f32[32,8,128]{2,1,0:T(8,128)}), f32[32,8,128]{2,1,0:T(8,128)S(1)}, u32[]{:S(2)}, u32[]{:S(2)}) async-start(f32[32,8,128]{2,1,0:T(8,128)} %broadcast_in_dim.50), calls=%async_computation | async-start | bytes 262144 | tf_op jit(solution)/shard_map/all_to_all | solution.py:99
  13.3 0.8 copy.21
  14.2 3.7 %convolution_bitcast_fusion = f32[4,1280]{1,0:T(4,128)S(1)} fusion(f32[1024,1280]{1,0:T(8,128)} %constant.145.clone, f32[4,1024]{1,0:T(4,128)S(1)} %copy-done), kind=kOutput, calls=%fused_computation.11 | convolution fusion | flops 31457280 | bytes 5279744 | tf_op jit(solution)/shard_map/dot_general | solution.py:57
  18.0 5.5 %all-to-all-done = f32[32,8,128]{2,1,0:T(8,128)S(1)} async-done(((f32[32,8,128]{2,1,0:T(8,128)}), f32[32,8,128]{2,1,0:T(8,128)S(1)}, u32[]{:S(2)}, u32[]{:S(2)}) %all-to-all-start) | async-done | bytes 131104 | tf_op jit(solution)/shard_map/all_to_all | solution.py:99
  23.7 1.3 %collective-permute-done = f32[32,1024]{1,0:T(8,128)S(1)} collective-permute-done((f32[32,1024]{1,0:T(8,128)S(1)}, f32[32,1024]{1,0:T(8,128)S(1)}, u32[]{:S(2)}, u32[]{:S(2)}) %collective-permute-start) | collective-permute-done | bytes 131104 | tf_op jit(solution)/shard_map/ppermute | solution.py:106
  25.1 1.7 %collective-permute-start.1 = (f32[64,1024]{1,0:T(8,128)S(1)}, f32[64,1024]{1,0:T(8,128)S(1)}, u32[]{:S(2)}, u32[]{:S(2)}) collective-permute-start(f32[64,1024]{1,0:T(8,128)S(1)} %get-tuple-element.26), channel_id=1, source_target_pairs={{0,2},{1,3},{2,4},{3,5},{4,6},{5,7},{6,0},{7,1},{8,10},{9,11},{10,... | collective-permute-start | bytes 786440 | tf_op jit(solution)/shard_map/ppermute | solution.py:110
  26.7 0.9 collective-permute-start.2
  27.7 2.7 %collective-permute-start.3 = (f32[64,1024]{1,0:T(8,128)S(1)}, f32[64,1024]{1,0:T(8,128)S(1)}, u32[]{:S(2)}, u32[]{:S(2)}) collective-permute-start(f32[64,1024]{1,0:T(8,128)S(1)} %get-tuple-element.26), channel_id=1, source_target_pairs={{0,6},{1,7},{2,0},{3,1},{4,2},{5,3},{6,4},{7,5},{8,14},{9,15},{10,... | collective-permute-start | bytes 786440 | tf_op jit(solution)/shard_map/ppermute | solution.py:110
  30.4 0.1 copy.22
  30.6 3.7 %collective-permute-done.1 = f32[64,1024]{1,0:T(8,128)S(1)} collective-permute-done((f32[64,1024]{1,0:T(8,128)S(1)}, f32[64,1024]{1,0:T(8,128)S(1)}, u32[]{:S(2)}, u32[]{:S(2)}) %collective-permute-start.1) | collective-permute-done | bytes 262176 | tf_op jit(solution)/shard_map/ppermute | solution.py:110
  34.3 3.1 %collective-permute-done.2 = f32[64,1024]{1,0:T(8,128)S(1)} collective-permute-done((f32[64,1024]{1,0:T(8,128)S(1)}, f32[64,1024]{1,0:T(8,128)S(1)}, u32[]{:S(2)}, u32[]{:S(2)}) %collective-permute-start.2) | collective-permute-done | bytes 262176 | tf_op jit(solution)/shard_map/ppermute | solution.py:110
  37.4 4.1 %collective-permute-done.3 = f32[64,1024]{1,0:T(8,128)S(1)} collective-permute-done((f32[64,1024]{1,0:T(8,128)S(1)}, f32[64,1024]{1,0:T(8,128)S(1)}, u32[]{:S(2)}, u32[]{:S(2)}) %collective-permute-start.3) | collective-permute-done | bytes 262176 | tf_op jit(solution)/shard_map/ppermute | solution.py:110
  41.5 0.6 gather_fusion
  42.2 0.2 multiply_reduce_fusion
  42.5 0.2 fusion.33
  42.7 5.0 %fusion.8 = f32[4,64,1280]{2,1,0:T(8,128)S(1)} fusion(f32[4,64,1024]{2,1,0:T(8,128)S(1)} %fusion.33, f32[1024,1280]{1,0:T(8,128)} %constant.145.clone), kind=kOutput, calls=%fused_computation.9 | convolution fusion | flops 2013265920 | bytes 7602176 | tf_op jit(solution)/shard_map/dot_general | solution.py:57
  47.7 1.1 %multiply_add_fusion.3 = (f32[4,64,640]{2,1,0:T(8,128)S(1)}, f32[4,64,640]{2,1,0:T(8,128)}, f32[4,640]{1,0:T(4,128)S(1)}) fusion(f32[4,64,1280]{2,1,0:T(8,128)S(1)} %fusion.8, f32[4,640]{1,0:T(4,128)S(1)} %get-tuple-element.35, f32[4,640]{1,0:T(4,128)S(1)} %get-tuple-element.34), kind=kLoop, calls=%fused_computation.50 | loop fusion | flops 1635840 | bytes 2652160 | tf_op jit(solution)/shard_map/add | solution.py:74
  48.7 0.1 reduce_max.9
  48.9 5.2 %multiply_add_fusion = f32[4,64,1024]{2,1,0:T(8,128)S(1)} fusion(f32[1024,1280]{1,0:T(8,128)} %constant.145.clone, f32[4,64,640]{2,1,0:T(8,128)} %get-tuple-element.21, f32[4,64,640]{2,1,0:T(8,128)S(1)} %get-tuple-element.20, f32[1280]{0:T(1024)S(1)} %copy-done.1, f32[4]{0:T(128)S(1)} %fusion.64, f32[4]{0:T(128)S(1)} %get-tuple-element.14, ...), kind=kOutput, calls=%fused_computation.12 | convolution fusion | flops 2015756288 | bytes 7607344 | tf_op jit(solution)/shard_map/dot_general | solution.py:61
  54.2 2.6 %fusion.4 = f32[4,64,1280]{2,1,0:T(8,128)S(1)} fusion(f32[4,64,1024]{2,1,0:T(8,128)S(1)} %multiply_add_fusion, f32[1024,1280]{1,0:T(8,128)S(1)} %bitcast.93), kind=kOutput, calls=%fused_computation.5 | convolution fusion | flops 2013265920 | bytes 7602176 | tf_op jit(solution)/shard_map/dot_general | solution.py:57
  56.8 0.3 subtract_reduce_fusion.1
  57.1 0.1 multiply_add_fusion.2
  57.2 2.4 %fusion.19 = f32[4,64,1024]{2,1,0:T(8,128)S(1)} fusion(f32[4,64,1024]{2,1,0:T(8,128)S(1)} %multiply_add_fusion, f32[1024,1280]{1,0:T(8,128)S(1)} %bitcast.93, f32[4,64,640]{2,1,0:T(8,128)S(1)} %get-tuple-element.19, f32[4,64,640]{2,1,0:T(8,128)S(1)} %get-tuple-element.18, f32[1280]{0:T(1024)S(1)} %copy-done.1, f32[4]{0:T(128)S(1)} %get-tuple-element.15), kind=kOutput, calls=%fused_computation.16 | convolution fusion | flops 2014445568 | bytes 8655888 | tf_op jit(solution)/shard_map/dot_general | solution.py:61
  59.6 2.8 %fusion = f32[4,64,1280]{2,1,0:T(8,128)S(1)} fusion(f32[1024,1280]{1,0:T(8,128)S(1)} %bitcast.93, f32[4,64,1024]{2,1,0:T(8,128)S(1)} %fusion.19, f32[4]{0:T(128)S(1)} %fusion.64, f32[4]{0:T(128)S(1)} %get-tuple-element.14), kind=kOutput, calls=%fused_computation.1 | convolution fusion | flops 2014052352 | bytes 7602208 | tf_op jit(solution)/shard_map/dot_general | solution.py:57
  62.5 0.3 subtract_reduce_fusion
  62.8 0.1 multiply_add_fusion.1
  62.9 0.1 pad_maximum_fusion
  63.0 1.4 %fusion.31 = f32[8,32,1280]{2,0,1:T(8,128)S(1)} fusion(f32[8,32,1280]{2,1,0:T(8,128)S(1)} %bitcast.95, s32[8]{0:T(128)S(1)} %eq.24), kind=kOutput, calls=%fused_computation.30 | convolution fusion | flops 31457344 | bytes 2621472 | tf_op jit(solution)/shard_map/bs,skx->bkx/dot_general | solution.py:155
  64.5 0.4 copy.25
  64.9 2.4 %fusion.22 = f32[260,1024]{1,0:T(8,128)S(1)} fusion(f32[1024,1280]{1,0:T(8,128)S(1)} %bitcast.93, f32[4,640]{1,0:T(4,128)S(1)} %get-tuple-element.7, f32[4,640]{1,0:T(4,128)S(1)} %get-tuple-element.6, f32[256,1280]{1,0:T(8,128)S(1)} %bitcast.96, f32[1280]{0:T(1024)S(1)} %copy-done.1), kind=kOutput, calls=%fused_computation.18 | convolution fusion | flops 2045721600 | bytes 7644160 | tf_op jit(solution)/shard_map/dot_general | solution.py:61
  67.3 0.1 slice.81
  67.7 1.8 %collective-permute-done.4 = f32[4,32,1024]{2,1,0:T(8,128)S(1)} collective-permute-done((f32[4,32,1024]{2,1,0:T(8,128)S(1)}, f32[4,32,1024]{2,1,0:T(8,128)S(1)}, u32[]{:S(2)}, u32[]{:S(2)}) %collective-permute-start.4) | collective-permute-done | bytes 524320 | tf_op jit(solution)/shard_map/ppermute | solution.py:163
  69.6 1.1 %collective-permute-start.5 = (f32[32,1024]{1,0:T(8,128)S(1)}, f32[32,1024]{1,0:T(8,128)S(1)}, u32[]{:S(2)}, u32[]{:S(2)}) collective-permute-start(f32[32,1024]{1,0:T(8,128)S(1)} %get-tuple-element.23), channel_id=1, source_target_pairs={{0,2},{1,3},{2,4},{3,5},{4,6},{5,7},{6,0},{7,1},{8,10},{9,11},{10,... | collective-permute-start | bytes 393224 | tf_op jit(solution)/shard_map/ppermute | solution.py:167
  70.7 1.6 %collective-permute-start.6 = (f32[32,1024]{1,0:T(8,128)S(1)}, f32[32,1024]{1,0:T(8,128)S(1)}, u32[]{:S(2)}, u32[]{:S(2)}) collective-permute-start(f32[32,1024]{1,0:T(8,128)S(1)} %get-tuple-element.25), channel_id=1, source_target_pairs={{0,4},{1,5},{2,6},{3,7},{4,0},{5,1},{6,2},{7,3},{8,12},{9,13},{10,... | collective-permute-start | bytes 393224 | tf_op jit(solution)/shard_map/ppermute | solution.py:167
  72.3 1.5 %collective-permute-start.7 = (f32[32,1024]{1,0:T(8,128)S(1)}, f32[32,1024]{1,0:T(8,128)S(1)}, u32[]{:S(2)}, u32[]{:S(2)}) collective-permute-start(f32[32,1024]{1,0:T(8,128)S(1)} %get-tuple-element.24), channel_id=1, source_target_pairs={{0,6},{1,7},{2,0},{3,1},{4,2},{5,3},{6,4},{7,5},{8,14},{9,15},{10,... | collective-permute-start | bytes 393224 | tf_op jit(solution)/shard_map/ppermute | solution.py:167
  73.8 2.2 %collective-permute-done.5 = f32[32,1024]{1,0:T(8,128)S(1)} collective-permute-done((f32[32,1024]{1,0:T(8,128)S(1)}, f32[32,1024]{1,0:T(8,128)S(1)}, u32[]{:S(2)}, u32[]{:S(2)}) %collective-permute-start.5) | collective-permute-done | bytes 131104 | tf_op jit(solution)/shard_map/ppermute | solution.py:167
  76.1 2.5 %collective-permute-done.6 = f32[32,1024]{1,0:T(8,128)S(1)} collective-permute-done((f32[32,1024]{1,0:T(8,128)S(1)}, f32[32,1024]{1,0:T(8,128)S(1)}, u32[]{:S(2)}, u32[]{:S(2)}) %collective-permute-start.6) | collective-permute-done | bytes 131104 | tf_op jit(solution)/shard_map/ppermute | solution.py:167
  78.6 1.5 %collective-permute-done.7 = f32[32,1024]{1,0:T(8,128)S(1)} collective-permute-done((f32[32,1024]{1,0:T(8,128)S(1)}, f32[32,1024]{1,0:T(8,128)S(1)}, u32[]{:S(2)}, u32[]{:S(2)}) %collective-permute-start.7) | collective-permute-done | bytes 131104 | tf_op jit(solution)/shard_map/ppermute | solution.py:167
  80.1 0.7 reshape.356
  80.9 4.3 %all-to-all-start.1 = ((f32[32,1,1024]{2,1,0:T(1,128)}), f32[32,1,1024]{2,1,0:T(1,128)S(1)}, u32[]{:S(2)}, u32[]{:S(2)}) async-start(f32[32,1,1024]{2,1,0:T(1,128)} %reshape.356), calls=%async_computation.1 | async-start | bytes 262144 | tf_op jit(solution)/shard_map/all_to_all | solution.py:169
  85.1 0.6 multiply_reduce_fusion.4
  86.4 0.6 multiply_reduce_fusion.2
  87.7 0.6 slice.80
  88.3 7.1 %all-to-all-done.1 = f32[32,1,1024]{2,1,0:T(1,128)S(1)} async-done(((f32[32,1,1024]{2,1,0:T(1,128)}), f32[32,1,1024]{2,1,0:T(1,128)S(1)}, u32[]{:S(2)}, u32[]{:S(2)}) %all-to-all-start.1) | async-done | bytes 131104 | tf_op jit(solution)/shard_map/all_to_all | solution.py:169
  95.4 0.1 reduce_sum.106
  95.5 0.7 multiply_reduce_fusion.1
  98.3 0.6 subtract_divide_fusion
  (44 shorter events, 1.1 us)
Async XLA Ops:
  0.6 13.5 %copy-start = (f32[4,1024]{1,0:T(4,128)S(1)}, f32[4,1024]{1,0:T(4,128)}, u32[]{:S(2)}) copy-start(f32[4,1024]{1,0:T(4,128)} %param.5) | copy-start | bytes 49156
  2.0 21.6 %all-to-all-start = ((f32[32,8,128]{2,1,0:T(8,128)}), f32[32,8,128]{2,1,0:T(8,128)S(1)}, u32[]{:S(2)}, u32[]{:S(2)}) async-start(f32[32,8,128]{2,1,0:T(8,128)} %broadcast_in_dim.50), calls=%async_computation | async-start | bytes 262144 | tf_op jit(solution)/shard_map/all_to_all | solution.py:99
  14.2 3.7 %copy-start.3 = (s32[4,2]{0,1:T(2,128)S(1)}, s32[4,2]{0,1:T(2,128)}, u32[]{:S(2)}) copy-start(s32[4,2]{0,1:T(2,128)} %param.6) | copy-start | bytes 100
  23.6 1.4 %collective-permute-start = (f32[32,1024]{1,0:T(8,128)S(1)}, f32[32,1024]{1,0:T(8,128)S(1)}, u32[]{:S(2)}, u32[]{:S(2)}) collective-permute-start(f32[32,1024]{1,0:T(8,128)S(1)} %bitcast.102), channel_id=1, source_target_pairs={{0,1},{1,0},{2,3},{3,2},{4,5},{5,4},{6,7},{7,6},{8,9},{9,8},{10,11... | collective-permute-start | bytes 393224 | tf_op jit(solution)/shard_map/ppermute | solution.py:106
  25.1 9.3 %collective-permute-start.1 = (f32[64,1024]{1,0:T(8,128)S(1)}, f32[64,1024]{1,0:T(8,128)S(1)}, u32[]{:S(2)}, u32[]{:S(2)}) collective-permute-start(f32[64,1024]{1,0:T(8,128)S(1)} %get-tuple-element.26), channel_id=1, source_target_pairs={{0,2},{1,3},{2,4},{3,5},{4,6},{5,7},{6,0},{7,1},{8,10},{9,11},{10,... | collective-permute-start | bytes 786440 | tf_op jit(solution)/shard_map/ppermute | solution.py:110
  26.7 10.7 %collective-permute-start.2 = (f32[64,1024]{1,0:T(8,128)S(1)}, f32[64,1024]{1,0:T(8,128)S(1)}, u32[]{:S(2)}, u32[]{:S(2)}) collective-permute-start(f32[64,1024]{1,0:T(8,128)S(1)} %get-tuple-element.26), channel_id=1, source_target_pairs={{0,4},{1,5},{2,6},{3,7},{4,0},{5,1},{6,2},{7,3},{8,12},{9,13},{10,... | collective-permute-start | bytes 786440 | tf_op jit(solution)/shard_map/ppermute | solution.py:110
  27.7 13.8 %collective-permute-start.3 = (f32[64,1024]{1,0:T(8,128)S(1)}, f32[64,1024]{1,0:T(8,128)S(1)}, u32[]{:S(2)}, u32[]{:S(2)}) collective-permute-start(f32[64,1024]{1,0:T(8,128)S(1)} %get-tuple-element.26), channel_id=1, source_target_pairs={{0,6},{1,7},{2,0},{3,1},{4,2},{5,3},{6,4},{7,5},{8,14},{9,15},{10,... | collective-permute-start | bytes 786440 | tf_op jit(solution)/shard_map/ppermute | solution.py:110
  47.7 1.2 %copy-start.1 = (f32[1280]{0:T(1024)S(1)}, f32[1280]{0:T(1024)}, u32[]{:S(2)}) copy-start(f32[1280]{0:T(1024)} %constant.146.clone) | copy-start | bytes 15364
  47.7 6.5 %slice-start = ((s8[5242880]{0:T(1024)(128)(4,1)}), s8[1048576]{0:T(1024)(128)(4,1)S(1)}, s32[]{:S(2)}) async-start(s8[5242880]{0:T(1024)(128)(4,1)} %bitcast.92), calls=%async_computation.2 | async-start | bytes 2097152
  48.9 5.3 %slice-start.1 = ((s8[5242880]{0:T(1024)(128)(4,1)}), s8[4194304]{0:T(1024)(128)(4,1)S(1)}, s32[]{:S(2)}) async-start(s8[5242880]{0:T(1024)(128)(4,1)} %bitcast.92), calls=%async_computation.3 | async-start | bytes 8388608
  67.5 2.0 %collective-permute-start.4 = (f32[4,32,1024]{2,1,0:T(8,128)S(1)}, f32[4,32,1024]{2,1,0:T(8,128)S(1)}, u32[]{:S(2)}, u32[]{:S(2)}) collective-permute-start(f32[4,32,1024]{2,1,0:T(8,128)S(1)} %dynamic-slice_bitcast_fusion), channel_id=1, source_target_pairs={{0,1},{1,0},{2,3},{3,2},{4,5},{5,4},{6,7},{7,6},{8,9},{9,8},{10,11... | collective-permute-start | bytes 1572872 | tf_op jit(solution)/shard_map/ppermute | solution.py:163
  69.6 15.6 %copy-start.2 = (f32[1,1,1024]{2,1,0:T(1,128)S(1)}, f32[1,1,1024]{2,1,0:T(1,128)}, u32[]{:S(2)}) copy-start(f32[1,1,1024]{2,1,0:T(1,128)} %param.7) | copy-start | bytes 12292
  69.6 6.4 %collective-permute-start.5 = (f32[32,1024]{1,0:T(8,128)S(1)}, f32[32,1024]{1,0:T(8,128)S(1)}, u32[]{:S(2)}, u32[]{:S(2)}) collective-permute-start(f32[32,1024]{1,0:T(8,128)S(1)} %get-tuple-element.23), channel_id=1, source_target_pairs={{0,2},{1,3},{2,4},{3,5},{4,6},{5,7},{6,0},{7,1},{8,10},{9,11},{10,... | collective-permute-start | bytes 393224 | tf_op jit(solution)/shard_map/ppermute | solution.py:167
  70.7 7.9 %collective-permute-start.6 = (f32[32,1024]{1,0:T(8,128)S(1)}, f32[32,1024]{1,0:T(8,128)S(1)}, u32[]{:S(2)}, u32[]{:S(2)}) collective-permute-start(f32[32,1024]{1,0:T(8,128)S(1)} %get-tuple-element.25), channel_id=1, source_target_pairs={{0,4},{1,5},{2,6},{3,7},{4,0},{5,1},{6,2},{7,3},{8,12},{9,13},{10,... | collective-permute-start | bytes 393224 | tf_op jit(solution)/shard_map/ppermute | solution.py:167
  72.3 7.8 %collective-permute-start.7 = (f32[32,1024]{1,0:T(8,128)S(1)}, f32[32,1024]{1,0:T(8,128)S(1)}, u32[]{:S(2)}, u32[]{:S(2)}) collective-permute-start(f32[32,1024]{1,0:T(8,128)S(1)} %get-tuple-element.24), channel_id=1, source_target_pairs={{0,6},{1,7},{2,0},{3,1},{4,2},{5,3},{6,4},{7,5},{8,14},{9,15},{10,... | collective-permute-start | bytes 393224 | tf_op jit(solution)/shard_map/ppermute | solution.py:167
  80.9 14.5 %all-to-all-start.1 = ((f32[32,1,1024]{2,1,0:T(1,128)}), f32[32,1,1024]{2,1,0:T(1,128)S(1)}, u32[]{:S(2)}, u32[]{:S(2)}) async-start(f32[32,1,1024]{2,1,0:T(1,128)} %reshape.356), calls=%async_computation.1 | async-start | bytes 262144 | tf_op jit(solution)/shard_map/all_to_all | solution.py:169

commit v9 on v7

--- a/solution.py
+++ b/solution.py
@@ -152,7 +152,7 @@
     residual_spec = recon_spec - image_spec
     slot_terms = conj_times(code_spec, residual_spec[:, None, :]).reshape(slot_count, BLK, width)
     member = (jnp.arange(NBLK, dtype=jnp.int32)[:, None] == flat_ids[None, :]).astype(jnp.float32)
-    block_spec = jnp.einsum("bs,skx->bkx", member, slot_terms, precision=highest, preferred_element_type=jnp.float32)
+    block_spec = jnp.einsum("bs,skx->bkx", member, slot_terms, precision=fast, preferred_element_type=jnp.float32)
     both = inverse(jnp.concatenate([block_spec.reshape(NBLK * BLK, width), recon_spec], axis=0), table, weight)
     partial = both[:NBLK * BLK].reshape(NBLK, BLK, pixels)
     recon = both[NBLK * BLK:]

time: 99.1 us -> 98.8 us (level)
  no operation moved by 1% of the time
where the time goes in v9:
time: 98.8 us; the launch traced here: 98.4 us
  waiting for transfers between devices  34.1 us (35%)
  starting transfers between devices  25.2 us (26%)
  matrix products  25.2 us (26%)
  local copies, waits for them, and re-layouts  5.39 us (5%)
  other arithmetic  5.29 us (5%)
  between operations  3.18 us (3%)
    dot_general x4, matrix products, forward(): jnp.dot(values, table, precision=fast, preferred_element_type=jnp.float32)  14.1 us
    all_to_all x1, starting transfers between devices, on_device(): lax.all_to_all(jnp.broadcast_to(dense, (tile_count, 8, pixels // 8)), 'ti...  11.3 us
    ppermute x3, waiting for transfers between devices, on_device(): lax.ppermute(pair, 'atom', [(i, (i // 2 + hop) % chips * 2 + i % 2) for i...  10.8 us
    dot_general x3, matrix products, inverse(): lax.dot_general(spectra * weight, table, (((spectra.ndim - 1,), (1,)), ((...  10 us
    all_to_all x1, waiting for transfers between devices, on_device(): lax.all_to_all(arrived, 'tile', 0, 0, tiled=True)  8.35 us
    ppermute x3, waiting for transfers between devices, on_device(): lax.ppermute(sent, 'atom', [(i, (i // 2 + hop) % chips * 2 + i % 2) for i...  6.26 us
    all_to_all x1, waiting for transfers between devices, on_device(): lax.all_to_all(jnp.broadcast_to(dense, (tile_count, 8, pixels // 8)), 'ti...  5.53 us
    ppermute x3, starting transfers between devices, on_device(): lax.ppermute(pair, 'atom', [(i, (i // 2 + hop) % chips * 2 + i % 2) for i...  5.26 us
  transfers between devices with their start and end apart: 10, of which 10 were waited for; matrix products, arithmetic and copies ran while one was open for 6% of the time, Pallas kernels for 0%

profile of v9, /device:TPU:8, one launch (start us, length us, event | category | flops | bytes accessed | tf_op | source)
XLA Modules:
  0.0 98.4 jit_solution(11978990018639920602)
XLA Ops:
  0.6 1.4 %broadcast_in_dim.47 = f32[32,8,128]{2,1,0:T(8,128)} broadcast(f32[8,128]{1,0:T(8,128)} %bitcast.104), dimensions={1,2} | broadcast | bytes 135168 | tf_op jit(solution)/shard_map/broadcast_in_dim | solution.py:99
  2.0 11.3 %all-to-all-start = ((f32[32,8,128]{2,1,0:T(8,128)}), f32[32,8,128]{2,1,0:T(8,128)S(1)}, u32[]{:S(2)}, u32[]{:S(2)}) async-start(f32[32,8,128]{2,1,0:T(8,128)} %broadcast_in_dim.47), calls=%async_computation | async-start | bytes 262144 | tf_op jit(solution)/shard_map/all_to_all | solution.py:99
  13.3 0.8 copy.21
  14.2 3.7 %convolution_bitcast_fusion = f32[4,1280]{1,0:T(4,128)S(1)} fusion(f32[1024,1280]{1,0:T(8,128)} %constant.139.clone, f32[4,1024]{1,0:T(4,128)S(1)} %copy-done), kind=kOutput, calls=%fused_computation.11 | convolution fusion | flops 31457280 | bytes 5279744 | tf_op jit(solution)/shard_map/dot_general | solution.py:57
  18.1 5.5 %all-to-all-done = f32[32,8,128]{2,1,0:T(8,128)S(1)} async-done(((f32[32,8,128]{2,1,0:T(8,128)}), f32[32,8,128]{2,1,0:T(8,128)S(1)}, u32[]{:S(2)}, u32[]{:S(2)}) %all-to-all-start) | async-done | bytes 131104 | tf_op jit(solution)/shard_map/all_to_all | solution.py:99
  23.8 1.3 %collective-permute-done = f32[32,1024]{1,0:T(8,128)S(1)} collective-permute-done((f32[32,1024]{1,0:T(8,128)S(1)}, f32[32,1024]{1,0:T(8,128)S(1)}, u32[]{:S(2)}, u32[]{:S(2)}) %collective-permute-start) | collective-permute-done | bytes 131104 | tf_op jit(solution)/shard_map/ppermute | solution.py:106
  25.1 1.7 %collective-permute-start.1 = (f32[64,1024]{1,0:T(8,128)S(1)}, f32[64,1024]{1,0:T(8,128)S(1)}, u32[]{:S(2)}, u32[]{:S(2)}) collective-permute-start(f32[64,1024]{1,0:T(8,128)S(1)} %get-tuple-element.24), channel_id=1, source_target_pairs={{0,2},{1,3},{2,4},{3,5},{4,6},{5,7},{6,0},{7,1},{8,10},{9,11},{10,... | collective-permute-start | bytes 786440 | tf_op jit(solution)/shard_map/ppermute | solution.py:110
  26.7 0.9 collective-permute-start.2
  27.7 2.7 %collective-permute-start.3 = (f32[64,1024]{1,0:T(8,128)S(1)}, f32[64,1024]{1,0:T(8,128)S(1)}, u32[]{:S(2)}, u32[]{:S(2)}) collective-permute-start(f32[64,1024]{1,0:T(8,128)S(1)} %get-tuple-element.24), channel_id=1, source_target_pairs={{0,6},{1,7},{2,0},{3,1},{4,2},{5,3},{6,4},{7,5},{8,14},{9,15},{10,... | collective-permute-start | bytes 786440 | tf_op jit(solution)/shard_map/ppermute | solution.py:110
  30.4 0.1 copy.22
  30.6 3.7 %collective-permute-done.1 = f32[64,1024]{1,0:T(8,128)S(1)} collective-permute-done((f32[64,1024]{1,0:T(8,128)S(1)}, f32[64,1024]{1,0:T(8,128)S(1)}, u32[]{:S(2)}, u32[]{:S(2)}) %collective-permute-start.1) | collective-permute-done | bytes 262176 | tf_op jit(solution)/shard_map/ppermute | solution.py:110
  34.4 3.1 %collective-permute-done.2 = f32[64,1024]{1,0:T(8,128)S(1)} collective-permute-done((f32[64,1024]{1,0:T(8,128)S(1)}, f32[64,1024]{1,0:T(8,128)S(1)}, u32[]{:S(2)}, u32[]{:S(2)}) %collective-permute-start.2) | collective-permute-done | bytes 262176 | tf_op jit(solution)/shard_map/ppermute | solution.py:110
  37.4 4.1 %collective-permute-done.3 = f32[64,1024]{1,0:T(8,128)S(1)} collective-permute-done((f32[64,1024]{1,0:T(8,128)S(1)}, f32[64,1024]{1,0:T(8,128)S(1)}, u32[]{:S(2)}, u32[]{:S(2)}) %collective-permute-start.3) | collective-permute-done | bytes 262176 | tf_op jit(solution)/shard_map/ppermute | solution.py:110
  41.6 0.6 gather_fusion
  42.2 0.2 multiply_reduce_fusion
  42.5 0.2 fusion.33
  42.7 5.0 %fusion.8 = f32[4,64,1280]{2,1,0:T(8,128)S(1)} fusion(f32[4,64,1024]{2,1,0:T(8,128)S(1)} %fusion.33, f32[1024,1280]{1,0:T(8,128)} %constant.139.clone), kind=kOutput, calls=%fused_computation.9 | convolution fusion | flops 2013265920 | bytes 7602176 | tf_op jit(solution)/shard_map/dot_general | solution.py:57
  47.7 1.1 %multiply_add_fusion.3 = (f32[4,64,640]{2,1,0:T(8,128)S(1)}, f32[4,64,640]{2,1,0:T(8,128)}, f32[4,640]{1,0:T(4,128)S(1)}) fusion(f32[4,64,1280]{2,1,0:T(8,128)S(1)} %fusion.8, f32[4,640]{1,0:T(4,128)S(1)} %get-tuple-element.33, f32[4,640]{1,0:T(4,128)S(1)} %get-tuple-element.32), kind=kLoop, calls=%fused_computation.50 | loop fusion | flops 1635840 | bytes 2652160 | tf_op jit(solution)/shard_map/add | solution.py:74
  48.8 0.1 reduce_max.9
  48.9 5.2 %multiply_add_fusion = f32[4,64,1024]{2,1,0:T(8,128)S(1)} fusion(f32[1024,1280]{1,0:T(8,128)} %constant.139.clone, f32[4,64,640]{2,1,0:T(8,128)} %get-tuple-element.19, f32[4,64,640]{2,1,0:T(8,128)S(1)} %get-tuple-element.18, f32[1280]{0:T(1024)S(1)} %copy-done.1, f32[4]{0:T(128)S(1)} %fusion.66, f32[4]{0:T(128)S(1)} %get-tuple-element.12, ...), kind=kOutput, calls=%fused_computation.12 | convolution fusion | flops 2015756288 | bytes 7607344 | tf_op jit(solution)/shard_map/dot_general | solution.py:61
  54.2 2.6 %fusion.4 = f32[4,64,1280]{2,1,0:T(8,128)S(1)} fusion(f32[4,64,1024]{2,1,0:T(8,128)S(1)} %multiply_add_fusion, f32[1024,1280]{1,0:T(8,128)S(1)} %bitcast.94), kind=kOutput, calls=%fused_computation.5 | convolution fusion | flops 2013265920 | bytes 7602176 | tf_op jit(solution)/shard_map/dot_general | solution.py:57
  56.8 0.3 subtract_reduce_fusion.1
  57.1 0.1 multiply_add_fusion.2
  57.3 2.4 %fusion.19 = f32[4,64,1024]{2,1,0:T(8,128)S(1)} fusion(f32[4,64,1024]{2,1,0:T(8,128)S(1)} %multiply_add_fusion, f32[1024,1280]{1,0:T(8,128)S(1)} %bitcast.94, f32[4,64,640]{2,1,0:T(8,128)S(1)} %get-tuple-element.17, f32[4,64,640]{2,1,0:T(8,128)S(1)} %get-tuple-element.16, f32[1280]{0:T(1024)S(1)} %copy-done.1, f32[4]{0:T(128)S(1)} %get-tuple-element.13), kind=kOutput, calls=%fused_computation.16 | convolution fusion | flops 2014445568 | bytes 8655888 | tf_op jit(solution)/shard_map/dot_general | solution.py:61
  59.6 2.8 %fusion = f32[4,64,1280]{2,1,0:T(8,128)S(1)} fusion(f32[1024,1280]{1,0:T(8,128)S(1)} %bitcast.94, f32[4,64,1024]{2,1,0:T(8,128)S(1)} %fusion.19, f32[4]{0:T(128)S(1)} %fusion.66, f32[4]{0:T(128)S(1)} %get-tuple-element.12), kind=kOutput, calls=%fused_computation.1 | convolution fusion | flops 2014052352 | bytes 7602208 | tf_op jit(solution)/shard_map/dot_general | solution.py:57
  62.5 0.3 subtract_reduce_fusion
  62.8 0.1 multiply_add_fusion.1
  63.0 0.1 pad_maximum_fusion
  63.1 1.1 %fusion.31 = f32[8,32,1280]{2,0,1:T(8,128)S(1)} fusion(f32[8,32,1280]{2,1,0:T(8,128)S(1)} %bitcast.96, s32[8]{0:T(128)S(1)} %eq.24), kind=kOutput, calls=%fused_computation.30 | convolution fusion | flops 15728704 | bytes 2621472 | tf_op jit(solution)/shard_map/bs,skx->bkx/dot_general | solution.py:155
  64.2 0.4 copy.25
  64.6 2.4 %fusion.22 = f32[260,1024]{1,0:T(8,128)S(1)} fusion(f32[1024,1280]{1,0:T(8,128)S(1)} %bitcast.94, f32[4,640]{1,0:T(4,128)S(1)} %get-tuple-element.7, f32[4,640]{1,0:T(4,128)S(1)} %get-tuple-element.6, f32[256,1280]{1,0:T(8,128)S(1)} %bitcast.97, f32[1280]{0:T(1024)S(1)} %copy-done.1), kind=kOutput, calls=%fused_computation.18 | convolution fusion | flops 2045721600 | bytes 7644160 | tf_op jit(solution)/shard_map/dot_general | solution.py:61
  67.0 0.1 slice.81
  67.4 1.8 %collective-permute-done.4 = f32[4,32,1024]{2,1,0:T(8,128)S(1)} collective-permute-done((f32[4,32,1024]{2,1,0:T(8,128)S(1)}, f32[4,32,1024]{2,1,0:T(8,128)S(1)}, u32[]{:S(2)}, u32[]{:S(2)}) %collective-permute-start.4) | collective-permute-done | bytes 524320 | tf_op jit(solution)/shard_map/ppermute | solution.py:163
  69.3 1.1 %collective-permute-start.5 = (f32[32,1024]{1,0:T(8,128)S(1)}, f32[32,1024]{1,0:T(8,128)S(1)}, u32[]{:S(2)}, u32[]{:S(2)}) collective-permute-start(f32[32,1024]{1,0:T(8,128)S(1)} %get-tuple-element.21), channel_id=1, source_target_pairs={{0,2},{1,3},{2,4},{3,5},{4,6},{5,7},{6,0},{7,1},{8,10},{9,11},{10,... | collective-permute-start | bytes 393224 | tf_op jit(solution)/shard_map/ppermute | solution.py:167
  70.4 1.6 %collective-permute-start.6 = (f32[32,1024]{1,0:T(8,128)S(1)}, f32[32,1024]{1,0:T(8,128)S(1)}, u32[]{:S(2)}, u32[]{:S(2)}) collective-permute-start(f32[32,1024]{1,0:T(8,128)S(1)} %get-tuple-element.23), channel_id=1, source_target_pairs={{0,4},{1,5},{2,6},{3,7},{4,0},{5,1},{6,2},{7,3},{8,12},{9,13},{10,... | collective-permute-start | bytes 393224 | tf_op jit(solution)/shard_map/ppermute | solution.py:167
  72.0 1.5 %collective-permute-start.7 = (f32[32,1024]{1,0:T(8,128)S(1)}, f32[32,1024]{1,0:T(8,128)S(1)}, u32[]{:S(2)}, u32[]{:S(2)}) collective-permute-start(f32[32,1024]{1,0:T(8,128)S(1)} %get-tuple-element.22), channel_id=1, source_target_pairs={{0,6},{1,7},{2,0},{3,1},{4,2},{5,3},{6,4},{7,5},{8,14},{9,15},{10,... | collective-permute-start | bytes 393224 | tf_op jit(solution)/shard_map/ppermute | solution.py:167
  73.5 2.2 %collective-permute-done.5 = f32[32,1024]{1,0:T(8,128)S(1)} collective-permute-done((f32[32,1024]{1,0:T(8,128)S(1)}, f32[32,1024]{1,0:T(8,128)S(1)}, u32[]{:S(2)}, u32[]{:S(2)}) %collective-permute-start.5) | collective-permute-done | bytes 131104 | tf_op jit(solution)/shard_map/ppermute | solution.py:167
  75.8 2.5 %collective-permute-done.6 = f32[32,1024]{1,0:T(8,128)S(1)} collective-permute-done((f32[32,1024]{1,0:T(8,128)S(1)}, f32[32,1024]{1,0:T(8,128)S(1)}, u32[]{:S(2)}, u32[]{:S(2)}) %collective-permute-start.6) | collective-permute-done | bytes 131104 | tf_op jit(solution)/shard_map/ppermute | solution.py:167
  78.3 1.5 %collective-permute-done.7 = f32[32,1024]{1,0:T(8,128)S(1)} collective-permute-done((f32[32,1024]{1,0:T(8,128)S(1)}, f32[32,1024]{1,0:T(8,128)S(1)}, u32[]{:S(2)}, u32[]{:S(2)}) %collective-permute-start.7) | collective-permute-done | bytes 131104 | tf_op jit(solution)/shard_map/ppermute | solution.py:167
  79.8 0.7 reshape.374
  80.6 4.3 %all-to-all-start.1 = ((f32[32,1,1024]{2,1,0:T(1,128)}), f32[32,1,1024]{2,1,0:T(1,128)S(1)}, u32[]{:S(2)}, u32[]{:S(2)}) async-start(f32[32,1,1024]{2,1,0:T(1,128)} %reshape.374), calls=%async_computation.1 | async-start | bytes 262144 | tf_op jit(solution)/shard_map/all_to_all | solution.py:169
  84.9 0.6 multiply_reduce_fusion.2
  86.2 0.6 slice.80
  86.8 8.3 %all-to-all-done.1 = f32[32,1,1024]{2,1,0:T(1,128)S(1)} async-done(((f32[32,1,1024]{2,1,0:T(1,128)}), f32[32,1,1024]{2,1,0:T(1,128)S(1)}, u32[]{:S(2)}, u32[]{:S(2)}) %all-to-all-start.1) | async-done | bytes 131104 | tf_op jit(solution)/shard_map/all_to_all | solution.py:169
  95.1 0.1 reduce_sum.97
  95.2 0.6 multiply_reduce_fusion.1
  96.5 0.6 fusion.49
  97.8 0.6 subtract_divide_fusion
  (44 shorter events, 1.1 us)
Async XLA Ops:
  0.6 13.6 %copy-start = (f32[4,1024]{1,0:T(4,128)S(1)}, f32[4,1024]{1,0:T(4,128)}, u32[]{:S(2)}) copy-start(f32[4,1024]{1,0:T(4,128)} %param.5) | copy-start | bytes 49156
  2.0 21.6 %all-to-all-start = ((f32[32,8,128]{2,1,0:T(8,128)}), f32[32,8,128]{2,1,0:T(8,128)S(1)}, u32[]{:S(2)}, u32[]{:S(2)}) async-start(f32[32,8,128]{2,1,0:T(8,128)} %broadcast_in_dim.47), calls=%async_computation | async-start | bytes 262144 | tf_op jit(solution)/shard_map/all_to_all | solution.py:99
  14.2 3.7 %copy-start.3 = (s32[4,2]{0,1:T(2,128)S(1)}, s32[4,2]{0,1:T(2,128)}, u32[]{:S(2)}) copy-start(s32[4,2]{0,1:T(2,128)} %param.6) | copy-start | bytes 100
  23.6 1.4 %collective-permute-start = (f32[32,1024]{1,0:T(8,128)S(1)}, f32[32,1024]{1,0:T(8,128)S(1)}, u32[]{:S(2)}, u32[]{:S(2)}) collective-permute-start(f32[32,1024]{1,0:T(8,128)S(1)} %bitcast.103), channel_id=1, source_target_pairs={{0,1},{1,0},{2,3},{3,2},{4,5},{5,4},{6,7},{7,6},{8,9},{9,8},{10,11... | collective-permute-start | bytes 393224 | tf_op jit(solution)/shard_map/ppermute | solution.py:106
  25.1 9.3 %collective-permute-start.1 = (f32[64,1024]{1,0:T(8,128)S(1)}, f32[64,1024]{1,0:T(8,128)S(1)}, u32[]{:S(2)}, u32[]{:S(2)}) collective-permute-start(f32[64,1024]{1,0:T(8,128)S(1)} %get-tuple-element.24), channel_id=1, source_target_pairs={{0,2},{1,3},{2,4},{3,5},{4,6},{5,7},{6,0},{7,1},{8,10},{9,11},{10,... | collective-permute-start | bytes 786440 | tf_op jit(solution)/shard_map/ppermute | solution.py:110
  26.7 10.7 %collective-permute-start.2 = (f32[64,1024]{1,0:T(8,128)S(1)}, f32[64,1024]{1,0:T(8,128)S(1)}, u32[]{:S(2)}, u32[]{:S(2)}) collective-permute-start(f32[64,1024]{1,0:T(8,128)S(1)} %get-tuple-element.24), channel_id=1, source_target_pairs={{0,4},{1,5},{2,6},{3,7},{4,0},{5,1},{6,2},{7,3},{8,12},{9,13},{10,... | collective-permute-start | bytes 786440 | tf_op jit(solution)/shard_map/ppermute | solution.py:110
  27.7 13.8 %collective-permute-start.3 = (f32[64,1024]{1,0:T(8,128)S(1)}, f32[64,1024]{1,0:T(8,128)S(1)}, u32[]{:S(2)}, u32[]{:S(2)}) collective-permute-start(f32[64,1024]{1,0:T(8,128)S(1)} %get-tuple-element.24), channel_id=1, source_target_pairs={{0,6},{1,7},{2,0},{3,1},{4,2},{5,3},{6,4},{7,5},{8,14},{9,15},{10,... | collective-permute-start | bytes 786440 | tf_op jit(solution)/shard_map/ppermute | solution.py:110
  47.7 1.2 %copy-start.1 = (f32[1280]{0:T(1024)S(1)}, f32[1280]{0:T(1024)}, u32[]{:S(2)}) copy-start(f32[1280]{0:T(1024)} %constant.140.clone) | copy-start | bytes 15364
  47.7 6.5 %slice-start = ((s8[5242880]{0:T(1024)(128)(4,1)}), s8[1048576]{0:T(1024)(128)(4,1)S(1)}, s32[]{:S(2)}) async-start(s8[5242880]{0:T(1024)(128)(4,1)} %bitcast.93), calls=%async_computation.2 | async-start | bytes 2097152
  48.9 5.3 %slice-start.1 = ((s8[5242880]{0:T(1024)(128)(4,1)}), s8[4194304]{0:T(1024)(128)(4,1)S(1)}, s32[]{:S(2)}) async-start(s8[5242880]{0:T(1024)(128)(4,1)} %bitcast.93), calls=%async_computation.3 | async-start | bytes 8388608
  67.2 2.0 %collective-permute-start.4 = (f32[4,32,1024]{2,1,0:T(8,128)S(1)}, f32[4,32,1024]{2,1,0:T(8,128)S(1)}, u32[]{:S(2)}, u32[]{:S(2)}) collective-permute-start(f32[4,32,1024]{2,1,0:T(8,128)S(1)} %dynamic-slice_bitcast_fusion), channel_id=1, source_target_pairs={{0,1},{1,0},{2,3},{3,2},{4,5},{5,4},{6,7},{7,6},{8,9},{9,8},{10,11... | collective-permute-start | bytes 1572872 | tf_op jit(solution)/shard_map/ppermute | solution.py:163
  69.3 15.6 %copy-start.2 = (f32[1,1,1024]{2,1,0:T(1,128)S(1)}, f32[1,1,1024]{2,1,0:T(1,128)}, u32[]{:S(2)}) copy-start(f32[1,1,1024]{2,1,0:T(1,128)} %param.7) | copy-start | bytes 12292
  69.3 6.4 %collective-permute-start.5 = (f32[32,1024]{1,0:T(8,128)S(1)}, f32[32,1024]{1,0:T(8,128)S(1)}, u32[]{:S(2)}, u32[]{:S(2)}) collective-permute-start(f32[32,1024]{1,0:T(8,128)S(1)} %get-tuple-element.21), channel_id=1, source_target_pairs={{0,2},{1,3},{2,4},{3,5},{4,6},{5,7},{6,0},{7,1},{8,10},{9,11},{10,... | collective-permute-start | bytes 393224 | tf_op jit(solution)/shard_map/ppermute | solution.py:167
  70.4 7.9 %collective-permute-start.6 = (f32[32,1024]{1,0:T(8,128)S(1)}, f32[32,1024]{1,0:T(8,128)S(1)}, u32[]{:S(2)}, u32[]{:S(2)}) collective-permute-start(f32[32,1024]{1,0:T(8,128)S(1)} %get-tuple-element.23), channel_id=1, source_target_pairs={{0,4},{1,5},{2,6},{3,7},{4,0},{5,1},{6,2},{7,3},{8,12},{9,13},{10,... | collective-permute-start | bytes 393224 | tf_op jit(solution)/shard_map/ppermute | solution.py:167
  72.0 7.8 %collective-permute-start.7 = (f32[32,1024]{1,0:T(8,128)S(1)}, f32[32,1024]{1,0:T(8,128)S(1)}, u32[]{:S(2)}, u32[]{:S(2)}) collective-permute-start(f32[32,1024]{1,0:T(8,128)S(1)} %get-tuple-element.22), channel_id=1, source_target_pairs={{0,6},{1,7},{2,0},{3,1},{4,2},{5,3},{6,4},{7,5},{8,14},{9,15},{10,... | collective-permute-start | bytes 393224 | tf_op jit(solution)/shard_map/ppermute | solution.py:167
  80.6 14.5 %all-to-all-start.1 = ((f32[32,1,1024]{2,1,0:T(1,128)}), f32[32,1,1024]{2,1,0:T(1,128)S(1)}, u32[]{:S(2)}, u32[]{:S(2)}) async-start(f32[32,1,1024]{2,1,0:T(1,128)} %reshape.374), calls=%async_computation.1 | async-start | bytes 262144 | tf_op jit(solution)/shard_map/all_to_all | solution.py:169

commit v10 on v9

--- a/solution.py
+++ b/solution.py
@@ -114,9 +114,10 @@
     slot_count = tiles_here * ACT
     flat_ids = active.reshape(slot_count)
     where_held = ((chip - flat_ids // 2) % chips) * 2 + (flat_ids % 2 != core).astype(jnp.int32)
-    chosen_atoms = unit_rows(jnp.take(every, where_held, axis=0).reshape(slot_count * BLK, pixels))
+    chosen_atoms = jnp.take(every, where_held, axis=0).reshape(slot_count * BLK, pixels)
+    norm = jnp.sqrt(jnp.mean(chosen_atoms * chosen_atoms, axis=-1, keepdims=True) + epsilon)
     rows = ACT * BLK
-    chosen = forward(chosen_atoms, table).reshape(tiles_here, rows, width)
+    chosen = (forward(chosen_atoms, table) / norm).reshape(tiles_here, rows, width)
     chosen_real, chosen_imag = parts(chosen)
     power = jnp.sum(chosen_real * chosen_real + chosen_imag * chosen_imag, axis=1)
     bound = jnp.max(power, axis=1) + epsilon

time: 98.8 us -> 98.7 us (level)
  no operation moved by 1% of the time
where the time goes in v10:
time: 98.7 us; the launch traced here: 98.3 us
  waiting for transfers between devices  34.3 us (35%)
  starting transfers between devices  25.2 us (26%)
  matrix products  25.2 us (26%)
  local copies, waits for them, and re-layouts  5.25 us (5%)
  other arithmetic  5.22 us (5%)
  between operations  3.17 us (3%)
    dot_general x4, matrix products, forward(): jnp.dot(values, table, precision=fast, preferred_element_type=jnp.float32)  14.1 us
    all_to_all x1, starting transfers between devices, on_device(): lax.all_to_all(jnp.broadcast_to(dense, (tile_count, 8, pixels // 8)), 'ti...  11.3 us
    ppermute x3, waiting for transfers between devices, on_device(): lax.ppermute(pair, 'atom', [(i, (i // 2 + hop) % chips * 2 + i % 2) for i...  11 us
    dot_general x3, matrix products, inverse(): lax.dot_general(spectra * weight, table, (((spectra.ndim - 1,), (1,)), ((...  10 us
    all_to_all x1, waiting for transfers between devices, on_device(): lax.all_to_all(arrived, 'tile', 0, 0, tiled=True)  8.35 us
    ppermute x3, waiting for transfers between devices, on_device(): lax.ppermute(sent, 'atom', [(i, (i // 2 + hop) % chips * 2 + i % 2) for i...  6.26 us
    all_to_all x1, waiting for transfers between devices, on_device(): lax.all_to_all(jnp.broadcast_to(dense, (tile_count, 8, pixels // 8)), 'ti...  5.59 us
    ppermute x3, starting transfers between devices, on_device(): lax.ppermute(pair, 'atom', [(i, (i // 2 + hop) % chips * 2 + i % 2) for i...  5.26 us
  transfers between devices with their start and end apart: 10, of which 10 were waited for; matrix products, arithmetic and copies ran while one was open for 6% of the time, Pallas kernels for 0%

profile of v10, /device:TPU:8, one launch (start us, length us, event | category | flops | bytes accessed | tf_op | source)
XLA Modules:
  0.0 98.3 jit_solution(7532248320588128729)
XLA Ops:
  0.6 1.3 %broadcast_in_dim.47 = f32[32,8,128]{2,1,0:T(8,128)} broadcast(f32[8,128]{1,0:T(8,128)} %bitcast.104), dimensions={1,2} | broadcast | bytes 135168 | tf_op jit(solution)/shard_map/broadcast_in_dim | solution.py:99
  2.0 11.3 %all-to-all-start = ((f32[32,8,128]{2,1,0:T(8,128)}), f32[32,8,128]{2,1,0:T(8,128)S(1)}, u32[]{:S(2)}, u32[]{:S(2)}) async-start(f32[32,8,128]{2,1,0:T(8,128)} %broadcast_in_dim.47), calls=%async_computation | async-start | bytes 262144 | tf_op jit(solution)/shard_map/all_to_all | solution.py:99
  13.3 0.8 copy.18
  14.2 3.7 %convolution_bitcast_fusion = f32[4,1280]{1,0:T(4,128)S(1)} fusion(f32[1024,1280]{1,0:T(8,128)} %constant.139.clone, f32[4,1024]{1,0:T(4,128)S(1)} %copy-done), kind=kOutput, calls=%fused_computation.10 | convolution fusion | flops 31457280 | bytes 5279744 | tf_op jit(solution)/shard_map/dot_general | solution.py:57
  18.0 5.6 %all-to-all-done = f32[32,8,128]{2,1,0:T(8,128)S(1)} async-done(((f32[32,8,128]{2,1,0:T(8,128)}), f32[32,8,128]{2,1,0:T(8,128)S(1)}, u32[]{:S(2)}, u32[]{:S(2)}) %all-to-all-start) | async-done | bytes 131104 | tf_op jit(solution)/shard_map/all_to_all | solution.py:99
  23.7 1.3 %collective-permute-done = f32[32,1024]{1,0:T(8,128)S(1)} collective-permute-done((f32[32,1024]{1,0:T(8,128)S(1)}, f32[32,1024]{1,0:T(8,128)S(1)}, u32[]{:S(2)}, u32[]{:S(2)}) %collective-permute-start) | collective-permute-done | bytes 131104 | tf_op jit(solution)/shard_map/ppermute | solution.py:106
  25.1 1.7 %collective-permute-start.1 = (f32[64,1024]{1,0:T(8,128)S(1)}, f32[64,1024]{1,0:T(8,128)S(1)}, u32[]{:S(2)}, u32[]{:S(2)}) collective-permute-start(f32[64,1024]{1,0:T(8,128)S(1)} %get-tuple-element.24), channel_id=1, source_target_pairs={{0,2},{1,3},{2,4},{3,5},{4,6},{5,7},{6,0},{7,1},{8,10},{9,11},{10,... | collective-permute-start | bytes 786440 | tf_op jit(solution)/shard_map/ppermute | solution.py:110
  26.7 0.9 collective-permute-start.2
  27.7 2.7 %collective-permute-start.3 = (f32[64,1024]{1,0:T(8,128)S(1)}, f32[64,1024]{1,0:T(8,128)S(1)}, u32[]{:S(2)}, u32[]{:S(2)}) collective-permute-start(f32[64,1024]{1,0:T(8,128)S(1)} %get-tuple-element.24), channel_id=1, source_target_pairs={{0,6},{1,7},{2,0},{3,1},{4,2},{5,3},{6,4},{7,5},{8,14},{9,15},{10,... | collective-permute-start | bytes 786440 | tf_op jit(solution)/shard_map/ppermute | solution.py:110
  30.5 3.8 %collective-permute-done.1 = f32[64,1024]{1,0:T(8,128)S(1)} collective-permute-done((f32[64,1024]{1,0:T(8,128)S(1)}, f32[64,1024]{1,0:T(8,128)S(1)}, u32[]{:S(2)}, u32[]{:S(2)}) %collective-permute-start.1) | collective-permute-done | bytes 262176 | tf_op jit(solution)/shard_map/ppermute | solution.py:110
  34.3 3.1 %collective-permute-done.2 = f32[64,1024]{1,0:T(8,128)S(1)} collective-permute-done((f32[64,1024]{1,0:T(8,128)S(1)}, f32[64,1024]{1,0:T(8,128)S(1)}, u32[]{:S(2)}, u32[]{:S(2)}) %collective-permute-start.2) | collective-permute-done | bytes 262176 | tf_op jit(solution)/shard_map/ppermute | solution.py:110
  37.4 4.1 %collective-permute-done.3 = f32[64,1024]{1,0:T(8,128)S(1)} collective-permute-done((f32[64,1024]{1,0:T(8,128)S(1)}, f32[64,1024]{1,0:T(8,128)S(1)}, u32[]{:S(2)}, u32[]{:S(2)}) %collective-permute-start.3) | collective-permute-done | bytes 262176 | tf_op jit(solution)/shard_map/ppermute | solution.py:110
  41.5 0.6 gather_fusion
  42.2 0.2 multiply_reduce_fusion
  42.4 0.1 bitcast_select_fusion
  42.6 5.0 %convolution_divide_fusion = f32[256,1280]{1,0:T(8,128)S(1)} fusion(f32[256,1024]{1,0:T(8,128)S(1)} %bitcast_select_fusion, f32[1024,1280]{1,0:T(8,128)} %constant.139.clone, f32[256]{0:T(256)S(1)} %sqrt.24), kind=kOutput, calls=%fused_computation.9 | convolution fusion | flops 2013593600 | bytes 7603200 | tf_op jit(solution)/shard_map/dot_general | solution.py:57
  47.7 1.1 %multiply_add_fusion.3 = (f32[4,64,640]{2,1,0:T(8,128)S(1)}, f32[4,64,640]{2,1,0:T(8,128)}, f32[4,640]{1,0:T(4,128)S(1)}) fusion(f32[4,64,1280]{2,1,0:T(8,128)S(1)} %bitcast.92, f32[4,640]{1,0:T(4,128)S(1)} %get-tuple-element.33, f32[4,640]{1,0:T(4,128)S(1)} %get-tuple-element.32), kind=kLoop, calls=%fused_computation.48 | loop fusion | flops 1635840 | bytes 2652160 | tf_op jit(solution)/shard_map/add | solution.py:74
  48.7 0.1 reduce_max.9
  48.9 5.2 %multiply_add_fusion = f32[4,64,1024]{2,1,0:T(8,128)S(1)} fusion(f32[1024,1280]{1,0:T(8,128)} %constant.139.clone, f32[4,64,640]{2,1,0:T(8,128)} %get-tuple-element.19, f32[4,64,640]{2,1,0:T(8,128)S(1)} %get-tuple-element.18, f32[1280]{0:T(1024)S(1)} %copy-done.1, f32[4]{0:T(128)S(1)} %fusion.60, f32[4]{0:T(128)S(1)} %get-tuple-element.12, ...), kind=kOutput, calls=%fused_computation.11 | convolution fusion | flops 2015756288 | bytes 7607344 | tf_op jit(solution)/shard_map/dot_general | solution.py:61
  54.1 2.6 %fusion.4 = f32[4,64,1280]{2,1,0:T(8,128)S(1)} fusion(f32[4,64,1024]{2,1,0:T(8,128)S(1)} %multiply_add_fusion, f32[1024,1280]{1,0:T(8,128)S(1)} %bitcast.91), kind=kOutput, calls=%fused_computation.5 | convolution fusion | flops 2013265920 | bytes 7602176 | tf_op jit(solution)/shard_map/dot_general | solution.py:57
  56.7 0.3 subtract_reduce_fusion.1
  57.0 0.1 multiply_add_fusion.2
  57.2 2.4 %fusion.17 = f32[4,64,1024]{2,1,0:T(8,128)S(1)} fusion(f32[4,64,1024]{2,1,0:T(8,128)S(1)} %multiply_add_fusion, f32[1024,1280]{1,0:T(8,128)S(1)} %bitcast.91, f32[4,64,640]{2,1,0:T(8,128)S(1)} %get-tuple-element.17, f32[4,64,640]{2,1,0:T(8,128)S(1)} %get-tuple-element.16, f32[1280]{0:T(1024)S(1)} %copy-done.1, f32[4]{0:T(128)S(1)} %get-tuple-element.13), kind=kOutput, calls=%fused_computation.15 | convolution fusion | flops 2014445568 | bytes 8655888 | tf_op jit(solution)/shard_map/dot_general | solution.py:61
  59.6 2.8 %fusion = f32[4,64,1280]{2,1,0:T(8,128)S(1)} fusion(f32[1024,1280]{1,0:T(8,128)S(1)} %bitcast.91, f32[4,64,1024]{2,1,0:T(8,128)S(1)} %fusion.17, f32[4]{0:T(128)S(1)} %fusion.60, f32[4]{0:T(128)S(1)} %get-tuple-element.12), kind=kOutput, calls=%fused_computation.1 | convolution fusion | flops 2014052352 | bytes 7602208 | tf_op jit(solution)/shard_map/dot_general | solution.py:57
  62.4 0.3 subtract_reduce_fusion
  62.7 0.1 multiply_add_fusion.1
  62.9 0.1 pad_maximum_fusion
  63.0 1.1 %fusion.29 = f32[8,32,1280]{2,0,1:T(8,128)S(1)} fusion(f32[8,32,1280]{2,1,0:T(8,128)S(1)} %bitcast.96, s32[8]{0:T(128)S(1)} %eq.24), kind=kOutput, calls=%fused_computation.29 | convolution fusion | flops 15728704 | bytes 2621472 | tf_op jit(solution)/shard_map/bs,skx->bkx/dot_general | solution.py:156
  64.1 0.4 copy.21
  64.5 2.4 %fusion.20 = f32[260,1024]{1,0:T(8,128)S(1)} fusion(f32[1024,1280]{1,0:T(8,128)S(1)} %bitcast.91, f32[4,640]{1,0:T(4,128)S(1)} %get-tuple-element.7, f32[4,640]{1,0:T(4,128)S(1)} %get-tuple-element.6, f32[256,1280]{1,0:T(8,128)S(1)} %bitcast.97, f32[1280]{0:T(1024)S(1)} %copy-done.1), kind=kOutput, calls=%fused_computation.17 | convolution fusion | flops 2045721600 | bytes 7644160 | tf_op jit(solution)/shard_map/dot_general | solution.py:61
  66.9 0.1 slice.81
  67.1 0.1 collective-permute-start.4
  67.3 1.8 %collective-permute-done.4 = f32[4,32,1024]{2,1,0:T(8,128)S(1)} collective-permute-done((f32[4,32,1024]{2,1,0:T(8,128)S(1)}, f32[4,32,1024]{2,1,0:T(8,128)S(1)}, u32[]{:S(2)}, u32[]{:S(2)}) %collective-permute-start.4) | collective-permute-done | bytes 524320 | tf_op jit(solution)/shard_map/ppermute | solution.py:164
  69.2 1.1 %collective-permute-start.5 = (f32[32,1024]{1,0:T(8,128)S(1)}, f32[32,1024]{1,0:T(8,128)S(1)}, u32[]{:S(2)}, u32[]{:S(2)}) collective-permute-start(f32[32,1024]{1,0:T(8,128)S(1)} %get-tuple-element.21), channel_id=1, source_target_pairs={{0,2},{1,3},{2,4},{3,5},{4,6},{5,7},{6,0},{7,1},{8,10},{9,11},{10,... | collective-permute-start | bytes 393224 | tf_op jit(solution)/shard_map/ppermute | solution.py:168
  70.3 1.6 %collective-permute-start.6 = (f32[32,1024]{1,0:T(8,128)S(1)}, f32[32,1024]{1,0:T(8,128)S(1)}, u32[]{:S(2)}, u32[]{:S(2)}) collective-permute-start(f32[32,1024]{1,0:T(8,128)S(1)} %get-tuple-element.23), channel_id=1, source_target_pairs={{0,4},{1,5},{2,6},{3,7},{4,0},{5,1},{6,2},{7,3},{8,12},{9,13},{10,... | collective-permute-start | bytes 393224 | tf_op jit(solution)/shard_map/ppermute | solution.py:168
  71.9 1.5 %collective-permute-start.7 = (f32[32,1024]{1,0:T(8,128)S(1)}, f32[32,1024]{1,0:T(8,128)S(1)}, u32[]{:S(2)}, u32[]{:S(2)}) collective-permute-start(f32[32,1024]{1,0:T(8,128)S(1)} %get-tuple-element.22), channel_id=1, source_target_pairs={{0,6},{1,7},{2,0},{3,1},{4,2},{5,3},{6,4},{7,5},{8,14},{9,15},{10,... | collective-permute-start | bytes 393224 | tf_op jit(solution)/shard_map/ppermute | solution.py:168
  73.5 2.2 %collective-permute-done.5 = f32[32,1024]{1,0:T(8,128)S(1)} collective-permute-done((f32[32,1024]{1,0:T(8,128)S(1)}, f32[32,1024]{1,0:T(8,128)S(1)}, u32[]{:S(2)}, u32[]{:S(2)}) %collective-permute-start.5) | collective-permute-done | bytes 131104 | tf_op jit(solution)/shard_map/ppermute | solution.py:168
  75.7 2.5 %collective-permute-done.6 = f32[32,1024]{1,0:T(8,128)S(1)} collective-permute-done((f32[32,1024]{1,0:T(8,128)S(1)}, f32[32,1024]{1,0:T(8,128)S(1)}, u32[]{:S(2)}, u32[]{:S(2)}) %collective-permute-start.6) | collective-permute-done | bytes 131104 | tf_op jit(solution)/shard_map/ppermute | solution.py:168
  78.2 1.5 %collective-permute-done.7 = f32[32,1024]{1,0:T(8,128)S(1)} collective-permute-done((f32[32,1024]{1,0:T(8,128)S(1)}, f32[32,1024]{1,0:T(8,128)S(1)}, u32[]{:S(2)}, u32[]{:S(2)}) %collective-permute-start.7) | collective-permute-done | bytes 131104 | tf_op jit(solution)/shard_map/ppermute | solution.py:168
  79.8 0.7 reshape.363
  80.5 4.2 %all-to-all-start.1 = ((f32[32,1,1024]{2,1,0:T(1,128)}), f32[32,1,1024]{2,1,0:T(1,128)S(1)}, u32[]{:S(2)}, u32[]{:S(2)}) async-start(f32[32,1,1024]{2,1,0:T(1,128)} %reshape.363), calls=%async_computation.1 | async-start | bytes 262144 | tf_op jit(solution)/shard_map/all_to_all | solution.py:170
  84.7 0.6 multiply_reduce_fusion.2
  86.0 0.6 slice.80
  86.6 8.3 %all-to-all-done.1 = f32[32,1,1024]{2,1,0:T(1,128)S(1)} async-done(((f32[32,1,1024]{2,1,0:T(1,128)}), f32[32,1,1024]{2,1,0:T(1,128)S(1)}, u32[]{:S(2)}, u32[]{:S(2)}) %all-to-all-start.1) | async-done | bytes 131104 | tf_op jit(solution)/shard_map/all_to_all | solution.py:170
  95.0 0.1 reduce_sum.97
  95.1 0.6 multiply_reduce_fusion.1
  96.4 0.6 fusion.46
  97.7 0.6 subtract_divide_fusion
  (40 shorter events, 1.0 us)
Async XLA Ops:
  0.6 13.5 %copy-start = (f32[4,1024]{1,0:T(4,128)S(1)}, f32[4,1024]{1,0:T(4,128)}, u32[]{:S(2)}) copy-start(f32[4,1024]{1,0:T(4,128)} %param.5) | copy-start | bytes 49156
  2.0 21.6 %all-to-all-start = ((f32[32,8,128]{2,1,0:T(8,128)}), f32[32,8,128]{2,1,0:T(8,128)S(1)}, u32[]{:S(2)}, u32[]{:S(2)}) async-start(f32[32,8,128]{2,1,0:T(8,128)} %broadcast_in_dim.47), calls=%async_computation | async-start | bytes 262144 | tf_op jit(solution)/shard_map/all_to_all | solution.py:99
  23.6 1.4 %collective-permute-start = (f32[32,1024]{1,0:T(8,128)S(1)}, f32[32,1024]{1,0:T(8,128)S(1)}, u32[]{:S(2)}, u32[]{:S(2)}) collective-permute-start(f32[32,1024]{1,0:T(8,128)S(1)} %bitcast.103), channel_id=1, source_target_pairs={{0,1},{1,0},{2,3},{3,2},{4,5},{5,4},{6,7},{7,6},{8,9},{9,8},{10,11... | collective-permute-start | bytes 393224 | tf_op jit(solution)/shard_map/ppermute | solution.py:106
  25.1 9.3 %collective-permute-start.1 = (f32[64,1024]{1,0:T(8,128)S(1)}, f32[64,1024]{1,0:T(8,128)S(1)}, u32[]{:S(2)}, u32[]{:S(2)}) collective-permute-start(f32[64,1024]{1,0:T(8,128)S(1)} %get-tuple-element.24), channel_id=1, source_target_pairs={{0,2},{1,3},{2,4},{3,5},{4,6},{5,7},{6,0},{7,1},{8,10},{9,11},{10,... | collective-permute-start | bytes 786440 | tf_op jit(solution)/shard_map/ppermute | solution.py:110
  26.7 10.7 %collective-permute-start.2 = (f32[64,1024]{1,0:T(8,128)S(1)}, f32[64,1024]{1,0:T(8,128)S(1)}, u32[]{:S(2)}, u32[]{:S(2)}) collective-permute-start(f32[64,1024]{1,0:T(8,128)S(1)} %get-tuple-element.24), channel_id=1, source_target_pairs={{0,4},{1,5},{2,6},{3,7},{4,0},{5,1},{6,2},{7,3},{8,12},{9,13},{10,... | collective-permute-start | bytes 786440 | tf_op jit(solution)/shard_map/ppermute | solution.py:110
  27.7 13.8 %collective-permute-start.3 = (f32[64,1024]{1,0:T(8,128)S(1)}, f32[64,1024]{1,0:T(8,128)S(1)}, u32[]{:S(2)}, u32[]{:S(2)}) collective-permute-start(f32[64,1024]{1,0:T(8,128)S(1)} %get-tuple-element.24), channel_id=1, source_target_pairs={{0,6},{1,7},{2,0},{3,1},{4,2},{5,3},{6,4},{7,5},{8,14},{9,15},{10,... | collective-permute-start | bytes 786440 | tf_op jit(solution)/shard_map/ppermute | solution.py:110
  47.6 1.2 %copy-start.1 = (f32[1280]{0:T(1024)S(1)}, f32[1280]{0:T(1024)}, u32[]{:S(2)}) copy-start(f32[1280]{0:T(1024)} %constant.140.clone) | copy-start | bytes 15364
  47.6 6.5 %slice-start = ((s8[5242880]{0:T(1024)(128)(4,1)}), s8[1048576]{0:T(1024)(128)(4,1)S(1)}, s32[]{:S(2)}) async-start(s8[5242880]{0:T(1024)(128)(4,1)} %bitcast.90), calls=%async_computation.2 | async-start | bytes 2097152
  48.9 5.3 %slice-start.1 = ((s8[5242880]{0:T(1024)(128)(4,1)}), s8[4194304]{0:T(1024)(128)(4,1)S(1)}, s32[]{:S(2)}) async-start(s8[5242880]{0:T(1024)(128)(4,1)} %bitcast.90), calls=%async_computation.3 | async-start | bytes 8388608
  67.1 2.0 %collective-permute-start.4 = (f32[4,32,1024]{2,1,0:T(8,128)S(1)}, f32[4,32,1024]{2,1,0:T(8,128)S(1)}, u32[]{:S(2)}, u32[]{:S(2)}) collective-permute-start(f32[4,32,1024]{2,1,0:T(8,128)S(1)} %dynamic-slice_bitcast_fusion), channel_id=1, source_target_pairs={{0,1},{1,0},{2,3},{3,2},{4,5},{5,4},{6,7},{7,6},{8,9},{9,8},{10,11... | collective-permute-start | bytes 1572872 | tf_op jit(solution)/shard_map/ppermute | solution.py:164
  69.2 15.5 %copy-start.2 = (f32[1,1,1024]{2,1,0:T(1,128)S(1)}, f32[1,1,1024]{2,1,0:T(1,128)}, u32[]{:S(2)}) copy-start(f32[1,1,1024]{2,1,0:T(1,128)} %param.7) | copy-start | bytes 12292
  69.2 6.4 %collective-permute-start.5 = (f32[32,1024]{1,0:T(8,128)S(1)}, f32[32,1024]{1,0:T(8,128)S(1)}, u32[]{:S(2)}, u32[]{:S(2)}) collective-permute-start(f32[32,1024]{1,0:T(8,128)S(1)} %get-tuple-element.21), channel_id=1, source_target_pairs={{0,2},{1,3},{2,4},{3,5},{4,6},{5,7},{6,0},{7,1},{8,10},{9,11},{10,... | collective-permute-start | bytes 393224 | tf_op jit(solution)/shard_map/ppermute | solution.py:168
  70.3 7.9 %collective-permute-start.6 = (f32[32,1024]{1,0:T(8,128)S(1)}, f32[32,1024]{1,0:T(8,128)S(1)}, u32[]{:S(2)}, u32[]{:S(2)}) collective-permute-start(f32[32,1024]{1,0:T(8,128)S(1)} %get-tuple-element.23), channel_id=1, source_target_pairs={{0,4},{1,5},{2,6},{3,7},{4,0},{5,1},{6,2},{7,3},{8,12},{9,13},{10,... | collective-permute-start | bytes 393224 | tf_op jit(solution)/shard_map/ppermute | solution.py:168
  71.9 7.8 %collective-permute-start.7 = (f32[32,1024]{1,0:T(8,128)S(1)}, f32[32,1024]{1,0:T(8,128)S(1)}, u32[]{:S(2)}, u32[]{:S(2)}) collective-permute-start(f32[32,1024]{1,0:T(8,128)S(1)} %get-tuple-element.22), channel_id=1, source_target_pairs={{0,6},{1,7},{2,0},{3,1},{4,2},{5,3},{6,4},{7,5},{8,14},{9,15},{10,... | collective-permute-start | bytes 393224 | tf_op jit(solution)/shard_map/ppermute | solution.py:168
  80.5 14.5 %all-to-all-start.1 = ((f32[32,1,1024]{2,1,0:T(1,128)}), f32[32,1,1024]{2,1,0:T(1,128)S(1)}, u32[]{:S(2)}, u32[]{:S(2)}) async-start(f32[32,1,1024]{2,1,0:T(1,128)} %reshape.363), calls=%async_computation.1 | async-start | bytes 262144 | tf_op jit(solution)/shard_map/all_to_all | solution.py:170
